TPU v7x, 32 devices: a whole 2x2x4 slice. The times are simulated.
32 devices in a mesh: dp: 2 (over y), pipe: 4 (over z), tensor: 4 (over x, core).
Axes of the slice: x: 2, y: 2, z: 4, core: 2. Of those that a mesh axis runs over, the one named last changes fastest.
Arguments:
- kept_qkv: bfloat16 [2, 4, 3, 192, 6144], P('dp', 'pipe', None, None, 'tensor'), may hold values from -20 to 20
- held_qkv: bfloat16 [2, 4, 3, 192, 6144], P('dp', 'pipe', None, None, 'tensor'), may hold values from -20 to 20
- sent_grad: bfloat16 [2, 4, 2, 64, 6144], P('dp', 'pipe', None, 'tensor'), may hold values from -60 to 60
- order: int32 [2, 4], P('dp', 'pipe'), may hold values from 0 to 1
- offsets: int32 [2, 4, 2], P('dp'), may hold values from 0 to 128, as said below
Outputs:
- query_grad: bfloat16 [2, 4, 2, 64, 6144], P('dp', 'pipe', None, None, 'tensor')
- key_value_grad: bfloat16 [2, 4, 2, 2, 192, 6144], P('dp', 'pipe', None, None, None, 'tensor')
- bias_grad: float32 [4, 3, 6144], P('pipe', None, 'tensor')
Inputs may be any that keep to these rules, and one draw needn't show every extreme that they name: `offsets`: multiples of 64.
All inputs are finite; a program needn't handle non-finite values.
Results may differ from a plain program's by a relative error of at most 0.019.
Values may be sent and summed in bfloat16 or wider, within the bound.
No kernel may reach another device: no remote copies, remote signals or barrier semaphores. Data moves between devices by JAX's collectives and lax.ppermute only.
A program may use at most 64 MiB of HBM per device.

v0:
```python
import math

import jax
import jax.numpy as jnp
from jax import lax
from jax.sharding import PartitionSpec as P

HD = 128


MASK_FILL = -1e30


def from_behind(value, axis, steps):
    count = lax.axis_size(axis)
    pairs = [(source, (source + steps) % count) for source in range(count)]
    return lax.ppermute(value, axis, pairs)


def slice_backward(stash, grad_out, offset):
    key_count = stash.shape[1]
    row_count = grad_out.shape[0]
    feature_count = stash.shape[2]
    head_count = feature_count // HD
    score_scale = 1.0 / math.sqrt(HD)
    queries = lax.dynamic_slice_in_dim(stash[0], offset, row_count, 0).reshape(
        row_count, head_count, HD
    )
    key_rows = stash[1].reshape(key_count, head_count, HD)
    value_rows = stash[2].reshape(key_count, head_count, HD)
    out_grad = grad_out.reshape(row_count, head_count, HD)
    positions = offset + jnp.arange(row_count, dtype=jnp.int32)
    columns = jnp.arange(key_count, dtype=jnp.int32)
    visible = columns[None, :] <= positions[:, None]
    scores = (
        jnp.einsum("qhd,khd->hqk", queries, key_rows, preferred_element_type=jnp.float32)
        * score_scale
    )
    scores = jnp.where(visible[None], scores, MASK_FILL)
    row_max = jnp.max(scores, axis=-1, keepdims=True)
    expos = jnp.exp(scores - row_max)
    attention = expos / jnp.sum(expos, axis=-1, keepdims=True)
    attention_low = attention.astype(jnp.bfloat16)
    context = jnp.einsum(
        "hqk,khd->qhd", attention_low, value_rows, preferred_element_type=jnp.float32
    ).astype(jnp.bfloat16)
    delta = jnp.sum(out_grad.astype(jnp.float32) * context.astype(jnp.float32), axis=-1).T
    value_grad = jnp.einsum(
        "hqk,qhd->khd", attention_low, out_grad, preferred_element_type=jnp.float32
    ).astype(jnp.bfloat16)
    prob_grad = jnp.einsum("qhd,khd->hqk", out_grad, value_rows, preferred_element_type=jnp.float32)
    score_grad = (attention * (prob_grad - delta[:, :, None]) * score_scale).astype(jnp.bfloat16)
    query_grad = jnp.einsum(
        "hqk,khd->qhd", score_grad, key_rows, preferred_element_type=jnp.float32
    ).astype(jnp.bfloat16)
    key_grad = jnp.einsum(
        "hqk,qhd->khd", score_grad, queries, preferred_element_type=jnp.float32
    ).astype(jnp.bfloat16)
    both_grads = jnp.stack(
        [key_grad.reshape(key_count, feature_count), value_grad.reshape(key_count, feature_count)]
    )
    return (query_grad.reshape(row_count, feature_count), both_grads)


def body(kept_qkv, held_qkv, sent_grad, order, offsets):
    arrived = from_behind(sent_grad, "pipe", -1)
    regrouped = lax.all_to_all(arrived, "tensor", split_axis=4, concat_axis=3, tiled=True)
    kept_first = order[0, 0] == 0
    grad_kept = jnp.where(kept_first, regrouped[0, 0, 0], regrouped[0, 0, 1])
    grad_held = jnp.where(kept_first, regrouped[0, 0, 1], regrouped[0, 0, 0])
    section_index = lax.axis_index("pipe")
    section_count = lax.axis_size("pipe")
    half_way = section_count // 2
    section_offsets = lax.dynamic_index_in_dim(offsets[0], section_index, 0, keepdims=False)
    kept_q, kept_kv = slice_backward(kept_qkv[0, 0], grad_kept, section_offsets[0])
    fetched = from_behind(held_qkv[0, 0], "pipe", half_way)
    held_q, held_kv = slice_backward(fetched, grad_held, section_offsets[1])
    query_grad = jnp.stack([kept_q, held_q])
    key_value_grad = jnp.stack([kept_kv, held_kv])
    query_sums = jnp.sum(query_grad.astype(jnp.float32), axis=(0, 1))
    key_sums = jnp.sum(key_value_grad[:, 0].astype(jnp.float32), axis=(0, 1))
    value_sums = jnp.sum(key_value_grad[:, 1].astype(jnp.float32), axis=(0, 1))
    column_sums = jnp.stack([query_sums, key_sums, value_sums])
    bias_grad = lax.psum(column_sums, "dp")
    return (query_grad[None, None], key_value_grad[None, None], bias_grad[None])


def solution(mesh):
    return jax.shard_map(
        body,
        mesh=mesh,
        in_specs=(
            P("dp", "pipe", None, None, "tensor"),
            P("dp", "pipe", None, None, "tensor"),
            P("dp", "pipe", None, "tensor", None),
            P("dp", "pipe"),
            P("dp", None, None),
        ),
        out_specs=(
            P("dp", "pipe", None, None, "tensor"),
            P("dp", "pipe", None, None, None, "tensor"),
            P("pipe", None, "tensor"),
        ),
        check_vma=False,
    )
```

profile of v0, /device:TPU:8, one launch (start us, length us, event | category | flops | bytes accessed | tf_op | source)
XLA Modules:
  0.0 121.3 jit_solution(14244090203486681753)
XLA Ops:
  0.6 0.0 copy-start
  0.6 0.1 collective-permute-start
  0.7 3.0 %collective-permute-start.1 = (bf16[3,192,1536]{2,1,0:T(8,128)(2,1)}, bf16[3,192,1536]{2,1,0:T(8,128)(2,1)}, u32[]{:S(2)}, u32[]{:S(2)}) collective-permute-start(bf16[3,192,1536]{2,1,0:T(8,128)(2,1)} %bitcast.67), channel_id=1, source_target_pairs={{0,8},{4,12},{8,0},{12,4},{1,9},{5,13},{9,1},{13,5},{2,10},{6,14},... | collective-permute-start | bytes 5308424 | tf_op jit(solution)/shard_map/ppermute | solution.py:17
  3.7 0.1 constant_dynamic-slice_fusion.2
  3.8 0.5 fusion.55
  4.4 0.6 iota_add_fusion.1
  5.7 2.4 %fusion.54 = (bf16[1,1,1,192,1536]{4,3,2,1,0:T(8,128)(2,1)S(1)}, bf16[1,1,1,192,1536]{4,3,2,1,0:T(8,128)(2,1)}, bf16[1,1,1,192,1536]{4,3,2,1,0:T(8,128)(2,1)S(1)}) fusion(bf16[1,1,3,192,1536]{4,3,2,1,0:T(8,128)(2,1)} %param.5), kind=kLoop, calls=%fused_computation.86 | loop fusion | bytes 3538944 | tf_op jit(solution)/shard_map/slice | solution.py:26
  9.4 0.1 constant_dynamic-slice_fusion.1
  9.4 0.1 iota_compare_fusion.1
  9.5 0.4 reshape_squeeze.12
  9.9 0.1 reshape.94
  10.1 0.6 iota_add_fusion
  10.7 1.4 %fusion.7 = f32[12,64,192]{2,1,0:T(8,128)} fusion(bf16[192,12,128]{2,1,0:T(8,128)(2,1)S(1)} %reshape_squeeze.12, pred[64,192]{1,0:T(8,128)(4,1)S(1)} %iota_compare_fusion.1, bf16[64,12,128]{2,1,0:T(8,128)(2,1)S(1)} %reshape.94), kind=kOutput, calls=%fused_computation.22 | convolution fusion | flops 38043648 | bytes 1388544 | tf_op jit(solution)/shard_map/qhd,khd->hqk/dot_general | solution.py:36
  12.1 38.8 %collective-permute-done = bf16[1,1,2,16,6144]{4,3,2,1,0:T(8,128)(2,1)} collective-permute-done((bf16[1,1,2,16,6144]{4,3,2,1,0:T(8,128)(2,1)}, bf16[1,1,2,16,6144]{4,3,2,1,0:T(8,128)(2,1)}, u32[]{:S(2)}, u32[]{:S(2)}) %collective-permute-start) | collective-permute-done | bytes 393248 | tf_op jit(solution)/shard_map/ppermute | solution.py:17
  50.9 6.1 %copy.86 = bf16[1,1,2,16,6144]{3,2,1,0,4:T(2,128)(2,1)S(1)} copy(bf16[1,1,2,16,6144]{4,3,2,1,0:T(8,128)(2,1)} %collective-permute-done) | data formatting | bytes 786432 | tf_op jit(solution)/shard_map/ppermute | solution.py:17
  57.0 4.0 %reshape.96 = bf16[4,2,24576]{2,1,0:T(2,128)(2,1)} reshape(bf16[6144,1,1,2,16]{4,3,2,1,0:T(2,128)(2,1)S(1)} %bitcast.62) | data formatting | bytes 786432
  61.0 4.2 %all-to-all-start = ((bf16[4,2,24576]{2,1,0:T(2,128)(2,1)}), bf16[4,2,24576]{2,1,0:T(2,128)(2,1)}, u32[]{:S(2)}, u32[]{:S(2)}) async-start(bf16[4,2,24576]{2,1,0:T(2,128)(2,1)} %reshape.96), calls=%async_computation | async-start | bytes 786432 | tf_op jit(solution)/shard_map/all_to_all | solution.py:67
  65.2 0.1 iota_compare_fusion
  66.6 2.2 %reshape_squeeze.13 = bf16[192,12,128]{2,1,0:T(8,128)(2,1)} reshape(bf16[1,1,1,192,1536]{4,3,2,1,0:T(8,128)(2,1)} %get-tuple-element.9) | data formatting | bytes 1179648 | tf_op jit(solution)/shard_map/reshape;squeeze | solution.py:30
  70.1 1.1 fusion.56
  71.2 1.5 %all-to-all-done = bf16[4,2,24576]{2,1,0:T(2,128)(2,1)} async-done(((bf16[4,2,24576]{2,1,0:T(2,128)(2,1)}), bf16[4,2,24576]{2,1,0:T(2,128)(2,1)}, u32[]{:S(2)}, u32[]{:S(2)}) %all-to-all-start) | async-done | bytes 393248 | tf_op jit(solution)/shard_map/all_to_all | solution.py:67
  72.7 3.5 %reshape.97 = bf16[6144,1,1,2,16]{4,3,2,1,0:T(2,128)(2,1)S(1)} reshape(bf16[4,2,24576]{2,1,0:T(2,128)(2,1)} %all-to-all-done) | data formatting | bytes 786432
  76.2 4.8 %copy.111 = bf16[1,1,2,16,4,1536]{5,4,3,2,1,0:T(4,128)(2,1)} copy(bf16[1,1,2,16,4,1536]{3,2,5,4,1,0:T(2,128)(2,1)S(1)} %bitcast.63) | data formatting | bytes 786432 | tf_op jit(solution)/shard_map/all_to_all | solution.py:67
  81.1 1.1 copy.88
  82.3 0.1 select_n.42
  82.4 3.0 %fusion.27 = f32[64,12]{0,1:T(8,128)S(1)} fusion(bf16[192,12,128]{2,1,0:T(8,128)(2,1)S(1)} %copy-done.8, bf16[64,12,128]{2,1,0:T(8,128)(2,1)S(1)} %select_n.42, f32[12,64]{1,0:T(8,128)S(1)} %get-tuple-element.15, f32[12,64,192]{2,1,0:T(8,128)} %fusion.7), kind=kOutput, calls=%fused_computation.48 | convolution fusion | flops 38682816 | bytes 1382400 | tf_op jit(solution)/shard_map/hqk,khd->qhd/dot_general | solution.py:44
  85.4 0.5 fusion.14
  85.9 0.6 copy-done.2
  86.6 0.3 fusion.29
  86.9 0.1 copy.94
  87.0 0.1 stack_reshape.18
  87.2 0.8 select_n.46
  88.0 3.1 %fusion.16 = bf16[192,12,128]{2,0,1:T(8,128)(2,1)S(1)} fusion(bf16[64,12,128]{2,1,0:T(8,128)(2,1)S(1)} %select_n.42, f32[12,64]{1,0:T(8,128)S(1)} %get-tuple-element.15, f32[12,64,192]{2,1,0:T(8,128)} %fusion.7), kind=kOutput, calls=%fused_computation.31 | convolution fusion | flops 38486976 | bytes 1379328 | tf_op jit(solution)/shard_map/hqk,qhd->khd/dot_general | solution.py:48
  91.1 0.4 copy.106
  91.5 0.4 stack_reshape.21
  91.9 0.4 fusion.15
  92.3 0.4 copy.104
  92.7 0.4 stack_reshape.20
  93.1 0.7 constant_dynamic-update-slice_fusion.1
  93.8 1.5 %fusion.53 = (bf16[1,192,1536]{2,1,0:T(8,128)(2,1)S(1)}, bf16[1,192,1536]{2,1,0:T(8,128)(2,1)S(1)}, bf16[1,192,1536]{2,1,0:T(8,128)(2,1)S(1)}) fusion(bf16[3,192,1536]{2,1,0:T(8,128)(2,1)} %collective-permute-done.1), kind=kLoop, calls=%fused_computation.85 | loop fusion | bytes 3538944 | tf_op jit(solution)/shard_map/slice | solution.py:26
  95.4 1.3 %reshape_squeeze.15 = bf16[192,12,128]{2,1,0:T(8,128)(2,1)} reshape(bf16[1,192,1536]{2,1,0:T(8,128)(2,1)S(1)} %get-tuple-element.6) | data formatting | bytes 1179648 | tf_op jit(solution)/shard_map/reshape;squeeze | solution.py:30
  96.7 0.4 reshape_squeeze.14
  97.1 0.1 constant_dynamic-slice_fusion
  97.2 0.1 reshape.95
  97.3 0.5 fusion.10
  97.8 1.1 fusion.57
  98.9 2.5 %fusion.18 = bf16[192,12,128]{2,0,1:T(8,128)(2,1)} fusion(bf16[64,12,128]{2,1,0:T(8,128)(2,1)S(1)} %copy-done.10, f32[12,64]{1,0:T(8,128)S(1)} %get-tuple-element.17, f32[12,64,192]{2,1,0:T(8,128)S(1)} %fusion.10), kind=kOutput, calls=%fused_computation.33 | convolution fusion | flops 38486976 | bytes 1379328 | tf_op jit(solution)/shard_map/hqk,qhd->khd/dot_general | solution.py:48
  101.4 2.7 %fusion.28 = f32[64,12]{0,1:T(8,128)S(1)} fusion(bf16[192,12,128]{2,1,0:T(8,128)(2,1)} %reshape_squeeze.15, bf16[64,12,128]{2,1,0:T(8,128)(2,1)S(1)} %copy-done.10, f32[12,64]{1,0:T(8,128)S(1)} %get-tuple-element.17, f32[12,64,192]{2,1,0:T(8,128)S(1)} %fusion.10), kind=kOutput, calls=%fused_computation.49 | convolution fusion | flops 38682816 | bytes 1382400 | tf_op jit(solution)/shard_map/hqk,khd->qhd/dot_general | solution.py:44
  104.1 1.9 %fusion.13 = bf16[12,64,192]{2,1,0:T(8,128)(2,1)S(1)} fusion(bf16[192,12,128]{2,1,0:T(8,128)(2,1)} %reshape_squeeze.15, f32[12,64]{1,0:T(8,128)S(1)} %bitcast.68, f32[12,64,192]{2,1,0:T(8,128)} %get-tuple-element.18, f32[12,64]{1,0:T(8,128)S(1)} %get-tuple-element.17, bf16[64,12,128]{2,1,0:T(8,128)(2,1)S(1)} %copy-done.10), kind=kOutput, calls=%fused_computation.28 | convolution fusion | flops 38486016 | bytes 1677312 | tf_op jit(solution)/shard_map/qhd,khd->hqk/dot_general | solution.py:51
  106.0 1.0 fusion.30
  107.0 0.4 fusion.17
  107.4 0.4 copy.110
  107.8 0.4 stack_reshape.23
  108.2 0.4 copy.108
  108.6 0.4 stack_reshape.22
  109.0 0.2 maximum_bitcast_fusion
  109.2 1.6 %fusion.2 = bf16[1,1,2,2,192,1536]{5,4,3,2,1,0:T(8,128)(2,1)} fusion(bf16[1,2,192,1536]{3,2,1,0:T(8,128)(2,1)S(1)} %get-tuple-element.20, bf16[1,2,192,1536]{3,2,1,0:T(8,128)(2,1)S(1)} %get-tuple-element.19), kind=kLoop, calls=%fused_computation.7 | loop fusion | flops 1179648 | bytes 4718592 | tf_op jit(solution)/shard_map/broadcast_in_dim | solution.py:85
  110.9 0.4 convert_reduce_fusion.1
  111.2 0.5 copy-done.6
  111.8 0.1 copy.102
  111.9 0.1 stack_reshape.19
  112.1 0.0 copy-start.5
  112.1 0.1 convert_reduce_fusion.2
  112.3 9.0 %psum.7 = f32[1,3,1536]{2,0,1:T(1,128)} all-reduce(f32[1,3,1536]{2,0,1:T(1,128)S(1)} %broadcast_in_dim.44), channel_id=1, replica_groups=mesh['dp'=2,'pipe'=4,'tensor'=4] {'dp'}, use_global_device_ids=true, to_apply=%region_9.10 | all-reduce | flops 4608 | bytes 36864 | tf_op jit(solution)/shard_map/psum | solution.py:84
  (26 shorter events, 0.1 us)
Async XLA Ops:
  0.6 3.1 %copy-start = (s32[1,4,2]{1,2,0:T(2,128)S(1)}, s32[1,4,2]{1,2,0:T(2,128)}, u32[]{:S(2)}) copy-start(s32[1,4,2]{1,2,0:T(2,128)} %param.9) | copy-start | bytes 100
  0.6 50.3 %collective-permute-start = (bf16[1,1,2,16,6144]{4,3,2,1,0:T(8,128)(2,1)}, bf16[1,1,2,16,6144]{4,3,2,1,0:T(8,128)(2,1)}, u32[]{:S(2)}, u32[]{:S(2)}) collective-permute-start(bf16[1,1,2,16,6144]{4,3,2,1,0:T(8,128)(2,1)} %param.7), channel_id=1, source_target_pairs={{0,12},{4,0},{8,4},{12,8},{1,13},{5,1},{9,5},{13,9},{2,14},{6,2},{... | collective-permute-start | bytes 1179656 | tf_op jit(solution)/shard_map/ppermute | solution.py:17
  0.7 93.1 %collective-permute-start.1 = (bf16[3,192,1536]{2,1,0:T(8,128)(2,1)}, bf16[3,192,1536]{2,1,0:T(8,128)(2,1)}, u32[]{:S(2)}, u32[]{:S(2)}) collective-permute-start(bf16[3,192,1536]{2,1,0:T(8,128)(2,1)} %bitcast.67), channel_id=1, source_target_pairs={{0,8},{4,12},{8,0},{12,4},{1,9},{5,13},{9,1},{13,5},{2,10},{6,14},... | collective-permute-start | bytes 5308424 | tf_op jit(solution)/shard_map/ppermute | solution.py:17
  9.9 2.2 %copy-start.1 = (bf16[192,12,128]{2,1,0:T(8,128)(2,1)}, bf16[192,12,128]{2,1,0:T(8,128)(2,1)S(1)}, u32[]{:S(2)}) copy-start(bf16[192,12,128]{2,1,0:T(8,128)(2,1)S(1)} %reshape_squeeze.12) | copy-start | bytes 1769476
  61.0 9.1 %copy-start.3 = (f32[12,64,192]{2,1,0:T(8,128)S(1)}, f32[12,64,192]{2,1,0:T(8,128)}, u32[]{:S(2)}) copy-start(f32[12,64,192]{2,1,0:T(8,128)} %fusion.7) | copy-start | bytes 1769476
  61.0 11.7 %all-to-all-start = ((bf16[4,2,24576]{2,1,0:T(2,128)(2,1)}), bf16[4,2,24576]{2,1,0:T(2,128)(2,1)}, u32[]{:S(2)}, u32[]{:S(2)}) async-start(bf16[4,2,24576]{2,1,0:T(2,128)(2,1)} %reshape.96), calls=%async_computation | async-start | bytes 786432 | tf_op jit(solution)/shard_map/all_to_all | solution.py:67
  81.1 1.3 %copy-start.8 = (bf16[192,12,128]{2,1,0:T(8,128)(2,1)S(1)}, bf16[192,12,128]{2,1,0:T(8,128)(2,1)}, u32[]{:S(2)}) copy-start(bf16[192,12,128]{2,1,0:T(8,128)(2,1)} %reshape_squeeze.13) | copy-start | bytes 1769476
  82.4 3.0 %copy-start.7 = (f32[12,64,192]{2,1,0:T(8,128)S(1)}, f32[12,64,192]{2,1,0:T(8,128)}, u32[]{:S(2)}) copy-start(f32[12,64,192]{2,1,0:T(8,128)} %get-tuple-element.16) | copy-start | bytes 1769476
  85.4 1.1 copy-start.2
  97.8 1.1 copy-start.10
  106.0 1.4 %copy-start.9 = (bf16[192,12,128]{2,0,1:T(8,128)(2,1)S(1)}, bf16[192,12,128]{2,0,1:T(8,128)(2,1)}, u32[]{:S(2)}) copy-start(bf16[192,12,128]{2,0,1:T(8,128)(2,1)} %fusion.18) | copy-start | bytes 1769476
  110.8 0.9 copy-start.6
  110.9 1.2 %copy-start.4 = (bf16[2,64,1536]{2,1,0:T(8,128)(2,1)S(1)}, bf16[2,64,1536]{2,1,0:T(8,128)(2,1)}, u32[]{:S(2)}) copy-start(bf16[2,64,1536]{2,1,0:T(8,128)(2,1)} %constant_dynamic-update-slice_fusion.1) | copy-start | bytes 1179652
  112.1 9.2 %copy-start.5 = (bf16[2,64,1536]{2,1,0:T(8,128)(2,1)}, bf16[2,64,1536]{2,1,0:T(8,128)(2,1)S(1)}, u32[]{:S(2)}) copy-start(bf16[2,64,1536]{2,1,0:T(8,128)(2,1)S(1)} %constant_dynamic-update-slice_fusion) | copy-start | bytes 1179652
where the time goes:
time: 122 us; the launch traced here: 121 us
  waiting for transfers between devices  40.4 us (33%)
  local copies, waits for them, and re-layouts  35.5 us (29%)
  matrix products  17.6 us (14%)
  blocking collectives  9.02 us (7%)
  starting transfers between devices  7.32 us (6%)
  other arithmetic  5.92 us (5%)
  between operations  5.53 us (5%)
    ppermute x2, waiting for transfers between devices, from_behind(): return lax.ppermute(value, axis, pairs)  38.8 us
    unnamed x25, local copies, waits for them, and re-layouts  9.33 us
    psum x1, blocking collectives, body(): bias_grad = lax.psum(column_sums, 'dp')  9.02 us
    ppermute x1, local copies, waits for them, and re-layouts, from_behind(): return lax.ppermute(value, axis, pairs)  6.09 us
    all_to_all x2, local copies, waits for them, and re-layouts, body(): lax.all_to_all(arrived, 'tensor', split_axis=4, concat_axis=3, tiled=True)  5.98 us
    dot_general x2, matrix products, slice_backward(): jnp.einsum('hqk,khd->qhd', attention_low, value_rows, preferred_element_t...  5.64 us
    dot_general x2, matrix products, slice_backward(): jnp.einsum('hqk,qhd->khd', attention_low, out_grad, preferred_element_typ...  5.59 us
    all_to_all x1, starting transfers between devices, body(): lax.all_to_all(arrived, 'tensor', split_axis=4, concat_axis=3, tiled=True)  4.24 us
  transfers between devices with their start and end apart: 3, of which 2 were waited for; matrix products, arithmetic and copies ran while one was open for 33% of the time, Pallas kernels for 0%

commit v1 on v0

v1 whole, which is shorter than its diff:
```python
import math

import jax
import jax.numpy as jnp
from jax import lax
from jax.experimental import pallas as pl
from jax.experimental.pallas import tpu as pltpu
from jax.sharding import PartitionSpec as P

HD = 128
MASK_FILL = -1e30
MAX_CHUNKS = 4
NT_DIMS = (((1,), (1,)), ((), ()))


def from_behind(value, axis, steps):
    count = lax.axis_size(axis)
    pairs = [(source, (source + steps) % count) for source in range(count)]
    return lax.ppermute(value, axis, pairs)


def head_backward(q, k, v, g, visible):
    f32, bf16 = jnp.float32, jnp.bfloat16
    scale = 1.0 / math.sqrt(HD)
    s = lax.dot_general(q, k, NT_DIMS, preferred_element_type=f32) * scale
    s = jnp.where(visible, s, MASK_FILL)
    m = jnp.max(s, axis=1, keepdims=True)
    e = jnp.exp(s - m)
    p = e / jnp.sum(e, axis=1, keepdims=True)
    p_low = p.astype(bf16)
    ctx = jnp.dot(p_low, v, preferred_element_type=f32).astype(bf16)
    delta = jnp.sum(g.astype(f32) * ctx.astype(f32), axis=1, keepdims=True)
    dp = lax.dot_general(g, v, NT_DIMS, preferred_element_type=f32)
    ds = (p * (dp - delta) * scale).astype(bf16)
    dq = jnp.dot(ds, k, preferred_element_type=f32).astype(bf16)
    dk = jnp.dot(ds.T, q, preferred_element_type=f32).astype(bf16)
    dv = jnp.dot(p_low.T, g, preferred_element_type=f32).astype(bf16)
    return dq, dk, dv


def backward_kernel(sliced, off_ref, x_ref, g_ref, dq_ref, dk_ref, dv_ref, sum_ref):
    offset = off_ref[0]
    rows = g_ref.shape[0]
    keys = dk_ref.shape[0]
    heads = g_ref.shape[1] // HD
    pos = offset + lax.broadcasted_iota(jnp.int32, (rows, keys), 0)
    col = lax.broadcasted_iota(jnp.int32, (rows, keys), 1)
    visible = col <= pos
    f32 = jnp.float32

    def head(h, carry):
        cols = pl.ds(pl.multiple_of(h * HD, HD), HD)
        if sliced:
            q = x_ref[pl.ds(0, rows), cols]
            k = x_ref[pl.ds(rows, keys), cols]
            v = x_ref[pl.ds(rows + keys, keys), cols]
        else:
            start = pl.multiple_of(offset, 16)
            q = x_ref[0, pl.ds(start, rows), cols]
            k = x_ref[1, :, cols]
            v = x_ref[2, :, cols]
        g = g_ref[:, cols]
        dq, dk, dv = head_backward(q, k, v, g, visible)
        dq_ref[:, cols] = dq
        dk_ref[:, cols] = dk
        dv_ref[:, cols] = dv
        sum_ref[pl.ds(0, 1), cols] = jnp.sum(dq.astype(f32), axis=0, keepdims=True)
        sum_ref[pl.ds(1, 1), cols] = jnp.sum(dk.astype(f32), axis=0, keepdims=True)
        sum_ref[pl.ds(2, 1), cols] = jnp.sum(dv.astype(f32), axis=0, keepdims=True)
        return carry

    lax.fori_loop(0, heads, head, 0)


def slice_backward(x, g, offset, sliced):
    rows, feats = g.shape
    keys = (x.shape[0] - rows) // 2 if sliced else x.shape[1]
    heads = feats // HD
    bf16 = jnp.bfloat16
    out_shape = (
        jax.ShapeDtypeStruct((rows, feats), bf16),
        jax.ShapeDtypeStruct((keys, feats), bf16),
        jax.ShapeDtypeStruct((keys, feats), bf16),
        jax.ShapeDtypeStruct((3, feats), jnp.float32),
    )
    vmem = pl.BlockSpec(memory_space=pltpu.VMEM)
    cost = pl.CostEstimate(
        flops=heads * 12 * rows * keys * HD,
        transcendentals=heads * rows * keys,
        bytes_accessed=2 * feats * (3 * rows + 4 * keys),
    )
    kernel = lambda *refs: backward_kernel(sliced, *refs)
    return pl.pallas_call(
        kernel,
        out_shape=out_shape,
        in_specs=[pl.BlockSpec(memory_space=pltpu.SMEM), vmem, vmem],
        out_specs=(vmem, vmem, vmem, vmem),
        cost_estimate=cost,
        name="slice_backward",
    )(jnp.reshape(offset, (1,)).astype(jnp.int32), x, g)


def chunk_count(heads):
    for count in range(min(MAX_CHUNKS, heads), 0, -1):
        if heads % count == 0:
            return count
    return 1


def body(kept_qkv, held_qkv, sent_grad, order, offsets):
    section_count = lax.axis_size("pipe")
    half_way = section_count // 2
    section_index = lax.axis_index("pipe")
    feats = kept_qkv.shape[-1]
    keys = kept_qkv.shape[-2]
    heads = feats // HD

    owner = (section_index + section_count - half_way) % section_count
    owner_offset = lax.dynamic_index_in_dim(offsets[0], owner, 0, keepdims=False)[1]
    rows = sent_grad.shape[3] * lax.axis_size("tensor")
    held = held_qkv[0, 0]
    held_q = lax.dynamic_slice_in_dim(held[0], owner_offset, rows, 0)
    packed = jnp.concatenate([held_q, held[1], held[2]], axis=0)
    chunks = chunk_count(heads)
    width = feats // chunks
    parts = packed.reshape(packed.shape[0], chunks, width).transpose(1, 0, 2)
    fetched = [from_behind(parts[c], "pipe", half_way) for c in range(chunks)]

    arrived = from_behind(sent_grad[0, 0], "pipe", -1)
    tensor_count = lax.axis_size("tensor")
    local_rows = arrived.shape[1]
    split = arrived.reshape(2, local_rows, tensor_count, feats).transpose(2, 0, 1, 3)
    regrouped = lax.all_to_all(split, "tensor", split_axis=0, concat_axis=0, tiled=True)
    regrouped = regrouped.transpose(1, 0, 2, 3).reshape(2, rows, feats)
    pick = order[0, 0]
    grad_kept = lax.dynamic_index_in_dim(regrouped, pick, 0, keepdims=False)
    grad_held = lax.dynamic_index_in_dim(regrouped, 1 - pick, 0, keepdims=False)

    section_offsets = lax.dynamic_index_in_dim(offsets[0], section_index, 0, keepdims=False)
    kept_q, kept_k, kept_v, kept_sums = slice_backward(
        kept_qkv[0, 0], grad_kept, section_offsets[0], sliced=False
    )
    held_parts = []
    for c in range(chunks):
        g_part = grad_held[:, c * width:(c + 1) * width]
        held_parts.append(slice_backward(fetched[c], g_part, section_offsets[1], sliced=True))
    held_q = jnp.concatenate([part[0] for part in held_parts], axis=1)
    held_k = jnp.concatenate([part[1] for part in held_parts], axis=1)
    held_v = jnp.concatenate([part[2] for part in held_parts], axis=1)
    held_sums = jnp.concatenate([part[3] for part in held_parts], axis=1)

    query_grad = jnp.stack([kept_q, held_q])
    key_value_grad = jnp.stack([jnp.stack([kept_k, kept_v]), jnp.stack([held_k, held_v])])
    column_sums = kept_sums + held_sums
    if lax.axis_size("dp") == 2:
        bias_grad = column_sums + from_behind(column_sums, "dp", 1)
    else:
        bias_grad = lax.psum(column_sums, "dp")
    return (query_grad[None, None], key_value_grad[None, None], bias_grad[None])


def solution(mesh):
    return jax.shard_map(
        body,
        mesh=mesh,
        in_specs=(
            P("dp", "pipe", None, None, "tensor"),
            P("dp", "pipe", None, None, "tensor"),
            P("dp", "pipe", None, "tensor", None),
            P("dp", "pipe"),
            P("dp", None, None),
        ),
        out_specs=(
            P("dp", "pipe", None, None, "tensor"),
            P("dp", "pipe", None, None, None, "tensor"),
            P("pipe", None, "tensor"),
        ),
        check_vma=False,
    )
```

time: 122 us -> 106 us (0.87)
  the two profiles are of different devices: /device:TPU:8 before, /device:TPU:0 now
where the time goes in v1:
time: 106 us; the launch traced here: 105 us
  waiting for transfers between devices  40.7 us (38%)
  Pallas kernels  30.5 us (29%)
  starting transfers between devices  16.1 us (15%)
  local copies, waits for them, and re-layouts  9.65 us (9%)
  other arithmetic  4.96 us (5%)
  between operations  3.51 us (3%)
    ppermute x6, waiting for transfers between devices, from_behind(): return lax.ppermute(value, axis, pairs)  40.6 us
    pallas_call x5, Pallas kernels, slice_backward(): pl.pallas_call(kernel, out_shape=out_shape, in_specs=[pl.BlockSpec(memory...  30.5 us
    ppermute x6, starting transfers between devices, from_behind(): return lax.ppermute(value, axis, pairs)  12.6 us
    unnamed x43, local copies, waits for them, and re-layouts  3.76 us
    all_to_all x1, starting transfers between devices, body(): lax.all_to_all(split, 'tensor', split_axis=0, concat_axis=0, tiled=True)  3.46 us
    broadcast_in_dim x3, other arithmetic, body(): return (query_grad[None, None], key_value_grad[None, None], bias_grad[None])  2.4 us
  transfers between devices with their start and end apart: 7, of which 5 were waited for; matrix products, arithmetic and copies ran while one was open for 9% of the time, Pallas kernels for 25%

profile of v1, /device:TPU:0, one launch (start us, length us, event | category | flops | bytes accessed | tf_op | source)
XLA Modules:
  0.0 105.4 jit_solution(3984833029844141926)
XLA Ops:
  0.6 5.1 %collective-permute-start = (bf16[2,16,6144]{2,1,0:T(8,128)(2,1)}, bf16[2,16,6144]{2,1,0:T(8,128)(2,1)S(1)}, u32[]{:S(2)}, u32[]{:S(2)}) collective-permute-start(bf16[2,16,6144]{2,1,0:T(8,128)(2,1)} %bitcast.60), channel_id=1, source_target_pairs={{0,12},{4,0},{8,4},{12,8},{1,13},{5,1},{9,5},{13,9},{2,14},{6,2},{... | collective-permute-start | bytes 1179656 | tf_op jit(solution)/shard_map/ppermute | solution.py:19
  5.7 1.5 %fusion = (bf16[1,1,1,192,1536]{4,3,2,1,0:T(8,128)(2,1)S(1)}, bf16[1,1,1,192,1536]{4,3,2,1,0:T(8,128)(2,1)S(1)}, bf16[1,1,1,192,1536]{4,3,2,1,0:T(8,128)(2,1)S(1)}) fusion(bf16[1,1,3,192,1536]{4,3,2,1,0:T(8,128)(2,1)} %param.6), kind=kLoop, calls=%fused_computation.19 | loop fusion | bytes 3538944 | tf_op jit(solution)/shard_map/slice | solution.py:122
  7.3 0.0 copy-done.20
  7.3 0.1 constant_dynamic-slice_fusion.1
  7.4 0.5 slice.60
  9.8 0.1 constant_dynamic-slice_fusion
  9.9 0.1 concatenate.22
  10.0 0.1 concatenate.24
  10.1 0.1 copy.23
  10.2 0.1 concatenate.23
  10.4 0.1 copy.22
  10.4 0.1 maximum_bitcast_fusion.1
  10.6 3.8 %collective-permute-done = bf16[2,16,6144]{2,1,0:T(8,128)(2,1)S(1)} collective-permute-done((bf16[2,16,6144]{2,1,0:T(8,128)(2,1)}, bf16[2,16,6144]{2,1,0:T(8,128)(2,1)S(1)}, u32[]{:S(2)}, u32[]{:S(2)}) %collective-permute-start) | collective-permute-done | bytes 393248 | tf_op jit(solution)/shard_map/ppermute | solution.py:19
  14.4 0.3 reshape.34
  14.7 0.8 copy.19
  15.5 3.5 %all-to-all-start = ((bf16[4,2,16,1536]{3,2,1,0:T(8,128)(2,1)}), bf16[4,2,16,1536]{3,2,1,0:T(8,128)(2,1)S(1)}, u32[]{:S(2)}, u32[]{:S(2)}) async-start(bf16[4,2,16,1536]{3,2,1,0:T(8,128)(2,1)} %copy.19), calls=%async_computation | async-start | bytes 786432 | tf_op jit(solution)/shard_map/all_to_all | solution.py:133
  19.0 0.1 slice_bitcast_fusion.3
  19.1 1.4 %collective-permute-start.1 = (bf16[448,384]{1,0:T(8,128)(2,1)S(1)}, bf16[448,384]{1,0:T(8,128)(2,1)S(1)}, u32[]{:S(2)}, u32[]{:S(2)}) collective-permute-start(bf16[448,384]{1,0:T(8,128)(2,1)S(1)} %get-tuple-element.58), channel_id=1, source_target_pairs={{0,8},{4,12},{8,0},{12,4},{1,9},{5,13},{9,1},{13,5},{2,10},{6,14},... | collective-permute-start | bytes 1032200 | tf_op jit(solution)/shard_map/ppermute | solution.py:19
  20.6 1.6 %collective-permute-start.4 = (bf16[448,384]{1,0:T(8,128)(2,1)S(1)}, bf16[448,384]{1,0:T(8,128)(2,1)S(1)}, u32[]{:S(2)}, u32[]{:S(2)}) collective-permute-start(bf16[448,384]{1,0:T(8,128)(2,1)S(1)} %get-tuple-element.59), channel_id=1, source_target_pairs={{0,8},{4,12},{8,0},{12,4},{1,9},{5,13},{9,1},{13,5},{2,10},{6,14},... | collective-permute-start | bytes 1032200 | tf_op jit(solution)/shard_map/ppermute | solution.py:19
  22.1 1.4 %collective-permute-start.3 = (bf16[448,384]{1,0:T(8,128)(2,1)S(1)}, bf16[448,384]{1,0:T(8,128)(2,1)S(1)}, u32[]{:S(2)}, u32[]{:S(2)}) collective-permute-start(bf16[448,384]{1,0:T(8,128)(2,1)S(1)} %get-tuple-element.60), channel_id=1, source_target_pairs={{0,8},{4,12},{8,0},{12,4},{1,9},{5,13},{9,1},{13,5},{2,10},{6,14},... | collective-permute-start | bytes 1032200 | tf_op jit(solution)/shard_map/ppermute | solution.py:19
  23.5 1.6 %collective-permute-start.2 = (bf16[448,384]{1,0:T(8,128)(2,1)S(1)}, bf16[448,384]{1,0:T(8,128)(2,1)S(1)}, u32[]{:S(2)}, u32[]{:S(2)}) collective-permute-start(bf16[448,384]{1,0:T(8,128)(2,1)S(1)} %get-tuple-element.61), channel_id=1, source_target_pairs={{0,8},{4,12},{8,0},{12,4},{1,9},{5,13},{9,1},{13,5},{2,10},{6,14},... | collective-permute-start | bytes 1032200 | tf_op jit(solution)/shard_map/ppermute | solution.py:19
  25.7 0.5 fusion.2
  26.3 0.1 all-to-all-done
  26.4 0.7 dynamic-slice_bitcast_fusion.1
  27.1 0.7 fusion.1
  27.8 32.6 %collective-permute-done.1.refs_1_ = bf16[448,384]{1,0:T(8,128)(2,1)S(1)} collective-permute-done((bf16[448,384]{1,0:T(8,128)(2,1)S(1)}, bf16[448,384]{1,0:T(8,128)(2,1)S(1)}, u32[]{:S(2)}, u32[]{:S(2)}) %collective-permute-start.1) | collective-permute-done | bytes 344096 | tf_op jit(solution)/shard_map/ppermute | solution.py:19
  60.5 0.7 copy-done.3
  61.2 4.6 %slice_backward.6 = (bf16[64,384]{1,0:T(8,128)(2,1)}, bf16[192,384]{1,0:T(8,128)(2,1)}, bf16[192,384]{1,0:T(8,128)(2,1)}, f32[3,384]{1,0:T(4,128)}) custom-call(s32[1]{0:T(128)} %bitcast.9.refs_0_, bf16[448,384]{1,0:T(8,128)(2,1)} %copy-done.3, bf16[64,384]{1,0:T(8,128)(2,1)} %get-tuple-element.64.refs_2_), custom_call_target="tpu_custom_call" | custom-call | flops 56623104 | bytes 737280 | tf_op jit(solution)/shard_map/slice_backward/pallas_call | solution.py:93
  65.8 2.1 %collective-permute-done.4.refs_1_ = bf16[448,384]{1,0:T(8,128)(2,1)S(1)} collective-permute-done((bf16[448,384]{1,0:T(8,128)(2,1)S(1)}, bf16[448,384]{1,0:T(8,128)(2,1)S(1)}, u32[]{:S(2)}, u32[]{:S(2)}) %collective-permute-start.4) | collective-permute-done | bytes 344096 | tf_op jit(solution)/shard_map/ppermute | solution.py:19
  67.8 0.7 copy-done.2
  68.6 4.6 %slice_backward.9 = (bf16[64,384]{1,0:T(8,128)(2,1)}, bf16[192,384]{1,0:T(8,128)(2,1)}, bf16[192,384]{1,0:T(8,128)(2,1)}, f32[3,384]{1,0:T(4,128)}) custom-call(s32[1]{0:T(128)} %bitcast.9.refs_0_, bf16[448,384]{1,0:T(8,128)(2,1)} %copy-done.2, bf16[64,384]{1,0:T(8,128)(2,1)} %get-tuple-element.65.refs_2_), custom_call_target="tpu_custom_call" | custom-call | flops 56623104 | bytes 737280 | tf_op jit(solution)/shard_map/slice_backward/pallas_call | solution.py:93
  73.2 2.0 %collective-permute-done.3.refs_1_ = bf16[448,384]{1,0:T(8,128)(2,1)S(1)} collective-permute-done((bf16[448,384]{1,0:T(8,128)(2,1)S(1)}, bf16[448,384]{1,0:T(8,128)(2,1)S(1)}, u32[]{:S(2)}, u32[]{:S(2)}) %collective-permute-start.3) | collective-permute-done | bytes 344096 | tf_op jit(solution)/shard_map/ppermute | solution.py:19
  75.2 0.7 copy-done.1
  75.9 4.6 %slice_backward.8 = (bf16[64,384]{1,0:T(8,128)(2,1)}, bf16[192,384]{1,0:T(8,128)(2,1)}, bf16[192,384]{1,0:T(8,128)(2,1)}, f32[3,384]{1,0:T(4,128)}) custom-call(s32[1]{0:T(128)} %bitcast.9.refs_0_, bf16[448,384]{1,0:T(8,128)(2,1)} %copy-done.1, bf16[64,384]{1,0:T(8,128)(2,1)} %get-tuple-element.66.refs_2_), custom_call_target="tpu_custom_call" | custom-call | flops 56623104 | bytes 737280 | tf_op jit(solution)/shard_map/slice_backward/pallas_call | solution.py:93
  80.5 12.2 %slice_backward.5 = (bf16[64,1536]{1,0:T(8,128)(2,1)}, bf16[192,1536]{1,0:T(8,128)(2,1)}, bf16[192,1536]{1,0:T(8,128)(2,1)}, f32[3,1536]{1,0:T(4,128)}) custom-call(s32[1]{0:T(128)} %bitcast.refs_0_, bf16[3,192,1536]{2,1,0:T(8,128)(2,1)} %bitcast.54, bf16[64,1536]{1,0:T(8,128)(2,1)} %get-tuple-element.62.refs_2_), custom_call_target="tpu_custom_call" | custom-call | flops 226492416 | bytes 2949120 | tf_op jit(solution)/shard_map/slice_backward/pallas_call | solution.py:93
  92.7 0.0 collective-permute-done.2.refs_1_
  92.7 0.7 copy-done
  93.4 4.6 %slice_backward.7 = (bf16[64,384]{1,0:T(8,128)(2,1)}, bf16[192,384]{1,0:T(8,128)(2,1)}, bf16[192,384]{1,0:T(8,128)(2,1)}, f32[3,384]{1,0:T(4,128)}) custom-call(s32[1]{0:T(128)} %bitcast.9.refs_0_, bf16[448,384]{1,0:T(8,128)(2,1)} %copy-done, bf16[64,384]{1,0:T(8,128)(2,1)} %get-tuple-element.67.refs_2_), custom_call_target="tpu_custom_call" | custom-call | flops 56623104 | bytes 737280 | tf_op jit(solution)/shard_map/slice_backward/pallas_call | solution.py:93
  98.0 0.0 copy-done.17
  98.0 0.0 copy-done.18
  98.0 0.0 copy-done.19
  98.0 0.8 maximum_add_fusion
  98.8 1.6 %collective-permute-start.5 = (f32[3,1536]{1,0:T(4,128)S(1)}, f32[3,1536]{1,0:T(4,128)S(1)}, u32[]{:S(2)}, u32[]{:S(2)}) collective-permute-start(f32[3,1536]{1,0:T(4,128)S(1)} %maximum_add_fusion), channel_id=1, source_target_pairs={{0,16},{16,0},{1,17},{17,1},{2,18},{18,2},{3,19},{19,3},{4,20},{20... | collective-permute-start | bytes 55304 | tf_op jit(solution)/shard_map/ppermute | solution.py:19
  100.4 0.0 copy-start.9
  100.4 0.0 copy-start.10
  100.4 0.0 copy-start.11
  100.4 0.0 copy-start.12
  100.4 1.4 %maximum_bitcast_fusion.2 = bf16[1,2,192,1536]{3,2,1,0:T(8,128)(2,1)S(1)} fusion(bf16[1,192,1536]{2,1,0:T(8,128)(2,1)} %bitcast.58, bf16[1,192,1536]{2,1,0:T(8,128)(2,1)} %bitcast.57), kind=kLoop, calls=%fused_computation.2 | loop fusion | flops 589824 | bytes 2359296 | tf_op jit(solution)/shard_map/stack | solution.py:153
  101.9 0.0 copy-done.9
  101.9 0.0 copy-done.10
  102.0 0.0 copy-done.11
  102.0 0.0 copy-done.12
  102.1 0.1 maximum_bitcast_fusion.4
  102.2 0.1 maximum_bitcast_fusion.3
  102.3 0.0 copy-start.13
  102.3 0.0 copy-start.14
  102.3 0.0 copy-start.15
  102.3 0.0 copy-start.16
  102.3 0.0 copy-start.4
  102.3 1.6 %maximum_bitcast_fusion = bf16[1,1,2,2,192,1536]{5,4,3,2,1,0:T(8,128)(2,1)} fusion(bf16[1,2,192,1536]{3,2,1,0:T(8,128)(2,1)S(1)} %maximum_bitcast_fusion.3, bf16[1,2,192,1536]{3,2,1,0:T(8,128)(2,1)S(1)} %maximum_bitcast_fusion.2), kind=kLoop, calls=%fused_computation | loop fusion | flops 1179648 | bytes 4718592 | tf_op jit(solution)/shard_map/broadcast_in_dim | solution.py:159
  104.0 0.0 copy-done.16
  104.0 0.8 maximum_bitcast_fusion.6
  104.8 0.0 collective-permute-done.5
  104.8 0.6 copy.24
  (24 shorter events, 0.1 us)
Async XLA Ops:
  0.6 13.8 %collective-permute-start = (bf16[2,16,6144]{2,1,0:T(8,128)(2,1)}, bf16[2,16,6144]{2,1,0:T(8,128)(2,1)S(1)}, u32[]{:S(2)}, u32[]{:S(2)}) collective-permute-start(bf16[2,16,6144]{2,1,0:T(8,128)(2,1)} %bitcast.60), channel_id=1, source_target_pairs={{0,12},{4,0},{8,4},{12,8},{1,13},{5,1},{9,5},{13,9},{2,14},{6,2},{... | collective-permute-start | bytes 1179656 | tf_op jit(solution)/shard_map/ppermute | solution.py:19
  5.7 1.6 %copy-start.20 = (s32[1,4,2]{1,2,0:T(2,128)S(1)}, s32[1,4,2]{1,2,0:T(2,128)}, u32[]{:S(2)}) copy-start(s32[1,4,2]{1,2,0:T(2,128)} %param.9) | copy-start | bytes 100
  15.5 10.9 %all-to-all-start = ((bf16[4,2,16,1536]{3,2,1,0:T(8,128)(2,1)}), bf16[4,2,16,1536]{3,2,1,0:T(8,128)(2,1)S(1)}, u32[]{:S(2)}, u32[]{:S(2)}) async-start(bf16[4,2,16,1536]{3,2,1,0:T(8,128)(2,1)} %copy.19), calls=%async_computation | async-start | bytes 786432 | tf_op jit(solution)/shard_map/all_to_all | solution.py:133
  19.1 41.3 %collective-permute-start.1 = (bf16[448,384]{1,0:T(8,128)(2,1)S(1)}, bf16[448,384]{1,0:T(8,128)(2,1)S(1)}, u32[]{:S(2)}, u32[]{:S(2)}) collective-permute-start(bf16[448,384]{1,0:T(8,128)(2,1)S(1)} %get-tuple-element.58), channel_id=1, source_target_pairs={{0,8},{4,12},{8,0},{12,4},{1,9},{5,13},{9,1},{13,5},{2,10},{6,14},... | collective-permute-start | bytes 1032200 | tf_op jit(solution)/shard_map/ppermute | solution.py:19
  20.6 47.3 %collective-permute-start.4 = (bf16[448,384]{1,0:T(8,128)(2,1)S(1)}, bf16[448,384]{1,0:T(8,128)(2,1)S(1)}, u32[]{:S(2)}, u32[]{:S(2)}) collective-permute-start(bf16[448,384]{1,0:T(8,128)(2,1)S(1)} %get-tuple-element.59), channel_id=1, source_target_pairs={{0,8},{4,12},{8,0},{12,4},{1,9},{5,13},{9,1},{13,5},{2,10},{6,14},... | collective-permute-start | bytes 1032200 | tf_op jit(solution)/shard_map/ppermute | solution.py:19
  22.1 53.1 %collective-permute-start.3 = (bf16[448,384]{1,0:T(8,128)(2,1)S(1)}, bf16[448,384]{1,0:T(8,128)(2,1)S(1)}, u32[]{:S(2)}, u32[]{:S(2)}) collective-permute-start(bf16[448,384]{1,0:T(8,128)(2,1)S(1)} %get-tuple-element.60), channel_id=1, source_target_pairs={{0,8},{4,12},{8,0},{12,4},{1,9},{5,13},{9,1},{13,5},{2,10},{6,14},... | collective-permute-start | bytes 1032200 | tf_op jit(solution)/shard_map/ppermute | solution.py:19
  23.5 69.2 %collective-permute-start.2 = (bf16[448,384]{1,0:T(8,128)(2,1)S(1)}, bf16[448,384]{1,0:T(8,128)(2,1)S(1)}, u32[]{:S(2)}, u32[]{:S(2)}) collective-permute-start(bf16[448,384]{1,0:T(8,128)(2,1)S(1)} %get-tuple-element.61), channel_id=1, source_target_pairs={{0,8},{4,12},{8,0},{12,4},{1,9},{5,13},{9,1},{13,5},{2,10},{6,14},... | collective-permute-start | bytes 1032200 | tf_op jit(solution)/shard_map/ppermute | solution.py:19
  60.5 0.7 copy-start.3
  67.8 0.7 copy-start.2
  75.2 0.7 copy-start.1
  80.5 17.5 %copy-start.17 = (f32[3,384]{1,0:T(4,128)S(1)}, f32[3,384]{1,0:T(4,128)}, u32[]{:S(2)}) copy-start(f32[3,384]{1,0:T(4,128)} %get-tuple-element.39) | copy-start | bytes 13828
  80.5 17.5 %copy-start.18 = (f32[3,384]{1,0:T(4,128)S(1)}, f32[3,384]{1,0:T(4,128)}, u32[]{:S(2)}) copy-start(f32[3,384]{1,0:T(4,128)} %get-tuple-element.42) | copy-start | bytes 13828
  80.5 17.5 %copy-start.19 = (f32[3,384]{1,0:T(4,128)S(1)}, f32[3,384]{1,0:T(4,128)}, u32[]{:S(2)}) copy-start(f32[3,384]{1,0:T(4,128)} %get-tuple-element.41) | copy-start | bytes 13828
  92.7 0.7 copy-start
  98.8 6.0 %collective-permute-start.5 = (f32[3,1536]{1,0:T(4,128)S(1)}, f32[3,1536]{1,0:T(4,128)S(1)}, u32[]{:S(2)}, u32[]{:S(2)}) collective-permute-start(f32[3,1536]{1,0:T(4,128)S(1)} %maximum_add_fusion), channel_id=1, source_target_pairs={{0,16},{16,0},{1,17},{17,1},{2,18},{18,2},{3,19},{19,3},{4,20},{20... | collective-permute-start | bytes 55304 | tf_op jit(solution)/shard_map/ppermute | solution.py:19
  100.4 1.5 %copy-start.5 = (bf16[192,384]{1,0:T(8,128)(2,1)S(1)}, bf16[192,384]{1,0:T(8,128)(2,1)}, u32[]{:S(2)}) copy-start(bf16[192,384]{1,0:T(8,128)(2,1)} %get-tuple-element.30) | copy-start | bytes 442372
  100.4 1.5 %copy-start.6 = (bf16[192,384]{1,0:T(8,128)(2,1)S(1)}, bf16[192,384]{1,0:T(8,128)(2,1)}, u32[]{:S(2)}) copy-start(bf16[192,384]{1,0:T(8,128)(2,1)} %get-tuple-element.34) | copy-start | bytes 442372
  100.4 1.5 %copy-start.7 = (bf16[192,384]{1,0:T(8,128)(2,1)S(1)}, bf16[192,384]{1,0:T(8,128)(2,1)}, u32[]{:S(2)}) copy-start(bf16[192,384]{1,0:T(8,128)(2,1)} %get-tuple-element.33) | copy-start | bytes 442372
  100.4 1.5 %copy-start.8 = (bf16[192,384]{1,0:T(8,128)(2,1)S(1)}, bf16[192,384]{1,0:T(8,128)(2,1)}, u32[]{:S(2)}) copy-start(bf16[192,384]{1,0:T(8,128)(2,1)} %get-tuple-element.37) | copy-start | bytes 442372
  100.4 1.5 %copy-start.9 = (bf16[192,384]{1,0:T(8,128)(2,1)S(1)}, bf16[192,384]{1,0:T(8,128)(2,1)}, u32[]{:S(2)}) copy-start(bf16[192,384]{1,0:T(8,128)(2,1)} %get-tuple-element.32) | copy-start | bytes 442372
  100.4 1.6 %copy-start.10 = (bf16[192,384]{1,0:T(8,128)(2,1)S(1)}, bf16[192,384]{1,0:T(8,128)(2,1)}, u32[]{:S(2)}) copy-start(bf16[192,384]{1,0:T(8,128)(2,1)} %get-tuple-element.36) | copy-start | bytes 442372
  100.4 1.6 %copy-start.11 = (bf16[192,384]{1,0:T(8,128)(2,1)S(1)}, bf16[192,384]{1,0:T(8,128)(2,1)}, u32[]{:S(2)}) copy-start(bf16[192,384]{1,0:T(8,128)(2,1)} %get-tuple-element.31) | copy-start | bytes 442372
  100.4 1.7 %copy-start.12 = (bf16[192,384]{1,0:T(8,128)(2,1)S(1)}, bf16[192,384]{1,0:T(8,128)(2,1)}, u32[]{:S(2)}) copy-start(bf16[192,384]{1,0:T(8,128)(2,1)} %get-tuple-element.35) | copy-start | bytes 442372
  102.3 1.7 %copy-start.13 = (bf16[64,384]{1,0:T(8,128)(2,1)S(1)}, bf16[64,384]{1,0:T(8,128)(2,1)}, u32[]{:S(2)}) copy-start(bf16[64,384]{1,0:T(8,128)(2,1)} %get-tuple-element.24) | copy-start | bytes 147460
  102.3 1.7 %copy-start.14 = (bf16[64,384]{1,0:T(8,128)(2,1)S(1)}, bf16[64,384]{1,0:T(8,128)(2,1)}, u32[]{:S(2)}) copy-start(bf16[64,384]{1,0:T(8,128)(2,1)} %get-tuple-element.27) | copy-start | bytes 147460
  102.3 1.6 %copy-start.15 = (bf16[64,384]{1,0:T(8,128)(2,1)S(1)}, bf16[64,384]{1,0:T(8,128)(2,1)}, u32[]{:S(2)}) copy-start(bf16[64,384]{1,0:T(8,128)(2,1)} %get-tuple-element.26) | copy-start | bytes 147460
  102.3 1.6 %copy-start.16 = (bf16[64,384]{1,0:T(8,128)(2,1)S(1)}, bf16[64,384]{1,0:T(8,128)(2,1)}, u32[]{:S(2)}) copy-start(bf16[64,384]{1,0:T(8,128)(2,1)} %get-tuple-element.25) | copy-start | bytes 147460
  102.3 1.7 %copy-start.4 = (bf16[64,1536]{1,0:T(8,128)(2,1)S(1)}, bf16[64,1536]{1,0:T(8,128)(2,1)}, u32[]{:S(2)}) copy-start(bf16[64,1536]{1,0:T(8,128)(2,1)} %get-tuple-element.23) | copy-start | bytes 589828

commit v2 on v1

v2 whole, which is shorter than its diff:
```python
import math

import jax
import jax.numpy as jnp
from jax import lax
from jax.experimental import pallas as pl
from jax.experimental.pallas import tpu as pltpu
from jax.sharding import PartitionSpec as P

HD = 128
MASK_FILL = -1e30
MAX_CHUNKS = 4
NT_DIMS = (((1,), (1,)), ((), ()))


def from_behind(value, axis, steps):
    count = lax.axis_size(axis)
    pairs = [(source, (source + steps) % count) for source in range(count)]
    return lax.ppermute(value, axis, pairs)


def head_backward(q, k, v, g, visible):
    f32, bf16 = jnp.float32, jnp.bfloat16
    scale = 1.0 / math.sqrt(HD)
    s = lax.dot_general(q, k, NT_DIMS, preferred_element_type=f32) * scale
    s = jnp.where(visible, s, MASK_FILL)
    m = jnp.max(s, axis=1, keepdims=True)
    e = jnp.exp(s - m)
    p = e / jnp.sum(e, axis=1, keepdims=True)
    p_low = p.astype(bf16)
    ctx = jnp.dot(p_low, v, preferred_element_type=f32).astype(bf16)
    delta = jnp.sum(g.astype(f32) * ctx.astype(f32), axis=1, keepdims=True)
    dp = lax.dot_general(g, v, NT_DIMS, preferred_element_type=f32)
    ds = (p * (dp - delta) * scale).astype(bf16)
    dq = jnp.dot(ds, k, preferred_element_type=f32).astype(bf16)
    dk = jnp.dot(ds.T, q, preferred_element_type=f32).astype(bf16)
    dv = jnp.dot(p_low.T, g, preferred_element_type=f32).astype(bf16)
    return dq, dk, dv


def head_loop(offset, load, store):
    rows, keys, heads = load.rows, load.keys, load.heads
    pos = offset + lax.broadcasted_iota(jnp.int32, (rows, keys), 0)
    col = lax.broadcasted_iota(jnp.int32, (rows, keys), 1)
    visible = col <= pos

    def head(h, carry):
        cols = pl.ds(pl.multiple_of(h * HD, HD), HD)
        q, k, v, g = load(cols)
        store(cols, *head_backward(q, k, v, g, visible))
        return carry

    lax.fori_loop(0, heads, head, 0)


class Loader:
    def __init__(self, fn, rows, keys, heads):
        self.fn, self.rows, self.keys, self.heads = fn, rows, keys, heads

    def __call__(self, cols):
        return self.fn(cols)


def store_into(qg_ref, kv_ref, sum_ref, add):
    f32 = jnp.float32

    def store(cols, dq, dk, dv):
        qg_ref[:, cols] = dq
        kv_ref[0, :, cols] = dk
        kv_ref[1, :, cols] = dv
        for row, value in enumerate((dq, dk, dv)):
            total = jnp.sum(value.astype(f32), axis=0, keepdims=True)
            if add:
                total = sum_ref[pl.ds(row, 1), cols] + total
            sum_ref[pl.ds(row, 1), cols] = total

    return store


def kept_kernel(meta_ref, x_ref, g_ref, qg_ref, kv_ref, sum_ref):
    offset = meta_ref[0]
    rows, feats = g_ref.shape
    keys = x_ref.shape[1]
    start = pl.multiple_of(offset, 16)
    load = Loader(
        lambda cols: (x_ref[0, pl.ds(start, rows), cols], x_ref[1, :, cols], x_ref[2, :, cols], g_ref[:, cols]),
        rows, keys, feats // HD,
    )
    head_loop(offset, load, store_into(qg_ref, kv_ref, sum_ref, add=False))


def held_kernel(meta_ref, x_ref, g_ref, qg_in, kv_in, sum_in, qg_ref, kv_ref, sum_ref):
    del qg_in, kv_in
    offset = meta_ref[0]
    rows, feats = g_ref.shape
    keys = (x_ref.shape[0] - rows) // 2
    load = Loader(
        lambda cols: (x_ref[pl.ds(0, rows), cols], x_ref[pl.ds(rows, keys), cols],
                      x_ref[pl.ds(rows + keys, keys), cols], g_ref[:, cols]),
        rows, keys, feats // HD,
    )
    sum_ref[...] = sum_in[...]
    head_loop(offset, load, store_into(qg_ref, kv_ref, sum_ref, add=True))


def kernel_cost(rows, keys, feats):
    heads = feats // HD
    return pl.CostEstimate(
        flops=heads * 12 * rows * keys * HD,
        transcendentals=heads * rows * keys,
        bytes_accessed=2 * feats * (3 * rows + 4 * keys),
    )


def kept_backward(stash, grads, offset, pick):
    _, keys, feats = stash.shape
    rows = grads.shape[1]
    bf16 = jnp.bfloat16
    out_shape = (
        jax.ShapeDtypeStruct((2, rows, feats), bf16),
        jax.ShapeDtypeStruct((2, 2, keys, feats), bf16),
        jax.ShapeDtypeStruct((3, feats), jnp.float32),
    )
    grid_spec = pltpu.PrefetchScalarGridSpec(
        num_scalar_prefetch=1,
        grid=(1,),
        in_specs=[
            pl.BlockSpec((3, keys, feats), lambda i, m: (0, 0, 0)),
            pl.BlockSpec((None, rows, feats), lambda i, m: (m[1], 0, 0)),
        ],
        out_specs=(
            pl.BlockSpec((None, rows, feats), lambda i, m: (0, 0, 0)),
            pl.BlockSpec((None, 2, keys, feats), lambda i, m: (0, 0, 0, 0)),
            pl.BlockSpec((3, feats), lambda i, m: (0, 0)),
        ),
    )
    meta = jnp.stack([offset, pick]).astype(jnp.int32)
    return pl.pallas_call(
        kept_kernel,
        out_shape=out_shape,
        grid_spec=grid_spec,
        cost_estimate=kernel_cost(rows, keys, feats),
        name="kept_backward",
    )(meta, stash, grads)


def held_backward(part, grads, offset, pick, chunk, qg, kv, sums):
    rows = grads.shape[1]
    width = part.shape[1]
    keys = (part.shape[0] - rows) // 2
    grid_spec = pltpu.PrefetchScalarGridSpec(
        num_scalar_prefetch=1,
        grid=(1,),
        in_specs=[
            pl.BlockSpec((part.shape[0], width), lambda i, m: (0, 0)),
            pl.BlockSpec((None, rows, width), lambda i, m: (m[1], 0, chunk)),
            pl.BlockSpec(memory_space=pl.ANY),
            pl.BlockSpec(memory_space=pl.ANY),
            pl.BlockSpec((3, width), lambda i, m: (0, chunk)),
        ],
        out_specs=(
            pl.BlockSpec((None, rows, width), lambda i, m: (1, 0, chunk)),
            pl.BlockSpec((None, 2, keys, width), lambda i, m: (1, 0, 0, chunk)),
            pl.BlockSpec((3, width), lambda i, m: (0, chunk)),
        ),
    )
    meta = jnp.stack([offset, 1 - pick]).astype(jnp.int32)
    return pl.pallas_call(
        held_kernel,
        out_shape=(
            jax.ShapeDtypeStruct(qg.shape, qg.dtype),
            jax.ShapeDtypeStruct(kv.shape, kv.dtype),
            jax.ShapeDtypeStruct(sums.shape, sums.dtype),
        ),
        grid_spec=grid_spec,
        input_output_aliases={3: 0, 4: 1, 5: 2},
        cost_estimate=kernel_cost(rows, keys, width),
        name="held_backward",
    )(meta, part, grads, qg, kv, sums)


def chunk_count(heads):
    for count in range(min(MAX_CHUNKS, heads), 0, -1):
        if heads % count == 0:
            return count
    return 1


def body(kept_qkv, held_qkv, sent_grad, order, offsets):
    section_count = lax.axis_size("pipe")
    half_way = section_count // 2
    section_index = lax.axis_index("pipe")
    feats = kept_qkv.shape[-1]
    keys = kept_qkv.shape[-2]
    heads = feats // HD

    owner = (section_index + section_count - half_way) % section_count
    owner_offset = lax.dynamic_index_in_dim(offsets[0], owner, 0, keepdims=False)[1]
    rows = sent_grad.shape[3] * lax.axis_size("tensor")
    held = held_qkv[0, 0]
    held_q = lax.dynamic_slice_in_dim(held[0], owner_offset, rows, 0)
    chunks = chunk_count(heads)
    width = feats // chunks
    fetched = []
    for c in range(chunks):
        cols = slice(c * width, (c + 1) * width)
        part = jnp.concatenate([held_q[:, cols], held[1, :, cols], held[2, :, cols]], axis=0)
        fetched.append(from_behind(part, "pipe", half_way))

    arrived = from_behind(sent_grad[0, 0], "pipe", -1)
    tensor_count = lax.axis_size("tensor")
    local_rows = arrived.shape[1]
    split = arrived.reshape(2, local_rows, tensor_count, feats).transpose(2, 0, 1, 3)
    regrouped = lax.all_to_all(split, "tensor", split_axis=0, concat_axis=0, tiled=True)
    regrouped = regrouped.transpose(1, 0, 2, 3).reshape(2, rows, feats)
    pick = order[0, 0]
    section_offsets = lax.dynamic_index_in_dim(offsets[0], section_index, 0, keepdims=False)
    qg, kv, column_sums = kept_backward(kept_qkv[0, 0], regrouped, section_offsets[0], pick)
    for c in range(chunks):
        qg, kv, column_sums = held_backward(
            fetched[c], regrouped, section_offsets[1], pick, c, qg, kv, column_sums
        )
    query_grad = qg
    key_value_grad = kv
    if lax.axis_size("dp") == 2:
        bias_grad = column_sums + from_behind(column_sums, "dp", 1)
    else:
        bias_grad = lax.psum(column_sums, "dp")
    return (query_grad[None, None], key_value_grad[None, None], bias_grad[None])


def solution(mesh):
    return jax.shard_map(
        body,
        mesh=mesh,
        in_specs=(
            P("dp", "pipe", None, None, "tensor"),
            P("dp", "pipe", None, None, "tensor"),
            P("dp", "pipe", None, "tensor", None),
            P("dp", "pipe"),
            P("dp", None, None),
        ),
        out_specs=(
            P("dp", "pipe", None, None, "tensor"),
            P("dp", "pipe", None, None, None, "tensor"),
            P("pipe", None, "tensor"),
        ),
        check_vma=False,
    )
```

time: 106 us -> 101 us (0.953)
  waiting for transfers between devices: 40.7 us -> 37.2 us
    ppermute x6, waiting for transfers between devices: 40.6 us -> 32.8 us  [from_behind(): return lax.ppermute(value, axis, pairs)]
    all_to_all x1, waiting for transfers between devices: 0.14 us -> 4.39 us  [body(): lax.all_to_all(split, 'tensor', split_axis=0, concat_axis=0, tiled=True)]
    broadcast_in_dim x3 -> x1, other arithmetic: 2.4 us -> 0.75 us  [body(): return (query_grad[None, None], key_value_grad[None, None], bias_grad[None])]
    another operation x4 -> x2, other arithmetic: 1.67 us -> 2.43 us  [the longest x1 1.28 us: kept_backward(): meta = jnp.stack([offset, pick]).astype(jnp.int32)]
    unnamed x43 -> x11, local copies, waits for them, and re-layouts: 3.76 us -> 3.53 us
  transfers between devices with their start and end apart: 7 -> 7, of which waited for: 5 -> 3; matrix products, arithmetic and copies ran while one was open for 9% -> 8% of each run, Pallas kernels for 25% -> 26%
where the time goes in v2:
time: 101 us; the launch traced here: 100 us
  waiting for transfers between devices  37.2 us (37%)
  Pallas kernels  30.7 us (30%)
  starting transfers between devices  16.1 us (16%)
  local copies, waits for them, and re-layouts  8.63 us (9%)
  other arithmetic  4.05 us (4%)
  between operations  3.34 us (3%)
    ppermute x6, waiting for transfers between devices, from_behind(): return lax.ppermute(value, axis, pairs)  32.8 us
    pallas_call x4, Pallas kernels, held_backward(): pl.pallas_call(held_kernel, out_shape=(jax.ShapeDtypeStruct(qg.shape, qg....  18.5 us
    ppermute x6, starting transfers between devices, from_behind(): return lax.ppermute(value, axis, pairs)  12.7 us
    pallas_call x1, Pallas kernels, kept_backward(): pl.pallas_call(kept_kernel, out_shape=out_shape, grid_spec=grid_spec, cos...  12.2 us
    all_to_all x1, waiting for transfers between devices, body(): lax.all_to_all(split, 'tensor', split_axis=0, concat_axis=0, tiled=True)  4.39 us
    unnamed x11, local copies, waits for them, and re-layouts  3.53 us
    all_to_all x1, starting transfers between devices, body(): lax.all_to_all(split, 'tensor', split_axis=0, concat_axis=0, tiled=True)  3.46 us
  transfers between devices with their start and end apart: 7, of which 3 were waited for; matrix products, arithmetic and copies ran while one was open for 8% of the time, Pallas kernels for 26%

profile of v2, /device:TPU:0, one launch (start us, length us, event | category | flops | bytes accessed | tf_op | source)
XLA Modules:
  0.0 100.0 jit_solution(16265399518478006109)
XLA Ops:
  0.6 0.0 copy-start
  0.6 5.1 %collective-permute-start.1 = (bf16[2,16,6144]{2,1,0:T(8,128)(2,1)}, bf16[2,16,6144]{2,1,0:T(8,128)(2,1)S(1)}, u32[]{:S(2)}, u32[]{:S(2)}) collective-permute-start(bf16[2,16,6144]{2,1,0:T(8,128)(2,1)} %bitcast.45), channel_id=1, source_target_pairs={{0,12},{4,0},{8,4},{12,8},{1,13},{5,1},{9,5},{13,9},{2,14},{6,2},{... | collective-permute-start | bytes 1179656 | tf_op jit(solution)/shard_map/ppermute | solution.py:19
  5.7 0.8 constant_dynamic-slice_fusion
  6.6 0.5 slice.62
  8.4 1.1 %slice.61 = bf16[1,1,1,192,1536]{4,3,2,1,0:T(8,128)(2,1)S(1)} slice(bf16[1,1,3,192,1536]{4,3,2,1,0:T(8,128)(2,1)} %param.6), slice={[0:1], [0:1], [0:1], [0:192], [0:1536]} | slice | bytes 1179648 | tf_op jit(solution)/shard_map/slice | solution.py:201
  10.1 0.1 dynamic-slice_bitcast_fusion
  10.2 0.0 copy-done
  10.2 0.1 slice_bitcast_fusion.1
  10.4 0.1 collective-permute-start
  10.6 3.0 %collective-permute-start.2 = (bf16[448,384]{1,0:T(8,128)(2,1)S(1)}, bf16[448,384]{1,0:T(8,128)(2,1)S(1)}, u32[]{:S(2)}, u32[]{:S(2)}) collective-permute-start(bf16[448,384]{1,0:T(8,128)(2,1)S(1)} %pad_maximum_fusion.1), channel_id=1, source_target_pairs={{0,8},{4,12},{8,0},{12,4},{1,9},{5,13},{9,1},{13,5},{2,10},{6,14},... | collective-permute-start | bytes 1032200 | tf_op jit(solution)/shard_map/ppermute | solution.py:19
  13.6 0.1 collective-permute-start.3
  13.7 0.8 pad_maximum_fusion.3
  14.4 2.9 %collective-permute-start.4 = (bf16[448,384]{1,0:T(8,128)(2,1)}, bf16[448,384]{1,0:T(8,128)(2,1)S(1)}, u32[]{:S(2)}, u32[]{:S(2)}) collective-permute-start(bf16[448,384]{1,0:T(8,128)(2,1)} %pad_maximum_fusion.3), channel_id=1, source_target_pairs={{0,8},{4,12},{8,0},{12,4},{1,9},{5,13},{9,1},{13,5},{2,10},{6,14},... | collective-permute-start | bytes 1032200 | tf_op jit(solution)/shard_map/ppermute | solution.py:19
  18.0 0.0 collective-permute-done.1
  18.0 0.3 reshape.26
  18.3 0.8 copy.24
  19.1 3.5 %all-to-all-start = ((bf16[4,2,16,1536]{3,2,1,0:T(8,128)(2,1)}), bf16[4,2,16,1536]{3,2,1,0:T(8,128)(2,1)S(1)}, u32[]{:S(2)}, u32[]{:S(2)}) async-start(bf16[4,2,16,1536]{3,2,1,0:T(8,128)(2,1)} %copy.24), calls=%async_computation | async-start | bytes 786432 | tf_op jit(solution)/shard_map/all_to_all | solution.py:214
  22.5 0.6 fusion.1
  23.1 1.3 %pad_add_fusion.1.meta_ref = s32[2]{0:T(128)} fusion(s32[1]{0:T(128)} %bitcast.33, s32[1]{0:T(128)} %bitcast.17), kind=kLoop, calls=%fused_computation.17 | loop fusion | flops 2 | bytes 16 | tf_op jit(solution)/shard_map/stack | solution.py:137
  24.4 1.2 %pad_add_fusion.meta_ref = s32[2]{0:T(128)} fusion(s32[1]{0:T(128)} %bitcast.1, s32[1]{0:T(128)} %bitcast), kind=kLoop, calls=%fused_computation.16 | loop fusion | flops 2 | bytes 16 | tf_op jit(solution)/shard_map/stack | solution.py:167
  25.6 4.4 %all-to-all-done = bf16[4,2,16,1536]{3,2,1,0:T(8,128)(2,1)S(1)} async-done(((bf16[4,2,16,1536]{3,2,1,0:T(8,128)(2,1)}), bf16[4,2,16,1536]{3,2,1,0:T(8,128)(2,1)S(1)}, u32[]{:S(2)}, u32[]{:S(2)}) %all-to-all-start) | async-done | bytes 393248 | tf_op jit(solution)/shard_map/all_to_all | solution.py:214
  30.0 0.8 copy.25
  30.7 12.2 %kept_backward.1 = (bf16[2,64,1536]{2,1,0:T(8,128)(2,1)}, bf16[2,2,192,1536]{3,2,1,0:T(8,128)(2,1)}, f32[3,1536]{1,0:T(4,128)}) custom-call(s32[2]{0:T(128)} %pad_add_fusion.1.meta_ref, bf16[3,192,1536]{2,1,0:T(8,128)(2,1)} %bitcast.42, bf16[2,64,1536]{2,1,0:T(8,128)(2,1)} %bitcast.35), custom_call_target="tpu_custom_call" | custom-call | flops 226492416 | bytes 2949120 | tf_op jit(solution)/shard_map/kept_backward/pallas_call | solution.py:138
  42.9 30.3 %collective-permute-done.4.x_ref = bf16[448,384]{1,0:T(8,128)(2,1)S(1)} collective-permute-done((bf16[448,384]{1,0:T(8,128)(2,1)}, bf16[448,384]{1,0:T(8,128)(2,1)S(1)}, u32[]{:S(2)}, u32[]{:S(2)}) %collective-permute-start.4) | collective-permute-done | bytes 344096 | tf_op jit(solution)/shard_map/ppermute | solution.py:19
  73.2 0.0 copy-start.4
  73.2 0.7 copy-done.4
  73.9 4.6 %held_backward.4 = (bf16[2,64,1536]{2,1,0:T(8,128)(2,1)}, bf16[2,2,192,1536]{3,2,1,0:T(8,128)(2,1)}, f32[3,1536]{1,0:T(4,128)}) custom-call(s32[2]{0:T(128)} %pad_add_fusion.meta_ref, bf16[448,384]{1,0:T(8,128)(2,1)} %copy-done.4, bf16[2,64,1536]{2,1,0:T(8,128)(2,1)} %bitcast.36, ...), custom_call_target="tpu_custom_call", output_to_operand_aliasing={{0}: (3, {}), {1}: (4, {}), {2}: (5, {})} | custom-call | flops 56623104 | bytes 737280 | tf_op jit(solution)/shard_map/held_backward/pallas_call | solution.py:168
  78.5 0.0 collective-permute-done.3.x_ref
  78.6 0.0 copy-start.3
  78.6 0.7 copy-done.3
  79.3 4.6 %held_backward.5 = (bf16[2,64,1536]{2,1,0:T(8,128)(2,1)}, bf16[2,2,192,1536]{3,2,1,0:T(8,128)(2,1)}, f32[3,1536]{1,0:T(4,128)}) custom-call(s32[2]{0:T(128)} %pad_add_fusion.meta_ref, bf16[448,384]{1,0:T(8,128)(2,1)} %copy-done.3, bf16[2,64,1536]{2,1,0:T(8,128)(2,1)} %bitcast.37, ...), custom_call_target="tpu_custom_call", output_to_operand_aliasing={{0}: (3, {}), {1}: (4, {}), {2}: (5, {})} | custom-call | flops 56623104 | bytes 737280 | tf_op jit(solution)/shard_map/held_backward/pallas_call | solution.py:168
  83.9 0.0 collective-permute-done.2.x_ref
  83.9 0.0 copy-start.2
  83.9 0.7 copy-done.2
  84.6 4.6 %held_backward.6 = (bf16[2,64,1536]{2,1,0:T(8,128)(2,1)}, bf16[2,2,192,1536]{3,2,1,0:T(8,128)(2,1)}, f32[3,1536]{1,0:T(4,128)}) custom-call(s32[2]{0:T(128)} %pad_add_fusion.meta_ref, bf16[448,384]{1,0:T(8,128)(2,1)} %copy-done.2, bf16[2,64,1536]{2,1,0:T(8,128)(2,1)} %bitcast.38, ...), custom_call_target="tpu_custom_call", output_to_operand_aliasing={{0}: (3, {}), {1}: (4, {}), {2}: (5, {})} | custom-call | flops 56623104 | bytes 737280 | tf_op jit(solution)/shard_map/held_backward/pallas_call | solution.py:168
  89.2 0.0 collective-permute-done.x_ref
  89.2 0.0 copy-start.1
  89.2 0.7 copy-done.1
  90.0 4.6 %held_backward.7 = (bf16[2,64,1536]{2,1,0:T(8,128)(2,1)}, bf16[2,2,192,1536]{3,2,1,0:T(8,128)(2,1)}, f32[3,1536]{1,0:T(4,128)}) custom-call(s32[2]{0:T(128)} %pad_add_fusion.meta_ref, bf16[448,384]{1,0:T(8,128)(2,1)} %copy-done.1, bf16[2,64,1536]{2,1,0:T(8,128)(2,1)} %bitcast.39, ...), custom_call_target="tpu_custom_call", output_to_operand_aliasing={{0}: (3, {}), {1}: (4, {}), {2}: (5, {})} | custom-call | flops 56623104 | bytes 737280 | tf_op jit(solution)/shard_map/held_backward/pallas_call | solution.py:168
  94.6 1.5 %collective-permute-start.5 = (f32[3,1536]{1,0:T(4,128)}, f32[3,1536]{1,0:T(4,128)S(1)}, u32[]{:S(2)}, u32[]{:S(2)}) collective-permute-start(f32[3,1536]{1,0:T(4,128)} %get-tuple-element.32), channel_id=1, source_target_pairs={{0,16},{16,0},{1,17},{17,1},{2,18},{18,2},{3,19},{19,3},{4,20},{20... | collective-permute-start | bytes 55304 | tf_op jit(solution)/shard_map/ppermute | solution.py:19
  96.1 2.5 %collective-permute-done.5 = f32[3,1536]{1,0:T(4,128)S(1)} collective-permute-done((f32[3,1536]{1,0:T(4,128)}, f32[3,1536]{1,0:T(4,128)S(1)}, u32[]{:S(2)}, u32[]{:S(2)}) %collective-permute-start.5) | collective-permute-done | bytes 18464 | tf_op jit(solution)/shard_map/ppermute | solution.py:19
  98.6 0.7 add_bitcast_fusion
  99.4 0.6 copy.26
  (4 shorter events, 0.1 us)
Async XLA Ops:
  0.6 9.6 %copy-start = (bf16[1,1,3,192,1536]{4,3,2,1,0:T(8,128)(2,1)S(1)}, bf16[1,1,3,192,1536]{4,3,2,1,0:T(8,128)(2,1)}, u32[]{:S(2)}) copy-start(bf16[1,1,3,192,1536]{4,3,2,1,0:T(8,128)(2,1)} %param.6) | copy-start | bytes 5308420
  0.6 17.3 %collective-permute-start.1 = (bf16[2,16,6144]{2,1,0:T(8,128)(2,1)}, bf16[2,16,6144]{2,1,0:T(8,128)(2,1)S(1)}, u32[]{:S(2)}, u32[]{:S(2)}) collective-permute-start(bf16[2,16,6144]{2,1,0:T(8,128)(2,1)} %bitcast.45), channel_id=1, source_target_pairs={{0,12},{4,0},{8,4},{12,8},{1,13},{5,1},{9,5},{13,9},{2,14},{6,2},{... | collective-permute-start | bytes 1179656 | tf_op jit(solution)/shard_map/ppermute | solution.py:19
  10.4 78.8 %collective-permute-start = (bf16[448,384]{1,0:T(8,128)(2,1)S(1)}, bf16[448,384]{1,0:T(8,128)(2,1)S(1)}, u32[]{:S(2)}, u32[]{:S(2)}) collective-permute-start(bf16[448,384]{1,0:T(8,128)(2,1)S(1)} %pad_maximum_fusion), channel_id=1, source_target_pairs={{0,8},{4,12},{8,0},{12,4},{1,9},{5,13},{9,1},{13,5},{2,10},{6,14},... | collective-permute-start | bytes 1032200 | tf_op jit(solution)/shard_map/ppermute | solution.py:19
  10.6 73.3 %collective-permute-start.2 = (bf16[448,384]{1,0:T(8,128)(2,1)S(1)}, bf16[448,384]{1,0:T(8,128)(2,1)S(1)}, u32[]{:S(2)}, u32[]{:S(2)}) collective-permute-start(bf16[448,384]{1,0:T(8,128)(2,1)S(1)} %pad_maximum_fusion.1), channel_id=1, source_target_pairs={{0,8},{4,12},{8,0},{12,4},{1,9},{5,13},{9,1},{13,5},{2,10},{6,14},... | collective-permute-start | bytes 1032200 | tf_op jit(solution)/shard_map/ppermute | solution.py:19
  13.6 65.0 %collective-permute-start.3 = (bf16[448,384]{1,0:T(8,128)(2,1)S(1)}, bf16[448,384]{1,0:T(8,128)(2,1)S(1)}, u32[]{:S(2)}, u32[]{:S(2)}) collective-permute-start(bf16[448,384]{1,0:T(8,128)(2,1)S(1)} %pad_maximum_fusion.2), channel_id=1, source_target_pairs={{0,8},{4,12},{8,0},{12,4},{1,9},{5,13},{9,1},{13,5},{2,10},{6,14},... | collective-permute-start | bytes 1032200 | tf_op jit(solution)/shard_map/ppermute | solution.py:19
  14.4 58.8 %collective-permute-start.4 = (bf16[448,384]{1,0:T(8,128)(2,1)}, bf16[448,384]{1,0:T(8,128)(2,1)S(1)}, u32[]{:S(2)}, u32[]{:S(2)}) collective-permute-start(bf16[448,384]{1,0:T(8,128)(2,1)} %pad_maximum_fusion.3), channel_id=1, source_target_pairs={{0,8},{4,12},{8,0},{12,4},{1,9},{5,13},{9,1},{13,5},{2,10},{6,14},... | collective-permute-start | bytes 1032200 | tf_op jit(solution)/shard_map/ppermute | solution.py:19
  19.1 10.9 %all-to-all-start = ((bf16[4,2,16,1536]{3,2,1,0:T(8,128)(2,1)}), bf16[4,2,16,1536]{3,2,1,0:T(8,128)(2,1)S(1)}, u32[]{:S(2)}, u32[]{:S(2)}) async-start(bf16[4,2,16,1536]{3,2,1,0:T(8,128)(2,1)} %copy.24), calls=%async_computation | async-start | bytes 786432 | tf_op jit(solution)/shard_map/all_to_all | solution.py:214
  73.2 0.7 copy-start.4
  78.6 0.7 copy-start.3
  83.9 0.7 copy-start.2
  89.2 0.7 copy-start.1
  94.6 4.0 %collective-permute-start.5 = (f32[3,1536]{1,0:T(4,128)}, f32[3,1536]{1,0:T(4,128)S(1)}, u32[]{:S(2)}, u32[]{:S(2)}) collective-permute-start(f32[3,1536]{1,0:T(4,128)} %get-tuple-element.32), channel_id=1, source_target_pairs={{0,16},{16,0},{1,17},{17,1},{2,18},{18,2},{3,19},{19,3},{4,20},{20... | collective-permute-start | bytes 55304 | tf_op jit(solution)/shard_map/ppermute | solution.py:19

commit v3 on v2

--- a/solution.py
+++ b/solution.py
@@ -9,7 +9,6 @@
 
 HD = 128
 MASK_FILL = -1e30
-MAX_CHUNKS = 4
 NT_DIMS = (((1,), (1,)), ((), ()))
 
 
@@ -50,7 +49,7 @@
         store(cols, *head_backward(q, k, v, g, visible))
         return carry
 
-    lax.fori_loop(0, heads, head, 0)
+    lax.fori_loop(0, heads, head, 0, unroll=True)
 
 
 class Loader:
@@ -144,10 +143,12 @@
     )(meta, stash, grads)
 
 
-def held_backward(part, grads, offset, pick, chunk, qg, kv, sums):
+def held_backward(part, grads, offset, pick, lo, qg, kv, sums):
     rows = grads.shape[1]
     width = part.shape[1]
     keys = (part.shape[0] - rows) // 2
+    assert lo % width == 0
+    chunk = lo // width
     grid_spec = pltpu.PrefetchScalarGridSpec(
         num_scalar_prefetch=1,
         grid=(1,),
@@ -179,13 +180,6 @@
     )(meta, part, grads, qg, kv, sums)
 
 
-def chunk_count(heads):
-    for count in range(min(MAX_CHUNKS, heads), 0, -1):
-        if heads % count == 0:
-            return count
-    return 1
-
-
 def body(kept_qkv, held_qkv, sent_grad, order, offsets):
     section_count = lax.axis_size("pipe")
     half_way = section_count // 2
@@ -199,12 +193,13 @@
     rows = sent_grad.shape[3] * lax.axis_size("tensor")
     held = held_qkv[0, 0]
     held_q = lax.dynamic_slice_in_dim(held[0], owner_offset, rows, 0)
-    chunks = chunk_count(heads)
-    width = feats // chunks
+    first = heads - heads // 3
+    bounds = [(0, first * HD), (first * HD, feats)]
     fetched = []
-    for c in range(chunks):
-        cols = slice(c * width, (c + 1) * width)
-        part = jnp.concatenate([held_q[:, cols], held[1, :, cols], held[2, :, cols]], axis=0)
+    for lo, hi in bounds:
+        part = jnp.concatenate([held_q[:, lo:hi], held[1, :, lo:hi], held[2, :, lo:hi]], axis=0)
+        if fetched:
+            fetched[-1], part = lax.optimization_barrier((fetched[-1], part))
         fetched.append(from_behind(part, "pipe", half_way))
 
     arrived = from_behind(sent_grad[0, 0], "pipe", -1)
@@ -216,9 +211,9 @@
     pick = order[0, 0]
     section_offsets = lax.dynamic_index_in_dim(offsets[0], section_index, 0, keepdims=False)
     qg, kv, column_sums = kept_backward(kept_qkv[0, 0], regrouped, section_offsets[0], pick)
-    for c in range(chunks):
+    for (lo, hi), part in zip(bounds, fetched):
         qg, kv, column_sums = held_backward(
-            fetched[c], regrouped, section_offsets[1], pick, c, qg, kv, column_sums
+            part, regrouped, section_offsets[1], pick, lo, qg, kv, column_sums
         )
     query_grad = qg
     key_value_grad = kv

time: 101 us -> 113 us (1.12)
  the two profiles are of different devices: /device:TPU:0 before, /device:TPU:12 now
where the time goes in v3:
time: 113 us; the launch traced here: 112 us
  waiting for transfers between devices  64.8 us (57%)
  Pallas kernels  23.9 us (21%)
  starting transfers between devices  10.4 us (9%)
  local copies, waits for them, and re-layouts  6.55 us (6%)
  between operations  3.35 us (3%)
  other arithmetic  3.29 us (3%)
    ppermute x4, waiting for transfers between devices, from_behind(): return lax.ppermute(value, axis, pairs)  60.4 us
    pallas_call x2, Pallas kernels, held_backward(): pl.pallas_call(held_kernel, out_shape=(jax.ShapeDtypeStruct(qg.shape, qg....  13 us
    pallas_call x1, Pallas kernels, kept_backward(): pl.pallas_call(kept_kernel, out_shape=out_shape, grid_spec=grid_spec, cos...  10.9 us
    ppermute x4, starting transfers between devices, from_behind(): return lax.ppermute(value, axis, pairs)  6.99 us
    all_to_all x1, waiting for transfers between devices, body(): lax.all_to_all(split, 'tensor', split_axis=0, concat_axis=0, tiled=True)  4.41 us
    all_to_all x1, starting transfers between devices, body(): lax.all_to_all(split, 'tensor', split_axis=0, concat_axis=0, tiled=True)  3.46 us
  transfers between devices with their start and end apart: 5, of which 3 were waited for; matrix products, arithmetic and copies ran while one was open for 4% of the time, Pallas kernels for 17%

profile of v3, /device:TPU:12, one launch (start us, length us, event | category | flops | bytes accessed | tf_op | source)
XLA Modules:
  0.0 112.4 jit_solution(12251484346601537601)
XLA Ops:
  0.6 0.0 copy-start
  0.7 0.9 constant_dynamic-slice_fusion
  1.6 0.5 slice.42
  3.4 1.1 slice.41
  5.1 0.1 dynamic-slice_bitcast_fusion
  5.2 0.0 copy-start.3
  5.2 0.0 copy-done
  5.2 0.1 slice_bitcast_fusion.1
  5.3 0.1 pad_maximum_fusion
  5.4 2.7 %collective-permute-start = (bf16[448,1024]{1,0:T(8,128)(2,1)S(1)}, bf16[448,1024]{1,0:T(8,128)(2,1)S(1)}, u32[]{:S(2)}, u32[]{:S(2)}) collective-permute-start(bf16[448,1024]{1,0:T(8,128)(2,1)S(1)} %pad_maximum_fusion), channel_id=1, source_target_pairs={{0,8},{4,12},{8,0},{12,4},{1,9},{5,13},{9,1},{13,5},{2,10},{6,14},... | collective-permute-start | bytes 2752520 | tf_op jit(solution)/shard_map/ppermute | solution.py:18
  8.0 0.0 copy-done.3
  8.0 0.4 collective-permute-start.2
  8.6 56.9 %collective-permute-done.x_ref = bf16[448,1024]{1,0:T(8,128)(2,1)S(1)} collective-permute-done((bf16[448,1024]{1,0:T(8,128)(2,1)S(1)}, bf16[448,1024]{1,0:T(8,128)(2,1)S(1)}, u32[]{:S(2)}, u32[]{:S(2)}) %collective-permute-start) | collective-permute-done | bytes 917536 | tf_op jit(solution)/shard_map/ppermute | solution.py:18
  65.5 0.0 copy-start.1
  65.5 3.4 %collective-permute-start.1 = (bf16[448,512]{1,0:T(8,128)(2,1)S(1)}, bf16[448,512]{1,0:T(8,128)(2,1)S(1)}, u32[]{:S(2)}, u32[]{:S(2)}) collective-permute-start(bf16[448,512]{1,0:T(8,128)(2,1)S(1)} %pad_maximum_fusion.1), channel_id=1, source_target_pairs={{0,8},{4,12},{8,0},{12,4},{1,9},{5,13},{9,1},{13,5},{2,10},{6,14},... | collective-permute-start | bytes 1376264 | tf_op jit(solution)/shard_map/ppermute | solution.py:18
  69.5 0.0 collective-permute-done.2
  69.5 0.3 reshape.26
  69.8 0.8 copy.18
  70.6 3.5 %all-to-all-start = ((bf16[4,2,16,1536]{3,2,1,0:T(8,128)(2,1)}), bf16[4,2,16,1536]{3,2,1,0:T(8,128)(2,1)S(1)}, u32[]{:S(2)}, u32[]{:S(2)}) async-start(bf16[4,2,16,1536]{3,2,1,0:T(8,128)(2,1)} %copy.18), calls=%async_computation | async-start | bytes 786432 | tf_op jit(solution)/shard_map/all_to_all | solution.py:209
  74.1 0.5 fusion
  74.6 1.3 %pad_add_fusion.1.meta_ref = s32[2]{0:T(128)} fusion(s32[1]{0:T(128)} %bitcast.25, s32[1]{0:T(128)} %bitcast.13), kind=kLoop, calls=%fused_computation.11 | loop fusion | flops 2 | bytes 16 | tf_op jit(solution)/shard_map/stack | solution.py:136
  75.9 1.2 %pad_add_fusion.meta_ref = s32[2]{0:T(128)} fusion(s32[1]{0:T(128)} %bitcast.1, s32[1]{0:T(128)} %bitcast), kind=kLoop, calls=%fused_computation.10 | loop fusion | flops 2 | bytes 16 | tf_op jit(solution)/shard_map/stack | solution.py:168
  77.1 4.4 %all-to-all-done = bf16[4,2,16,1536]{3,2,1,0:T(8,128)(2,1)S(1)} async-done(((bf16[4,2,16,1536]{3,2,1,0:T(8,128)(2,1)}), bf16[4,2,16,1536]{3,2,1,0:T(8,128)(2,1)S(1)}, u32[]{:S(2)}, u32[]{:S(2)}) %all-to-all-start) | async-done | bytes 393248 | tf_op jit(solution)/shard_map/all_to_all | solution.py:209
  81.5 0.8 copy.19
  82.3 10.9 %kept_backward.1 = (bf16[2,64,1536]{2,1,0:T(8,128)(2,1)}, bf16[2,2,192,1536]{3,2,1,0:T(8,128)(2,1)}, f32[3,1536]{1,0:T(4,128)}) custom-call(s32[2]{0:T(128)} %pad_add_fusion.1.meta_ref, bf16[3,192,1536]{2,1,0:T(8,128)(2,1)} %bitcast.32, bf16[2,64,1536]{2,1,0:T(8,128)(2,1)} %bitcast.27), custom_call_target="tpu_custom_call" | custom-call | flops 226492416 | bytes 2949120 | tf_op jit(solution)/shard_map/kept_backward/pallas_call | solution.py:137
  93.2 0.0 copy-done.1
  93.2 7.9 %held_backward.2 = (bf16[2,64,1536]{2,1,0:T(8,128)(2,1)}, bf16[2,2,192,1536]{3,2,1,0:T(8,128)(2,1)}, f32[3,1536]{1,0:T(4,128)}) custom-call(s32[2]{0:T(128)} %pad_add_fusion.meta_ref, bf16[448,1024]{1,0:T(8,128)(2,1)} %copy-done.1, bf16[2,64,1536]{2,1,0:T(8,128)(2,1)} %bitcast.28, ...), custom_call_target="tpu_custom_call", output_to_operand_aliasing={{0}: (3, {}), {1}: (4, {}), {2}: (5, {})} | custom-call | flops 150994944 | bytes 1966080 | tf_op jit(solution)/shard_map/held_backward/pallas_call | solution.py:169
  101.1 0.0 collective-permute-done.1.x_ref
  101.1 0.0 copy-start.2
  101.1 0.8 copy-done.2
  101.9 5.1 %held_backward.3 = (bf16[2,64,1536]{2,1,0:T(8,128)(2,1)}, bf16[2,2,192,1536]{3,2,1,0:T(8,128)(2,1)}, f32[3,1536]{1,0:T(4,128)}) custom-call(s32[2]{0:T(128)} %pad_add_fusion.meta_ref, bf16[448,512]{1,0:T(8,128)(2,1)} %copy-done.2, bf16[2,64,1536]{2,1,0:T(8,128)(2,1)} %bitcast.29, ...), custom_call_target="tpu_custom_call", output_to_operand_aliasing={{0}: (3, {}), {1}: (4, {}), {2}: (5, {})} | custom-call | flops 75497472 | bytes 983040 | tf_op jit(solution)/shard_map/held_backward/pallas_call | solution.py:169
  106.9 0.5 collective-permute-start.3
  107.5 3.5 %collective-permute-done.3 = f32[3,1536]{1,0:T(4,128)S(1)} collective-permute-done((f32[3,1536]{1,0:T(4,128)}, f32[3,1536]{1,0:T(4,128)S(1)}, u32[]{:S(2)}, u32[]{:S(2)}) %collective-permute-start.3) | collective-permute-done | bytes 18464 | tf_op jit(solution)/shard_map/ppermute | solution.py:18
  111.0 0.7 add_bitcast_fusion
  111.7 0.6 copy.20
  (4 shorter events, 0.1 us)
Async XLA Ops:
  0.6 4.6 %copy-start = (bf16[1,1,3,192,1536]{4,3,2,1,0:T(8,128)(2,1)S(1)}, bf16[1,1,3,192,1536]{4,3,2,1,0:T(8,128)(2,1)}, u32[]{:S(2)}) copy-start(bf16[1,1,3,192,1536]{4,3,2,1,0:T(8,128)(2,1)} %param.6) | copy-start | bytes 5308420
  5.2 2.9 %copy-start.3 = (bf16[1,1,2,16,6144]{4,3,2,1,0:T(8,128)(2,1)S(1)}, bf16[1,1,2,16,6144]{4,3,2,1,0:T(8,128)(2,1)}, u32[]{:S(2)}) copy-start(bf16[1,1,2,16,6144]{4,3,2,1,0:T(8,128)(2,1)} %param.7) | copy-start | bytes 1179652
  5.4 60.1 %collective-permute-start = (bf16[448,1024]{1,0:T(8,128)(2,1)S(1)}, bf16[448,1024]{1,0:T(8,128)(2,1)S(1)}, u32[]{:S(2)}, u32[]{:S(2)}) collective-permute-start(bf16[448,1024]{1,0:T(8,128)(2,1)S(1)} %pad_maximum_fusion), channel_id=1, source_target_pairs={{0,8},{4,12},{8,0},{12,4},{1,9},{5,13},{9,1},{13,5},{2,10},{6,14},... | collective-permute-start | bytes 2752520 | tf_op jit(solution)/shard_map/ppermute | solution.py:18
  8.0 61.4 %collective-permute-start.2 = (bf16[2,16,6144]{2,1,0:T(8,128)(2,1)S(1)}, bf16[2,16,6144]{2,1,0:T(8,128)(2,1)S(1)}, u32[]{:S(2)}, u32[]{:S(2)}) collective-permute-start(bf16[2,16,6144]{2,1,0:T(8,128)(2,1)S(1)} %bitcast.36), channel_id=1, source_target_pairs={{0,12},{4,0},{8,4},{12,8},{1,13},{5,1},{9,5},{13,9},{2,14},{6,2},{... | collective-permute-start | bytes 1179656 | tf_op jit(solution)/shard_map/ppermute | solution.py:18
  65.5 27.7 %copy-start.1 = (bf16[448,1024]{1,0:T(8,128)(2,1)}, bf16[448,1024]{1,0:T(8,128)(2,1)S(1)}, u32[]{:S(2)}) copy-start(bf16[448,1024]{1,0:T(8,128)(2,1)S(1)} %collective-permute-done.x_ref) | copy-start | bytes 2752516
  65.5 35.6 %collective-permute-start.1 = (bf16[448,512]{1,0:T(8,128)(2,1)S(1)}, bf16[448,512]{1,0:T(8,128)(2,1)S(1)}, u32[]{:S(2)}, u32[]{:S(2)}) collective-permute-start(bf16[448,512]{1,0:T(8,128)(2,1)S(1)} %pad_maximum_fusion.1), channel_id=1, source_target_pairs={{0,8},{4,12},{8,0},{12,4},{1,9},{5,13},{9,1},{13,5},{2,10},{6,14},... | collective-permute-start | bytes 1376264 | tf_op jit(solution)/shard_map/ppermute | solution.py:18
  70.6 10.9 %all-to-all-start = ((bf16[4,2,16,1536]{3,2,1,0:T(8,128)(2,1)}), bf16[4,2,16,1536]{3,2,1,0:T(8,128)(2,1)S(1)}, u32[]{:S(2)}, u32[]{:S(2)}) async-start(bf16[4,2,16,1536]{3,2,1,0:T(8,128)(2,1)} %copy.18), calls=%async_computation | async-start | bytes 786432 | tf_op jit(solution)/shard_map/all_to_all | solution.py:209
  101.1 0.8 copy-start.2
  106.9 4.0 %collective-permute-start.3 = (f32[3,1536]{1,0:T(4,128)}, f32[3,1536]{1,0:T(4,128)S(1)}, u32[]{:S(2)}, u32[]{:S(2)}) collective-permute-start(f32[3,1536]{1,0:T(4,128)} %get-tuple-element.24), channel_id=1, source_target_pairs={{0,16},{16,0},{1,17},{17,1},{2,18},{18,2},{3,19},{19,3},{4,20},{20... | collective-permute-start | bytes 55304 | tf_op jit(solution)/shard_map/ppermute | solution.py:18

commit v4 on v3

--- a/solution.py
+++ b/solution.py
@@ -193,14 +193,13 @@
     rows = sent_grad.shape[3] * lax.axis_size("tensor")
     held = held_qkv[0, 0]
     held_q = lax.dynamic_slice_in_dim(held[0], owner_offset, rows, 0)
-    first = heads - heads // 3
+    first = heads - max(1, heads // 6)
     bounds = [(0, first * HD), (first * HD, feats)]
-    fetched = []
-    for lo, hi in bounds:
-        part = jnp.concatenate([held_q[:, lo:hi], held[1, :, lo:hi], held[2, :, lo:hi]], axis=0)
-        if fetched:
-            fetched[-1], part = lax.optimization_barrier((fetched[-1], part))
-        fetched.append(from_behind(part, "pipe", half_way))
+    parts = [
+        jnp.concatenate([held_q[:, lo:hi], held[1, :, lo:hi], held[2, :, lo:hi]], axis=0)
+        for lo, hi in bounds
+    ]
+    fetched_first = from_behind(parts[0], "pipe", half_way)
 
     arrived = from_behind(sent_grad[0, 0], "pipe", -1)
     tensor_count = lax.axis_size("tensor")
@@ -211,6 +210,10 @@
     pick = order[0, 0]
     section_offsets = lax.dynamic_index_in_dim(offsets[0], section_index, 0, keepdims=False)
     qg, kv, column_sums = kept_backward(kept_qkv[0, 0], regrouped, section_offsets[0], pick)
+    fetched_first, second, qg, kv, column_sums = lax.optimization_barrier(
+        (fetched_first, parts[1], qg, kv, column_sums)
+    )
+    fetched = [fetched_first, from_behind(second, "pipe", half_way)]
     for (lo, hi), part in zip(bounds, fetched):
         qg, kv, column_sums = held_backward(
             part, regrouped, section_offsets[1], pick, lo, qg, kv, column_sums

time: 113 us -> 114 us (level)
  the two profiles are of different devices: /device:TPU:12 before, /device:TPU:0 now
where the time goes in v4:
time: 114 us; the launch traced here: 113 us
  waiting for transfers between devices  39.2 us (34%)
  starting transfers between devices  35.2 us (31%)
  Pallas kernels  23.9 us (21%)
  local copies, waits for them, and re-layouts  7.45 us (7%)
  other arithmetic  4.3 us (4%)
  between operations  3.36 us (3%)
    ppermute x4, waiting for transfers between devices, from_behind(): return lax.ppermute(value, axis, pairs)  31.9 us
    ppermute x4, starting transfers between devices, from_behind(): return lax.ppermute(value, axis, pairs)  31.8 us
    pallas_call x2, Pallas kernels, held_backward(): pl.pallas_call(held_kernel, out_shape=(jax.ShapeDtypeStruct(qg.shape, qg....  13 us
    pallas_call x1, Pallas kernels, kept_backward(): pl.pallas_call(kept_kernel, out_shape=out_shape, grid_spec=grid_spec, cos...  10.9 us
    all_to_all x1, waiting for transfers between devices, body(): lax.all_to_all(split, 'tensor', split_axis=0, concat_axis=0, tiled=True)  7.35 us
    all_to_all x1, starting transfers between devices, body(): lax.all_to_all(split, 'tensor', split_axis=0, concat_axis=0, tiled=True)  3.46 us
  transfers between devices with their start and end apart: 5, of which 3 were waited for; matrix products, arithmetic and copies ran while one was open for 5% of the time, Pallas kernels for 18%

profile of v4, /device:TPU:0, one launch (start us, length us, event | category | flops | bytes accessed | tf_op | source)
XLA Modules:
  0.0 113.4 jit_solution(18153719333250426136)
XLA Ops:
  0.6 0.0 copy-start
  0.7 0.9 constant_dynamic-slice_fusion
  1.6 0.5 slice.42
  3.4 1.1 slice.41
  5.1 0.1 dynamic-slice_bitcast_fusion
  5.2 0.0 copy-start.2
  5.2 0.0 copy-done
  5.2 0.0 copy-start.4
  5.2 0.1 slice_bitcast_fusion.1
  5.3 1.1 pad_maximum_fusion
  6.4 4.0 %collective-permute-start = (bf16[448,1280]{1,0:T(8,128)(2,1)}, bf16[448,1280]{1,0:T(8,128)(2,1)S(1)}, u32[]{:S(2)}, u32[]{:S(2)}) collective-permute-start(bf16[448,1280]{1,0:T(8,128)(2,1)} %pad_maximum_fusion), channel_id=1, source_target_pairs={{0,8},{4,12},{8,0},{12,4},{1,9},{5,13},{9,1},{13,5},{2,10},{6,14},... | collective-permute-start | bytes 3440648 | tf_op jit(solution)/shard_map/ppermute | solution.py:18
  10.5 0.0 copy-done.4
  10.5 1.3 %collective-permute-start.1 = (bf16[2,16,6144]{2,1,0:T(8,128)(2,1)S(1)}, bf16[2,16,6144]{2,1,0:T(8,128)(2,1)}, u32[]{:S(2)}, u32[]{:S(2)}) collective-permute-start(bf16[2,16,6144]{2,1,0:T(8,128)(2,1)S(1)} %bitcast.36), channel_id=1, source_target_pairs={{0,12},{4,0},{8,4},{12,8},{1,13},{5,1},{9,5},{13,9},{2,14},{6,2},{... | collective-permute-start | bytes 1179656 | tf_op jit(solution)/shard_map/ppermute | solution.py:18
  11.8 0.0 copy-done.2
  11.8 0.0 slice-start
  12.5 0.6 fusion
  13.1 1.2 %pad_add_fusion.1.meta_ref = s32[2]{0:T(128)} fusion(s32[1]{0:T(128)} %bitcast.25, s32[1]{0:T(128)} %bitcast.9), kind=kLoop, calls=%fused_computation.11 | loop fusion | flops 2 | bytes 16 | tf_op jit(solution)/shard_map/stack | solution.py:136
  14.3 29.4 %collective-permute-done.1 = bf16[2,16,6144]{2,1,0:T(8,128)(2,1)} collective-permute-done((bf16[2,16,6144]{2,1,0:T(8,128)(2,1)S(1)}, bf16[2,16,6144]{2,1,0:T(8,128)(2,1)}, u32[]{:S(2)}, u32[]{:S(2)}) %collective-permute-start.1) | collective-permute-done | bytes 393248 | tf_op jit(solution)/shard_map/ppermute | solution.py:18
  43.7 1.3 %reshape.26 = bf16[2,16,4,1536]{3,2,1,0:T(4,128)(2,1)S(1)} reshape(bf16[2,16,6144]{2,1,0:T(8,128)(2,1)} %collective-permute-done.1) | data formatting | bytes 786432 | tf_op jit(solution)/shard_map/reshape | solution.py:207
  45.0 0.8 copy.18
  45.8 3.5 %all-to-all-start = ((bf16[4,2,16,1536]{3,2,1,0:T(8,128)(2,1)}), bf16[4,2,16,1536]{3,2,1,0:T(8,128)(2,1)S(1)}, u32[]{:S(2)}, u32[]{:S(2)}) async-start(bf16[4,2,16,1536]{3,2,1,0:T(8,128)(2,1)} %copy.18), calls=%async_computation | async-start | bytes 786432 | tf_op jit(solution)/shard_map/all_to_all | solution.py:208
  49.3 0.0 slice-done
  49.3 7.3 %all-to-all-done = bf16[4,2,16,1536]{3,2,1,0:T(8,128)(2,1)S(1)} async-done(((bf16[4,2,16,1536]{3,2,1,0:T(8,128)(2,1)}), bf16[4,2,16,1536]{3,2,1,0:T(8,128)(2,1)S(1)}, u32[]{:S(2)}, u32[]{:S(2)}) %all-to-all-start) | async-done | bytes 393248 | tf_op jit(solution)/shard_map/all_to_all | solution.py:208
  56.6 0.8 copy.19
  57.4 10.9 %kept_backward.1 = (bf16[2,64,1536]{2,1,0:T(8,128)(2,1)}, bf16[2,2,192,1536]{3,2,1,0:T(8,128)(2,1)}, f32[3,1536]{1,0:T(4,128)}) custom-call(s32[2]{0:T(128)} %pad_add_fusion.1.meta_ref, bf16[3,192,1536]{2,1,0:T(8,128)(2,1)} %bitcast.32, bf16[2,64,1536]{2,1,0:T(8,128)(2,1)} %bitcast.27), custom_call_target="tpu_custom_call" | custom-call | flops 226492416 | bytes 2949120 | tf_op jit(solution)/shard_map/kept_backward/pallas_call | solution.py:137
  68.3 0.0 collective-permute-done.x_ref
  68.3 0.0 copy-start.1
  68.3 24.8 %collective-permute-start.2 = (bf16[448,256]{1,0:T(8,128)(2,1)S(1)}, bf16[448,256]{1,0:T(8,128)(2,1)S(1)}, u32[]{:S(2)}, u32[]{:S(2)}) collective-permute-start(bf16[448,256]{1,0:T(8,128)(2,1)S(1)} %pad_maximum_fusion.1), channel_id=1, source_target_pairs={{0,8},{4,12},{8,0},{12,4},{1,9},{5,13},{9,1},{13,5},{2,10},{6,14},... | collective-permute-start | bytes 688136 | tf_op jit(solution)/shard_map/ppermute | solution.py:18
  93.1 1.2 %pad_add_fusion.meta_ref = s32[2]{0:T(128)} fusion(s32[1]{0:T(128)} %bitcast.1, s32[1]{0:T(128)} %bitcast), kind=kLoop, calls=%fused_computation.10 | loop fusion | flops 2 | bytes 16 | tf_op jit(solution)/shard_map/stack | solution.py:168
  94.4 0.0 copy-done.1
  94.4 9.3 %held_backward.2 = (bf16[2,64,1536]{2,1,0:T(8,128)(2,1)}, bf16[2,2,192,1536]{3,2,1,0:T(8,128)(2,1)}, f32[3,1536]{1,0:T(4,128)}) custom-call(s32[2]{0:T(128)} %pad_add_fusion.meta_ref, bf16[448,1280]{1,0:T(8,128)(2,1)} %copy-done.1, bf16[2,64,1536]{2,1,0:T(8,128)(2,1)} %bitcast.28, ...), custom_call_target="tpu_custom_call", output_to_operand_aliasing={{0}: (3, {}), {1}: (4, {}), {2}: (5, {})} | custom-call | flops 188743680 | bytes 2457600 | tf_op jit(solution)/shard_map/held_backward/pallas_call | solution.py:169
  103.7 0.0 collective-permute-done.2.x_ref
  103.7 0.0 copy-start.3
  103.7 0.7 copy-done.3
  104.4 3.7 %held_backward.3 = (bf16[2,64,1536]{2,1,0:T(8,128)(2,1)}, bf16[2,2,192,1536]{3,2,1,0:T(8,128)(2,1)}, f32[3,1536]{1,0:T(4,128)}) custom-call(s32[2]{0:T(128)} %pad_add_fusion.meta_ref, bf16[448,256]{1,0:T(8,128)(2,1)} %copy-done.3, bf16[2,64,1536]{2,1,0:T(8,128)(2,1)} %bitcast.29, ...), custom_call_target="tpu_custom_call", output_to_operand_aliasing={{0}: (3, {}), {1}: (4, {}), {2}: (5, {})} | custom-call | flops 37748736 | bytes 491520 | tf_op jit(solution)/shard_map/held_backward/pallas_call | solution.py:169
  108.0 1.6 %collective-permute-start.3 = (f32[3,1536]{1,0:T(4,128)}, f32[3,1536]{1,0:T(4,128)S(1)}, u32[]{:S(2)}, u32[]{:S(2)}) collective-permute-start(f32[3,1536]{1,0:T(4,128)} %get-tuple-element.30), channel_id=1, source_target_pairs={{0,16},{16,0},{1,17},{17,1},{2,18},{18,2},{3,19},{19,3},{4,20},{20... | collective-permute-start | bytes 55304 | tf_op jit(solution)/shard_map/ppermute | solution.py:18
  109.6 2.5 %collective-permute-done.3 = f32[3,1536]{1,0:T(4,128)S(1)} collective-permute-done((f32[3,1536]{1,0:T(4,128)}, f32[3,1536]{1,0:T(4,128)S(1)}, u32[]{:S(2)}, u32[]{:S(2)}) %collective-permute-start.3) | collective-permute-done | bytes 18464 | tf_op jit(solution)/shard_map/ppermute | solution.py:18
  112.1 0.7 add_bitcast_fusion
  112.8 0.6 copy.20
  (3 shorter events, 0.0 us)
Async XLA Ops:
  0.6 4.6 %copy-start = (bf16[1,1,3,192,1536]{4,3,2,1,0:T(8,128)(2,1)S(1)}, bf16[1,1,3,192,1536]{4,3,2,1,0:T(8,128)(2,1)}, u32[]{:S(2)}) copy-start(bf16[1,1,3,192,1536]{4,3,2,1,0:T(8,128)(2,1)} %param.6) | copy-start | bytes 5308420
  5.2 6.6 %copy-start.2 = (bf16[64,1536]{1,0:T(8,128)(2,1)}, bf16[64,1536]{1,0:T(8,128)(2,1)S(1)}, u32[]{:S(2)}) copy-start(bf16[64,1536]{1,0:T(8,128)(2,1)S(1)} %dynamic-slice_bitcast_fusion) | copy-start | bytes 589828
  5.2 5.2 %copy-start.4 = (bf16[1,1,2,16,6144]{4,3,2,1,0:T(8,128)(2,1)S(1)}, bf16[1,1,2,16,6144]{4,3,2,1,0:T(8,128)(2,1)}, u32[]{:S(2)}) copy-start(bf16[1,1,2,16,6144]{4,3,2,1,0:T(8,128)(2,1)} %param.7) | copy-start | bytes 1179652
  6.4 61.9 %collective-permute-start = (bf16[448,1280]{1,0:T(8,128)(2,1)}, bf16[448,1280]{1,0:T(8,128)(2,1)S(1)}, u32[]{:S(2)}, u32[]{:S(2)}) collective-permute-start(bf16[448,1280]{1,0:T(8,128)(2,1)} %pad_maximum_fusion), channel_id=1, source_target_pairs={{0,8},{4,12},{8,0},{12,4},{1,9},{5,13},{9,1},{13,5},{2,10},{6,14},... | collective-permute-start | bytes 3440648 | tf_op jit(solution)/shard_map/ppermute | solution.py:18
  10.5 33.2 %collective-permute-start.1 = (bf16[2,16,6144]{2,1,0:T(8,128)(2,1)S(1)}, bf16[2,16,6144]{2,1,0:T(8,128)(2,1)}, u32[]{:S(2)}, u32[]{:S(2)}) collective-permute-start(bf16[2,16,6144]{2,1,0:T(8,128)(2,1)S(1)} %bitcast.36), channel_id=1, source_target_pairs={{0,12},{4,0},{8,4},{12,8},{1,13},{5,1},{9,5},{13,9},{2,14},{6,2},{... | collective-permute-start | bytes 1179656 | tf_op jit(solution)/shard_map/ppermute | solution.py:18
  11.8 37.4 %slice-start = ((bf16[64,1536]{1,0:T(8,128)(2,1)}), bf16[64,256]{1,0:T(8,128)(2,1)S(1)}, s32[]{:S(2)}) async-start(bf16[64,1536]{1,0:T(8,128)(2,1)} %copy-done.2), calls=%async_computation.1 | async-start | bytes 65536 | tf_op jit(solution)/shard_map/slice | solution.py:199
  45.8 10.9 %all-to-all-start = ((bf16[4,2,16,1536]{3,2,1,0:T(8,128)(2,1)}), bf16[4,2,16,1536]{3,2,1,0:T(8,128)(2,1)S(1)}, u32[]{:S(2)}, u32[]{:S(2)}) async-start(bf16[4,2,16,1536]{3,2,1,0:T(8,128)(2,1)} %copy.18), calls=%async_computation | async-start | bytes 786432 | tf_op jit(solution)/shard_map/all_to_all | solution.py:208
  68.3 26.1 %copy-start.1 = (bf16[448,1280]{1,0:T(8,128)(2,1)}, bf16[448,1280]{1,0:T(8,128)(2,1)S(1)}, u32[]{:S(2)}) copy-start(bf16[448,1280]{1,0:T(8,128)(2,1)S(1)} %collective-permute-done.x_ref) | copy-start | bytes 3440644
  68.3 35.4 %collective-permute-start.2 = (bf16[448,256]{1,0:T(8,128)(2,1)S(1)}, bf16[448,256]{1,0:T(8,128)(2,1)S(1)}, u32[]{:S(2)}, u32[]{:S(2)}) collective-permute-start(bf16[448,256]{1,0:T(8,128)(2,1)S(1)} %pad_maximum_fusion.1), channel_id=1, source_target_pairs={{0,8},{4,12},{8,0},{12,4},{1,9},{5,13},{9,1},{13,5},{2,10},{6,14},... | collective-permute-start | bytes 688136 | tf_op jit(solution)/shard_map/ppermute | solution.py:18
  103.7 0.7 copy-start.3
  108.0 4.0 %collective-permute-start.3 = (f32[3,1536]{1,0:T(4,128)}, f32[3,1536]{1,0:T(4,128)S(1)}, u32[]{:S(2)}, u32[]{:S(2)}) collective-permute-start(f32[3,1536]{1,0:T(4,128)} %get-tuple-element.30), channel_id=1, source_target_pairs={{0,16},{16,0},{1,17},{17,1},{2,18},{18,2},{3,19},{19,3},{4,20},{20... | collective-permute-start | bytes 55304 | tf_op jit(solution)/shard_map/ppermute | solution.py:18

commit v5 on v2

--- a/solution.py
+++ b/solution.py
@@ -9,7 +9,7 @@
 
 HD = 128
 MASK_FILL = -1e30
-MAX_CHUNKS = 4
+MAX_CHUNKS = 1
 NT_DIMS = (((1,), (1,)), ((), ()))
 
 
@@ -50,7 +50,7 @@
         store(cols, *head_backward(q, k, v, g, visible))
         return carry
 
-    lax.fori_loop(0, heads, head, 0)
+    lax.fori_loop(0, heads, head, 0, unroll=True)
 
 
 class Loader:

time: 101 us -> 117 us (1.16)
  the two profiles are of different devices: /device:TPU:0 before, /device:TPU:12 now
where the time goes in v5:
time: 117 us; the launch traced here: 116 us
  waiting for transfers between devices  74.1 us (63%)
  Pallas kernels  21.6 us (18%)
  local copies, waits for them, and re-layouts  7.06 us (6%)
  starting transfers between devices  7.02 us (6%)
  between operations  3.29 us (3%)
  other arithmetic  3.27 us (3%)
    ppermute x3, waiting for transfers between devices, from_behind(): return lax.ppermute(value, axis, pairs)  69.6 us
    pallas_call x1, Pallas kernels, kept_backward(): pl.pallas_call(kept_kernel, out_shape=out_shape, grid_spec=grid_spec, cos...  10.9 us
    pallas_call x1, Pallas kernels, held_backward(): pl.pallas_call(held_kernel, out_shape=(jax.ShapeDtypeStruct(qg.shape, qg....  10.8 us
    all_to_all x1, waiting for transfers between devices, body(): lax.all_to_all(split, 'tensor', split_axis=0, concat_axis=0, tiled=True)  4.44 us
    ppermute x3, starting transfers between devices, from_behind(): return lax.ppermute(value, axis, pairs)  3.56 us
    all_to_all x1, starting transfers between devices, body(): lax.all_to_all(split, 'tensor', split_axis=0, concat_axis=0, tiled=True)  3.46 us
  transfers between devices with their start and end apart: 4, of which 3 were waited for; matrix products, arithmetic and copies ran while one was open for 4% of the time, Pallas kernels for 9%

profile of v5, /device:TPU:12, one launch (start us, length us, event | category | flops | bytes accessed | tf_op | source)
XLA Modules:
  0.0 116.3 jit_solution(1115004333285299014)
XLA Ops:
  0.6 0.8 constant_dynamic-slice_fusion
  1.5 0.5 slice.31
  3.3 1.5 %fusion = (bf16[1,1,1,192,1536]{4,3,2,1,0:T(8,128)(2,1)S(1)}, bf16[192,1536]{1,0:T(8,128)(2,1)S(1)}, bf16[192,1536]{1,0:T(8,128)(2,1)S(1)}) fusion(bf16[1,1,3,192,1536]{4,3,2,1,0:T(8,128)(2,1)} %param.6), kind=kLoop, calls=%fused_computation.9 | loop fusion | bytes 3538944 | tf_op jit(solution)/shard_map/slice | solution.py:201
  5.5 0.0 copy-start.1
  5.5 0.1 dynamic-slice_bitcast_fusion
  5.6 0.1 pad_maximum_fusion
  5.7 2.7 %collective-permute-start = (bf16[448,1536]{1,0:T(8,128)(2,1)S(1)}, bf16[448,1536]{1,0:T(8,128)(2,1)S(1)}, u32[]{:S(2)}, u32[]{:S(2)}) collective-permute-start(bf16[448,1536]{1,0:T(8,128)(2,1)S(1)} %pad_maximum_fusion), channel_id=1, source_target_pairs={{0,8},{4,12},{8,0},{12,4},{1,9},{5,13},{9,1},{13,5},{2,10},{6,14},... | collective-permute-start | bytes 4128776 | tf_op jit(solution)/shard_map/ppermute | solution.py:19
  8.3 0.0 copy-done.1
  8.3 0.4 collective-permute-start.1
  9.4 66.0 %collective-permute-done.1 = bf16[2,16,6144]{2,1,0:T(8,128)(2,1)S(1)} collective-permute-done((bf16[2,16,6144]{2,1,0:T(8,128)(2,1)S(1)}, bf16[2,16,6144]{2,1,0:T(8,128)(2,1)S(1)}, u32[]{:S(2)}, u32[]{:S(2)}) %collective-permute-start.1) | collective-permute-done | bytes 393248 | tf_op jit(solution)/shard_map/ppermute | solution.py:19
  75.5 0.3 reshape.30
  75.7 0.8 copy.15
  76.5 3.5 %all-to-all-start = ((bf16[4,2,16,1536]{3,2,1,0:T(8,128)(2,1)}), bf16[4,2,16,1536]{3,2,1,0:T(8,128)(2,1)S(1)}, u32[]{:S(2)}, u32[]{:S(2)}) async-start(bf16[4,2,16,1536]{3,2,1,0:T(8,128)(2,1)} %copy.15), calls=%async_computation | async-start | bytes 786432 | tf_op jit(solution)/shard_map/all_to_all | solution.py:214
  80.0 0.5 fusion.1
  80.6 1.3 %pad_add_fusion.1.meta_ref = s32[2]{0:T(128)} fusion(s32[1]{0:T(128)} %bitcast.20, s32[1]{0:T(128)} %bitcast.10), kind=kLoop, calls=%fused_computation.8 | loop fusion | flops 2 | bytes 16 | tf_op jit(solution)/shard_map/stack | solution.py:137
  81.8 1.1 pad_add_fusion.meta_ref
  83.0 4.4 %all-to-all-done = bf16[4,2,16,1536]{3,2,1,0:T(8,128)(2,1)S(1)} async-done(((bf16[4,2,16,1536]{3,2,1,0:T(8,128)(2,1)}), bf16[4,2,16,1536]{3,2,1,0:T(8,128)(2,1)S(1)}, u32[]{:S(2)}, u32[]{:S(2)}) %all-to-all-start) | async-done | bytes 393248 | tf_op jit(solution)/shard_map/all_to_all | solution.py:214
  87.4 0.8 copy.16
  88.2 10.9 %kept_backward.1 = (bf16[2,64,1536]{2,1,0:T(8,128)(2,1)}, bf16[2,2,192,1536]{3,2,1,0:T(8,128)(2,1)}, f32[3,1536]{1,0:T(4,128)}) custom-call(s32[2]{0:T(128)} %pad_add_fusion.1.meta_ref, bf16[3,192,1536]{2,1,0:T(8,128)(2,1)} %bitcast.24, bf16[2,64,1536]{2,1,0:T(8,128)(2,1)} %bitcast.21), custom_call_target="tpu_custom_call" | custom-call | flops 226492416 | bytes 2949120 | tf_op jit(solution)/shard_map/kept_backward/pallas_call | solution.py:138
  99.1 0.0 collective-permute-done.x_ref
  99.1 0.0 copy-start
  99.1 1.1 copy-done
  100.2 10.8 %held_backward.1 = (bf16[2,64,1536]{2,1,0:T(8,128)(2,1)}, bf16[2,2,192,1536]{3,2,1,0:T(8,128)(2,1)}, f32[3,1536]{1,0:T(4,128)}) custom-call(s32[2]{0:T(128)} %pad_add_fusion.meta_ref, bf16[448,1536]{1,0:T(8,128)(2,1)} %copy-done, bf16[2,64,1536]{2,1,0:T(8,128)(2,1)} %bitcast.22, ...), custom_call_target="tpu_custom_call", output_to_operand_aliasing={{0}: (3, {}), {1}: (4, {}), {2}: (5, {})} | custom-call | flops 226492416 | bytes 2949120 | tf_op jit(solution)/shard_map/held_backward/pallas_call | solution.py:168
  110.9 0.5 collective-permute-start.2
  111.4 3.6 %collective-permute-done.2 = f32[3,1536]{1,0:T(4,128)S(1)} collective-permute-done((f32[3,1536]{1,0:T(4,128)}, f32[3,1536]{1,0:T(4,128)S(1)}, u32[]{:S(2)}, u32[]{:S(2)}) %collective-permute-start.2) | collective-permute-done | bytes 18464 | tf_op jit(solution)/shard_map/ppermute | solution.py:19
  115.0 0.7 add_bitcast_fusion
  115.7 0.6 copy.17
Async XLA Ops:
  5.5 2.8 %copy-start.1 = (bf16[1,1,2,16,6144]{4,3,2,1,0:T(8,128)(2,1)S(1)}, bf16[1,1,2,16,6144]{4,3,2,1,0:T(8,128)(2,1)}, u32[]{:S(2)}) copy-start(bf16[1,1,2,16,6144]{4,3,2,1,0:T(8,128)(2,1)} %param.7) | copy-start | bytes 1179652
  5.7 93.4 %collective-permute-start = (bf16[448,1536]{1,0:T(8,128)(2,1)S(1)}, bf16[448,1536]{1,0:T(8,128)(2,1)S(1)}, u32[]{:S(2)}, u32[]{:S(2)}) collective-permute-start(bf16[448,1536]{1,0:T(8,128)(2,1)S(1)} %pad_maximum_fusion), channel_id=1, source_target_pairs={{0,8},{4,12},{8,0},{12,4},{1,9},{5,13},{9,1},{13,5},{2,10},{6,14},... | collective-permute-start | bytes 4128776 | tf_op jit(solution)/shard_map/ppermute | solution.py:19
  8.3 67.1 %collective-permute-start.1 = (bf16[2,16,6144]{2,1,0:T(8,128)(2,1)S(1)}, bf16[2,16,6144]{2,1,0:T(8,128)(2,1)S(1)}, u32[]{:S(2)}, u32[]{:S(2)}) collective-permute-start(bf16[2,16,6144]{2,1,0:T(8,128)(2,1)S(1)} %bitcast.28), channel_id=1, source_target_pairs={{0,12},{4,0},{8,4},{12,8},{1,13},{5,1},{9,5},{13,9},{2,14},{6,2},{... | collective-permute-start | bytes 1179656 | tf_op jit(solution)/shard_map/ppermute | solution.py:19
  76.5 10.9 %all-to-all-start = ((bf16[4,2,16,1536]{3,2,1,0:T(8,128)(2,1)}), bf16[4,2,16,1536]{3,2,1,0:T(8,128)(2,1)S(1)}, u32[]{:S(2)}, u32[]{:S(2)}) async-start(bf16[4,2,16,1536]{3,2,1,0:T(8,128)(2,1)} %copy.15), calls=%async_computation | async-start | bytes 786432 | tf_op jit(solution)/shard_map/all_to_all | solution.py:214
  99.1 1.1 copy-start
  110.9 4.0 %collective-permute-start.2 = (f32[3,1536]{1,0:T(4,128)}, f32[3,1536]{1,0:T(4,128)S(1)}, u32[]{:S(2)}, u32[]{:S(2)}) collective-permute-start(f32[3,1536]{1,0:T(4,128)} %get-tuple-element.14), channel_id=1, source_target_pairs={{0,16},{16,0},{1,17},{17,1},{2,18},{18,2},{3,19},{19,3},{4,20},{20... | collective-permute-start | bytes 55304 | tf_op jit(solution)/shard_map/ppermute | solution.py:19

commit v6 on v5

--- a/solution.py
+++ b/solution.py
@@ -9,7 +9,7 @@
 
 HD = 128
 MASK_FILL = -1e30
-MAX_CHUNKS = 1
+MAX_CHUNKS = 4
 NT_DIMS = (((1,), (1,)), ((), ()))
 
 
@@ -89,8 +89,7 @@
     head_loop(offset, load, store_into(qg_ref, kv_ref, sum_ref, add=False))
 
 
-def held_kernel(meta_ref, x_ref, g_ref, qg_in, kv_in, sum_in, qg_ref, kv_ref, sum_ref):
-    del qg_in, kv_in
+def held_kernel(meta_ref, x_ref, g_ref, qg_ref, kv_ref, sum_ref):
     offset = meta_ref[0]
     rows, feats = g_ref.shape
     keys = (x_ref.shape[0] - rows) // 2
@@ -99,8 +98,7 @@
                       x_ref[pl.ds(rows + keys, keys), cols], g_ref[:, cols]),
         rows, keys, feats // HD,
     )
-    sum_ref[...] = sum_in[...]
-    head_loop(offset, load, store_into(qg_ref, kv_ref, sum_ref, add=True))
+    head_loop(offset, load, store_into(qg_ref, kv_ref, sum_ref, add=False))
 
 
 def kernel_cost(rows, keys, feats):
@@ -144,39 +142,36 @@
     )(meta, stash, grads)
 
 
-def held_backward(part, grads, offset, pick, chunk, qg, kv, sums):
+def held_backward(part, grads, offset, pick, chunk):
     rows = grads.shape[1]
     width = part.shape[1]
     keys = (part.shape[0] - rows) // 2
+    bf16 = jnp.bfloat16
     grid_spec = pltpu.PrefetchScalarGridSpec(
         num_scalar_prefetch=1,
         grid=(1,),
         in_specs=[
             pl.BlockSpec((part.shape[0], width), lambda i, m: (0, 0)),
             pl.BlockSpec((None, rows, width), lambda i, m: (m[1], 0, chunk)),
-            pl.BlockSpec(memory_space=pl.ANY),
-            pl.BlockSpec(memory_space=pl.ANY),
-            pl.BlockSpec((3, width), lambda i, m: (0, chunk)),
         ],
         out_specs=(
-            pl.BlockSpec((None, rows, width), lambda i, m: (1, 0, chunk)),
-            pl.BlockSpec((None, 2, keys, width), lambda i, m: (1, 0, 0, chunk)),
-            pl.BlockSpec((3, width), lambda i, m: (0, chunk)),
+            pl.BlockSpec((rows, width), lambda i, m: (0, 0)),
+            pl.BlockSpec((2, keys, width), lambda i, m: (0, 0, 0)),
+            pl.BlockSpec((3, width), lambda i, m: (0, 0)),
         ),
     )
     meta = jnp.stack([offset, 1 - pick]).astype(jnp.int32)
     return pl.pallas_call(
         held_kernel,
         out_shape=(
-            jax.ShapeDtypeStruct(qg.shape, qg.dtype),
-            jax.ShapeDtypeStruct(kv.shape, kv.dtype),
-            jax.ShapeDtypeStruct(sums.shape, sums.dtype),
+            jax.ShapeDtypeStruct((rows, width), bf16),
+            jax.ShapeDtypeStruct((2, keys, width), bf16),
+            jax.ShapeDtypeStruct((3, width), jnp.float32),
         ),
         grid_spec=grid_spec,
-        input_output_aliases={3: 0, 4: 1, 5: 2},
         cost_estimate=kernel_cost(rows, keys, width),
         name="held_backward",
-    )(meta, part, grads, qg, kv, sums)
+    )(meta, part, grads)
 
 
 def chunk_count(heads):
@@ -216,10 +211,13 @@
     pick = order[0, 0]
     section_offsets = lax.dynamic_index_in_dim(offsets[0], section_index, 0, keepdims=False)
     qg, kv, column_sums = kept_backward(kept_qkv[0, 0], regrouped, section_offsets[0], pick)
-    for c in range(chunks):
-        qg, kv, column_sums = held_backward(
-            fetched[c], regrouped, section_offsets[1], pick, c, qg, kv, column_sums
-        )
+    held_parts = [
+        held_backward(fetched[c], regrouped, section_offsets[1], pick, c) for c in range(chunks)
+    ]
+    for c, (part_q, part_kv, _) in enumerate(held_parts):
+        qg = lax.dynamic_update_slice(qg, part_q[None], (1, 0, c * width))
+        kv = lax.dynamic_update_slice(kv, part_kv[None], (1, 0, 0, c * width))
+    column_sums = column_sums + jnp.concatenate([part[2] for part in held_parts], axis=1)
     query_grad = qg
     key_value_grad = kv
     if lax.axis_size("dp") == 2:

time: 117 us -> 96.9 us (0.83)
  the two profiles are of different devices: /device:TPU:12 before, /device:TPU:0 now
where the time goes in v6:
time: 96.9 us; the launch traced here: 96.4 us
  waiting for transfers between devices  30 us (31%)
  Pallas kernels  28.5 us (29%)
  starting transfers between devices  16.2 us (17%)
  local copies, waits for them, and re-layouts  14.2 us (15%)
  other arithmetic  4.18 us (4%)
  between operations  3.36 us (3%)
    ppermute x6, waiting for transfers between devices, from_behind(): return lax.ppermute(value, axis, pairs)  25.7 us
    pallas_call x4, Pallas kernels, held_backward(): pl.pallas_call(held_kernel, out_shape=(jax.ShapeDtypeStruct((rows, width)...  17.5 us
    ppermute x6, starting transfers between devices, from_behind(): return lax.ppermute(value, axis, pairs)  12.7 us
    pallas_call x1, Pallas kernels, kept_backward(): pl.pallas_call(kept_kernel, out_shape=out_shape, grid_spec=grid_spec, cos...  11 us
    all_to_all x1, waiting for transfers between devices, body(): lax.all_to_all(split, 'tensor', split_axis=0, concat_axis=0, tiled=True)  4.31 us
    unnamed x33, local copies, waits for them, and re-layouts  3.6 us
    all_to_all x1, starting transfers between devices, body(): lax.all_to_all(split, 'tensor', split_axis=0, concat_axis=0, tiled=True)  3.46 us
    dynamic_update_slice x4, local copies, waits for them, and re-layouts, body(): kv = lax.dynamic_update_slice(kv, part_kv[None], (1, 0, 0, c * width))  2.97 us
  transfers between devices with their start and end apart: 7, of which 4 were waited for; matrix products, arithmetic and copies ran while one was open for 14% of the time, Pallas kernels for 25%

profile of v6, /device:TPU:0, one launch (start us, length us, event | category | flops | bytes accessed | tf_op | source)
XLA Modules:
  0.0 96.4 jit_solution(3274256518755725306)
XLA Ops:
  0.6 0.0 copy-start
  0.6 5.1 %collective-permute-start = (bf16[2,16,6144]{2,1,0:T(8,128)(2,1)}, bf16[2,16,6144]{2,1,0:T(8,128)(2,1)S(1)}, u32[]{:S(2)}, u32[]{:S(2)}) collective-permute-start(bf16[2,16,6144]{2,1,0:T(8,128)(2,1)} %bitcast.60), channel_id=1, source_target_pairs={{0,12},{4,0},{8,4},{12,8},{1,13},{5,1},{9,5},{13,9},{2,14},{6,2},{... | collective-permute-start | bytes 1179656 | tf_op jit(solution)/shard_map/ppermute | solution.py:19
  5.7 0.8 constant_dynamic-slice_fusion
  6.6 0.5 slice.64
  8.4 1.1 %slice.63 = bf16[1,1,1,192,1536]{4,3,2,1,0:T(8,128)(2,1)S(1)} slice(bf16[1,1,3,192,1536]{4,3,2,1,0:T(8,128)(2,1)} %param.6), slice={[0:1], [0:1], [0:1], [0:192], [0:1536]} | slice | bytes 1179648 | tf_op jit(solution)/shard_map/slice | solution.py:196
  10.1 0.1 dynamic-slice_bitcast_fusion
  10.2 0.0 copy-done
  10.2 0.1 slice_bitcast_fusion.1
  10.4 0.8 pad_maximum_fusion
  11.1 0.0 collective-permute-start.1
  11.2 3.0 %collective-permute-start.2 = (bf16[448,384]{1,0:T(8,128)(2,1)S(1)}, bf16[448,384]{1,0:T(8,128)(2,1)S(1)}, u32[]{:S(2)}, u32[]{:S(2)}) collective-permute-start(bf16[448,384]{1,0:T(8,128)(2,1)S(1)} %pad_maximum_fusion.1), channel_id=1, source_target_pairs={{0,8},{4,12},{8,0},{12,4},{1,9},{5,13},{9,1},{13,5},{2,10},{6,14},... | collective-permute-start | bytes 1032200 | tf_op jit(solution)/shard_map/ppermute | solution.py:19
  14.2 0.1 collective-permute-start.3
  14.3 3.0 %collective-permute-start.4 = (bf16[448,384]{1,0:T(8,128)(2,1)S(1)}, bf16[448,384]{1,0:T(8,128)(2,1)S(1)}, u32[]{:S(2)}, u32[]{:S(2)}) collective-permute-start(bf16[448,384]{1,0:T(8,128)(2,1)S(1)} %pad_maximum_fusion.3), channel_id=1, source_target_pairs={{0,8},{4,12},{8,0},{12,4},{1,9},{5,13},{9,1},{13,5},{2,10},{6,14},... | collective-permute-start | bytes 1032200 | tf_op jit(solution)/shard_map/ppermute | solution.py:19
  18.0 0.0 collective-permute-done
  18.0 0.3 reshape.50
  18.3 0.8 copy.12
  19.1 3.5 %all-to-all-start = ((bf16[4,2,16,1536]{3,2,1,0:T(8,128)(2,1)}), bf16[4,2,16,1536]{3,2,1,0:T(8,128)(2,1)S(1)}, u32[]{:S(2)}, u32[]{:S(2)}) async-start(bf16[4,2,16,1536]{3,2,1,0:T(8,128)(2,1)} %copy.12), calls=%async_computation | async-start | bytes 786432 | tf_op jit(solution)/shard_map/all_to_all | solution.py:209
  22.5 0.6 fusion.1
  23.1 1.3 %pad_add_fusion.1.meta_ref = s32[2]{0:T(128)} fusion(s32[1]{0:T(128)} %bitcast.9, s32[1]{0:T(128)} %bitcast.8), kind=kLoop, calls=%fused_computation.26 | loop fusion | flops 2 | bytes 16 | tf_op jit(solution)/shard_map/stack | solution.py:163
  24.4 1.2 %pad_add_fusion.meta_ref = s32[2]{0:T(128)} fusion(s32[1]{0:T(128)} %bitcast.49, s32[1]{0:T(128)} %bitcast), kind=kLoop, calls=%fused_computation.25 | loop fusion | flops 2 | bytes 16 | tf_op jit(solution)/shard_map/stack | solution.py:135
  25.6 4.3 %all-to-all-done = bf16[4,2,16,1536]{3,2,1,0:T(8,128)(2,1)S(1)} async-done(((bf16[4,2,16,1536]{3,2,1,0:T(8,128)(2,1)}), bf16[4,2,16,1536]{3,2,1,0:T(8,128)(2,1)S(1)}, u32[]{:S(2)}, u32[]{:S(2)}) %all-to-all-start) | async-done | bytes 393248 | tf_op jit(solution)/shard_map/all_to_all | solution.py:209
  29.9 0.8 copy.13
  30.7 21.1 %collective-permute-done.1.x_ref = bf16[448,384]{1,0:T(8,128)(2,1)S(1)} collective-permute-done((bf16[448,384]{1,0:T(8,128)(2,1)}, bf16[448,384]{1,0:T(8,128)(2,1)S(1)}, u32[]{:S(2)}, u32[]{:S(2)}) %collective-permute-start.1) | collective-permute-done | bytes 344096 | tf_op jit(solution)/shard_map/ppermute | solution.py:19
  51.9 0.0 copy-start.4
  51.9 0.7 copy-done.4
  52.6 4.4 %held_backward.4 = (bf16[64,384]{1,0:T(8,128)(2,1)}, bf16[2,192,384]{2,1,0:T(8,128)(2,1)}, f32[3,384]{1,0:T(4,128)}) custom-call(s32[2]{0:T(128)} %pad_add_fusion.1.meta_ref, bf16[448,384]{1,0:T(8,128)(2,1)} %copy-done.4, bf16[2,64,1536]{2,1,0:T(8,128)(2,1)} %bitcast.50), custom_call_target="tpu_custom_call" | custom-call | flops 56623104 | bytes 737280 | tf_op jit(solution)/shard_map/held_backward/pallas_call | solution.py:164
  57.0 0.0 copy-start.13
  57.0 0.0 copy-start.9
  57.0 0.0 copy-start.5
  57.0 2.2 %collective-permute-done.2.x_ref = bf16[448,384]{1,0:T(8,128)(2,1)S(1)} collective-permute-done((bf16[448,384]{1,0:T(8,128)(2,1)S(1)}, bf16[448,384]{1,0:T(8,128)(2,1)S(1)}, u32[]{:S(2)}, u32[]{:S(2)}) %collective-permute-start.2) | collective-permute-done | bytes 344096 | tf_op jit(solution)/shard_map/ppermute | solution.py:19
  59.2 0.7 copy-done.3
  60.0 4.4 %held_backward.5 = (bf16[64,384]{1,0:T(8,128)(2,1)}, bf16[2,192,384]{2,1,0:T(8,128)(2,1)}, f32[3,384]{1,0:T(4,128)}) custom-call(s32[2]{0:T(128)} %pad_add_fusion.1.meta_ref, bf16[448,384]{1,0:T(8,128)(2,1)} %copy-done.3, bf16[2,64,1536]{2,1,0:T(8,128)(2,1)} %bitcast.51), custom_call_target="tpu_custom_call" | custom-call | flops 56623104 | bytes 737280 | tf_op jit(solution)/shard_map/held_backward/pallas_call | solution.py:164
  64.3 0.0 copy-start.14
  64.3 0.0 copy-start.10
  64.3 2.3 %collective-permute-done.3.x_ref = bf16[448,384]{1,0:T(8,128)(2,1)S(1)} collective-permute-done((bf16[448,384]{1,0:T(8,128)(2,1)S(1)}, bf16[448,384]{1,0:T(8,128)(2,1)S(1)}, u32[]{:S(2)}, u32[]{:S(2)}) %collective-permute-start.3) | collective-permute-done | bytes 344096 | tf_op jit(solution)/shard_map/ppermute | solution.py:19
  66.6 0.7 copy-done.2
  67.3 4.4 %held_backward.6 = (bf16[64,384]{1,0:T(8,128)(2,1)}, bf16[2,192,384]{2,1,0:T(8,128)(2,1)}, f32[3,384]{1,0:T(4,128)}) custom-call(s32[2]{0:T(128)} %pad_add_fusion.1.meta_ref, bf16[448,384]{1,0:T(8,128)(2,1)} %copy-done.2, bf16[2,64,1536]{2,1,0:T(8,128)(2,1)} %bitcast.52), custom_call_target="tpu_custom_call" | custom-call | flops 56623104 | bytes 737280 | tf_op jit(solution)/shard_map/held_backward/pallas_call | solution.py:164
  71.7 11.0 %kept_backward.1 = (bf16[2,64,1536]{2,1,0:T(8,128)(2,1)}, bf16[2,2,192,1536]{3,2,1,0:T(8,128)(2,1)}, f32[3,1536]{1,0:T(4,128)}) custom-call(s32[2]{0:T(128)} %pad_add_fusion.meta_ref, bf16[3,192,1536]{2,1,0:T(8,128)(2,1)} %bitcast.56, bf16[2,64,1536]{2,1,0:T(8,128)(2,1)} %bitcast.53), custom_call_target="tpu_custom_call" | custom-call | flops 226492416 | bytes 2949120 | tf_op jit(solution)/shard_map/kept_backward/pallas_call | solution.py:136
  82.7 0.0 collective-permute-done.4.x_ref
  82.8 0.7 copy-done.1
  83.5 4.4 %held_backward.7 = (bf16[64,384]{1,0:T(8,128)(2,1)}, bf16[2,192,384]{2,1,0:T(8,128)(2,1)}, f32[3,384]{1,0:T(4,128)}) custom-call(s32[2]{0:T(128)} %pad_add_fusion.1.meta_ref, bf16[448,384]{1,0:T(8,128)(2,1)} %copy-done.1, bf16[2,64,1536]{2,1,0:T(8,128)(2,1)} %bitcast.54), custom_call_target="tpu_custom_call" | custom-call | flops 56623104 | bytes 737280 | tf_op jit(solution)/shard_map/held_backward/pallas_call | solution.py:164
  87.9 0.0 copy-done.13
  87.9 0.0 copy-done.14
  87.9 0.0 copy-done.15
  87.9 0.8 maximum_add_fusion
  88.7 1.6 %collective-permute-start.5 = (f32[3,1536]{1,0:T(4,128)S(1)}, f32[3,1536]{1,0:T(4,128)S(1)}, u32[]{:S(2)}, u32[]{:S(2)}) collective-permute-start(f32[3,1536]{1,0:T(4,128)S(1)} %maximum_add_fusion), channel_id=1, source_target_pairs={{0,16},{16,0},{1,17},{17,1},{2,18},{18,2},{3,19},{19,3},{4,20},{20... | collective-permute-start | bytes 55304 | tf_op jit(solution)/shard_map/ppermute | solution.py:19
  90.3 0.0 copy-done.9
  90.3 0.6 bitcast_dynamic-update-slice_fusion.7
  90.9 0.0 copy-done.10
  90.9 0.6 bitcast_dynamic-update-slice_fusion.6
  91.5 0.0 copy-done.12
  91.5 0.6 bitcast_dynamic-update-slice_fusion.5
  92.2 0.0 copy-done.5
  92.2 0.7 bitcast_dynamic-update-slice_fusion.3
  92.9 0.0 copy-done.6
  92.9 0.7 bitcast_dynamic-update-slice_fusion.2
  93.7 0.0 copy-done.7
  93.7 0.7 bitcast_dynamic-update-slice_fusion.1
  94.4 0.0 copy-done.8
  94.4 0.7 bitcast_dynamic-update-slice_fusion
  95.1 0.0 copy-done.11
  95.2 0.6 bitcast_dynamic-update-slice_fusion.4
  95.8 0.0 collective-permute-done.5
  95.8 0.6 copy.14
  (14 shorter events, 0.2 us)
Async XLA Ops:
  0.6 9.6 %copy-start = (bf16[1,1,3,192,1536]{4,3,2,1,0:T(8,128)(2,1)S(1)}, bf16[1,1,3,192,1536]{4,3,2,1,0:T(8,128)(2,1)}, u32[]{:S(2)}) copy-start(bf16[1,1,3,192,1536]{4,3,2,1,0:T(8,128)(2,1)} %param.6) | copy-start | bytes 5308420
  0.6 17.3 %collective-permute-start = (bf16[2,16,6144]{2,1,0:T(8,128)(2,1)}, bf16[2,16,6144]{2,1,0:T(8,128)(2,1)S(1)}, u32[]{:S(2)}, u32[]{:S(2)}) collective-permute-start(bf16[2,16,6144]{2,1,0:T(8,128)(2,1)} %bitcast.60), channel_id=1, source_target_pairs={{0,12},{4,0},{8,4},{12,8},{1,13},{5,1},{9,5},{13,9},{2,14},{6,2},{... | collective-permute-start | bytes 1179656 | tf_op jit(solution)/shard_map/ppermute | solution.py:19
  11.1 40.7 %collective-permute-start.1 = (bf16[448,384]{1,0:T(8,128)(2,1)}, bf16[448,384]{1,0:T(8,128)(2,1)S(1)}, u32[]{:S(2)}, u32[]{:S(2)}) collective-permute-start(bf16[448,384]{1,0:T(8,128)(2,1)} %pad_maximum_fusion), channel_id=1, source_target_pairs={{0,8},{4,12},{8,0},{12,4},{1,9},{5,13},{9,1},{13,5},{2,10},{6,14},... | collective-permute-start | bytes 1032200 | tf_op jit(solution)/shard_map/ppermute | solution.py:19
  11.2 48.1 %collective-permute-start.2 = (bf16[448,384]{1,0:T(8,128)(2,1)S(1)}, bf16[448,384]{1,0:T(8,128)(2,1)S(1)}, u32[]{:S(2)}, u32[]{:S(2)}) collective-permute-start(bf16[448,384]{1,0:T(8,128)(2,1)S(1)} %pad_maximum_fusion.1), channel_id=1, source_target_pairs={{0,8},{4,12},{8,0},{12,4},{1,9},{5,13},{9,1},{13,5},{2,10},{6,14},... | collective-permute-start | bytes 1032200 | tf_op jit(solution)/shard_map/ppermute | solution.py:19
  14.2 52.4 %collective-permute-start.3 = (bf16[448,384]{1,0:T(8,128)(2,1)S(1)}, bf16[448,384]{1,0:T(8,128)(2,1)S(1)}, u32[]{:S(2)}, u32[]{:S(2)}) collective-permute-start(bf16[448,384]{1,0:T(8,128)(2,1)S(1)} %pad_maximum_fusion.2), channel_id=1, source_target_pairs={{0,8},{4,12},{8,0},{12,4},{1,9},{5,13},{9,1},{13,5},{2,10},{6,14},... | collective-permute-start | bytes 1032200 | tf_op jit(solution)/shard_map/ppermute | solution.py:19
  14.3 68.4 %collective-permute-start.4 = (bf16[448,384]{1,0:T(8,128)(2,1)S(1)}, bf16[448,384]{1,0:T(8,128)(2,1)S(1)}, u32[]{:S(2)}, u32[]{:S(2)}) collective-permute-start(bf16[448,384]{1,0:T(8,128)(2,1)S(1)} %pad_maximum_fusion.3), channel_id=1, source_target_pairs={{0,8},{4,12},{8,0},{12,4},{1,9},{5,13},{9,1},{13,5},{2,10},{6,14},... | collective-permute-start | bytes 1032200 | tf_op jit(solution)/shard_map/ppermute | solution.py:19
  19.1 10.9 %all-to-all-start = ((bf16[4,2,16,1536]{3,2,1,0:T(8,128)(2,1)}), bf16[4,2,16,1536]{3,2,1,0:T(8,128)(2,1)S(1)}, u32[]{:S(2)}, u32[]{:S(2)}) async-start(bf16[4,2,16,1536]{3,2,1,0:T(8,128)(2,1)} %copy.12), calls=%async_computation | async-start | bytes 786432 | tf_op jit(solution)/shard_map/all_to_all | solution.py:209
  51.9 0.7 copy-start.4
  57.0 30.9 %copy-start.13 = (f32[3,384]{1,0:T(4,128)S(1)}, f32[3,384]{1,0:T(4,128)}, u32[]{:S(2)}) copy-start(f32[3,384]{1,0:T(4,128)} %get-tuple-element.29) | copy-start | bytes 13828
  57.0 33.3 %copy-start.9 = (bf16[64,384]{1,0:T(8,128)(2,1)S(1)}, bf16[64,384]{1,0:T(8,128)(2,1)}, u32[]{:S(2)}) copy-start(bf16[64,384]{1,0:T(8,128)(2,1)} %get-tuple-element.19) | copy-start | bytes 147460
  57.0 35.2 %copy-start.5 = (bf16[2,192,384]{2,1,0:T(8,128)(2,1)S(1)}, bf16[2,192,384]{2,1,0:T(8,128)(2,1)}, u32[]{:S(2)}) copy-start(bf16[2,192,384]{2,1,0:T(8,128)(2,1)} %get-tuple-element.24) | copy-start | bytes 884740
  59.2 0.7 copy-start.3
  64.3 23.5 %copy-start.14 = (f32[3,384]{1,0:T(4,128)S(1)}, f32[3,384]{1,0:T(4,128)}, u32[]{:S(2)}) copy-start(f32[3,384]{1,0:T(4,128)} %get-tuple-element.30) | copy-start | bytes 13828
  64.3 26.6 %copy-start.10 = (bf16[64,384]{1,0:T(8,128)(2,1)S(1)}, bf16[64,384]{1,0:T(8,128)(2,1)}, u32[]{:S(2)}) copy-start(bf16[64,384]{1,0:T(8,128)(2,1)} %get-tuple-element.20) | copy-start | bytes 147460
  64.3 28.6 %copy-start.6 = (bf16[2,192,384]{2,1,0:T(8,128)(2,1)S(1)}, bf16[2,192,384]{2,1,0:T(8,128)(2,1)}, u32[]{:S(2)}) copy-start(bf16[2,192,384]{2,1,0:T(8,128)(2,1)} %get-tuple-element.25) | copy-start | bytes 884740
  66.6 0.7 copy-start.2
  71.7 16.2 %copy-start.15 = (f32[3,384]{1,0:T(4,128)S(1)}, f32[3,384]{1,0:T(4,128)}, u32[]{:S(2)}) copy-start(f32[3,384]{1,0:T(4,128)} %get-tuple-element.31) | copy-start | bytes 13828
  71.7 19.8 %copy-start.12 = (bf16[64,384]{1,0:T(8,128)(2,1)S(1)}, bf16[64,384]{1,0:T(8,128)(2,1)}, u32[]{:S(2)}) copy-start(bf16[64,384]{1,0:T(8,128)(2,1)} %get-tuple-element.21) | copy-start | bytes 147460
  71.7 21.9 %copy-start.7 = (bf16[2,192,384]{2,1,0:T(8,128)(2,1)S(1)}, bf16[2,192,384]{2,1,0:T(8,128)(2,1)}, u32[]{:S(2)}) copy-start(bf16[2,192,384]{2,1,0:T(8,128)(2,1)} %get-tuple-element.26) | copy-start | bytes 884740
  82.8 0.7 copy-start.1
  87.9 6.5 %copy-start.8 = (bf16[2,192,384]{2,1,0:T(8,128)(2,1)S(1)}, bf16[2,192,384]{2,1,0:T(8,128)(2,1)}, u32[]{:S(2)}) copy-start(bf16[2,192,384]{2,1,0:T(8,128)(2,1)} %get-tuple-element.27) | copy-start | bytes 884740
  87.9 7.3 %copy-start.11 = (bf16[64,384]{1,0:T(8,128)(2,1)S(1)}, bf16[64,384]{1,0:T(8,128)(2,1)}, u32[]{:S(2)}) copy-start(bf16[64,384]{1,0:T(8,128)(2,1)} %get-tuple-element.22) | copy-start | bytes 147460
  88.7 7.1 %collective-permute-start.5 = (f32[3,1536]{1,0:T(4,128)S(1)}, f32[3,1536]{1,0:T(4,128)S(1)}, u32[]{:S(2)}, u32[]{:S(2)}) collective-permute-start(f32[3,1536]{1,0:T(4,128)S(1)} %maximum_add_fusion), channel_id=1, source_target_pairs={{0,16},{16,0},{1,17},{17,1},{2,18},{18,2},{3,19},{19,3},{4,20},{20... | collective-permute-start | bytes 55304 | tf_op jit(solution)/shard_map/ppermute | solution.py:19

commit v7 on v6

--- a/solution.py
+++ b/solution.py
@@ -211,6 +211,8 @@
     pick = order[0, 0]
     section_offsets = lax.dynamic_index_in_dim(offsets[0], section_index, 0, keepdims=False)
     qg, kv, column_sums = kept_backward(kept_qkv[0, 0], regrouped, section_offsets[0], pick)
+    first_part, qg, kv, column_sums = lax.optimization_barrier((fetched[0], qg, kv, column_sums))
+    fetched = [first_part] + fetched[1:]
     held_parts = [
         held_backward(fetched[c], regrouped, section_offsets[1], pick, c) for c in range(chunks)
     ]

time: 96.9 us -> 89.9 us (0.928)
  waiting for transfers between devices: 30 us -> 20.6 us
  local copies, waits for them, and re-layouts: 14.2 us -> 16.5 us
    ppermute x6, waiting for transfers between devices: 25.7 us -> 16.3 us  [from_behind(): return lax.ppermute(value, axis, pairs)]
    dynamic_update_slice x4, local copies, waits for them, and re-layouts: 2.5 us -> 4.89 us  [body(): qg = lax.dynamic_update_slice(qg, part_q[None], (1, 0, c * width))]
    unnamed x33 -> x23, local copies, waits for them, and re-layouts: 3.6 us -> 3.55 us
  transfers between devices with their start and end apart: 7 -> 7, of which waited for: 4 -> 5; matrix products, arithmetic and copies ran while one was open for 14% -> 18% of each run, Pallas kernels for 25% -> 27%
where the time goes in v7:
time: 89.9 us; the launch traced here: 89.3 us
  Pallas kernels  28.4 us (32%)
  waiting for transfers between devices  20.6 us (23%)
  local copies, waits for them, and re-layouts  16.5 us (18%)
  starting transfers between devices  16.2 us (18%)
  other arithmetic  4.23 us (5%)
  between operations  3.34 us (4%)
    pallas_call x4, Pallas kernels, held_backward(): pl.pallas_call(held_kernel, out_shape=(jax.ShapeDtypeStruct((rows, width)...  17.6 us
    ppermute x6, waiting for transfers between devices, from_behind(): return lax.ppermute(value, axis, pairs)  16.3 us
    ppermute x6, starting transfers between devices, from_behind(): return lax.ppermute(value, axis, pairs)  12.7 us
    pallas_call x1, Pallas kernels, kept_backward(): pl.pallas_call(kept_kernel, out_shape=out_shape, grid_spec=grid_spec, cos...  10.9 us
    dynamic_update_slice x4, local copies, waits for them, and re-layouts, body(): qg = lax.dynamic_update_slice(qg, part_q[None], (1, 0, c * width))  4.89 us
    all_to_all x1, waiting for transfers between devices, body(): lax.all_to_all(split, 'tensor', split_axis=0, concat_axis=0, tiled=True)  4.27 us
    unnamed x23, local copies, waits for them, and re-layouts  3.55 us
    all_to_all x1, starting transfers between devices, body(): lax.all_to_all(split, 'tensor', split_axis=0, concat_axis=0, tiled=True)  3.46 us
  transfers between devices with their start and end apart: 7, of which 5 were waited for; matrix products, arithmetic and copies ran while one was open for 18% of the time, Pallas kernels for 27%

profile of v7, /device:TPU:0, one launch (start us, length us, event | category | flops | bytes accessed | tf_op | source)
XLA Modules:
  0.0 89.3 jit_solution(15699484539598979535)
XLA Ops:
  0.6 0.0 copy-start
  0.6 5.1 %collective-permute-start.1 = (bf16[2,16,6144]{2,1,0:T(8,128)(2,1)}, bf16[2,16,6144]{2,1,0:T(8,128)(2,1)S(1)}, u32[]{:S(2)}, u32[]{:S(2)}) collective-permute-start(bf16[2,16,6144]{2,1,0:T(8,128)(2,1)} %bitcast.60), channel_id=1, source_target_pairs={{0,12},{4,0},{8,4},{12,8},{1,13},{5,1},{9,5},{13,9},{2,14},{6,2},{... | collective-permute-start | bytes 1179656 | tf_op jit(solution)/shard_map/ppermute | solution.py:19
  5.7 0.8 constant_dynamic-slice_fusion
  6.6 0.5 slice.60
  8.4 1.1 %slice.59 = bf16[1,1,1,192,1536]{4,3,2,1,0:T(8,128)(2,1)S(1)} slice(bf16[1,1,3,192,1536]{4,3,2,1,0:T(8,128)(2,1)} %param.6), slice={[0:1], [0:1], [0:1], [0:192], [0:1536]} | slice | bytes 1179648 | tf_op jit(solution)/shard_map/slice | solution.py:196
  10.1 0.1 dynamic-slice_bitcast_fusion
  10.2 0.0 copy-done
  10.2 0.1 slice_bitcast_fusion.1
  10.4 0.8 pad_maximum_fusion
  11.2 0.0 collective-permute-start
  11.2 3.0 %collective-permute-start.2 = (bf16[448,384]{1,0:T(8,128)(2,1)S(1)}, bf16[448,384]{1,0:T(8,128)(2,1)S(1)}, u32[]{:S(2)}, u32[]{:S(2)}) collective-permute-start(bf16[448,384]{1,0:T(8,128)(2,1)S(1)} %pad_maximum_fusion.1), channel_id=1, source_target_pairs={{0,8},{4,12},{8,0},{12,4},{1,9},{5,13},{9,1},{13,5},{2,10},{6,14},... | collective-permute-start | bytes 1032200 | tf_op jit(solution)/shard_map/ppermute | solution.py:19
  14.2 0.1 collective-permute-start.3
  14.3 3.0 %collective-permute-start.4 = (bf16[448,384]{1,0:T(8,128)(2,1)S(1)}, bf16[448,384]{1,0:T(8,128)(2,1)S(1)}, u32[]{:S(2)}, u32[]{:S(2)}) collective-permute-start(bf16[448,384]{1,0:T(8,128)(2,1)S(1)} %pad_maximum_fusion.3), channel_id=1, source_target_pairs={{0,8},{4,12},{8,0},{12,4},{1,9},{5,13},{9,1},{13,5},{2,10},{6,14},... | collective-permute-start | bytes 1032200 | tf_op jit(solution)/shard_map/ppermute | solution.py:19
  18.0 0.0 collective-permute-done.1
  18.0 0.3 reshape.50
  18.3 0.8 copy.12
  19.1 3.5 %all-to-all-start = ((bf16[4,2,16,1536]{3,2,1,0:T(8,128)(2,1)}), bf16[4,2,16,1536]{3,2,1,0:T(8,128)(2,1)S(1)}, u32[]{:S(2)}, u32[]{:S(2)}) async-start(bf16[4,2,16,1536]{3,2,1,0:T(8,128)(2,1)} %copy.12), calls=%async_computation | async-start | bytes 786432 | tf_op jit(solution)/shard_map/all_to_all | solution.py:209
  22.5 0.6 fusion.1
  23.1 1.2 %pad_add_fusion.1.meta_ref = s32[2]{0:T(128)} fusion(s32[1]{0:T(128)} %bitcast.14, s32[1]{0:T(128)} %bitcast.13), kind=kLoop, calls=%fused_computation.26 | loop fusion | flops 2 | bytes 16 | tf_op jit(solution)/shard_map/stack | solution.py:163
  24.3 1.3 %pad_add_fusion.meta_ref = s32[2]{0:T(128)} fusion(s32[1]{0:T(128)} %bitcast.49, s32[1]{0:T(128)} %bitcast.5), kind=kLoop, calls=%fused_computation.25 | loop fusion | flops 2 | bytes 16 | tf_op jit(solution)/shard_map/stack | solution.py:135
  25.7 4.3 %all-to-all-done = bf16[4,2,16,1536]{3,2,1,0:T(8,128)(2,1)S(1)} async-done(((bf16[4,2,16,1536]{3,2,1,0:T(8,128)(2,1)}), bf16[4,2,16,1536]{3,2,1,0:T(8,128)(2,1)S(1)}, u32[]{:S(2)}, u32[]{:S(2)}) %all-to-all-start) | async-done | bytes 393248 | tf_op jit(solution)/shard_map/all_to_all | solution.py:209
  29.9 0.8 copy.13
  30.7 10.9 %kept_backward.1 = (bf16[2,64,1536]{2,1,0:T(8,128)(2,1)}, bf16[2,2,192,1536]{3,2,1,0:T(8,128)(2,1)}, f32[3,1536]{1,0:T(4,128)}) custom-call(s32[2]{0:T(128)} %pad_add_fusion.meta_ref, bf16[3,192,1536]{2,1,0:T(8,128)(2,1)} %bitcast.56, bf16[2,64,1536]{2,1,0:T(8,128)(2,1)} %bitcast.50), custom_call_target="tpu_custom_call" | custom-call | flops 226492416 | bytes 2949120 | tf_op jit(solution)/shard_map/kept_backward/pallas_call | solution.py:136
  41.6 0.0 copy-start.10
  41.6 10.3 %collective-permute-done.x_ref = bf16[448,384]{1,0:T(8,128)(2,1)S(1)} collective-permute-done((bf16[448,384]{1,0:T(8,128)(2,1)}, bf16[448,384]{1,0:T(8,128)(2,1)S(1)}, u32[]{:S(2)}, u32[]{:S(2)}) %collective-permute-start) | collective-permute-done | bytes 344096 | tf_op jit(solution)/shard_map/ppermute | solution.py:19
  51.9 0.0 copy-start.4
  51.9 0.7 copy-done.4
  52.6 4.4 %held_backward.4 = (bf16[64,384]{1,0:T(8,128)(2,1)}, bf16[2,192,384]{2,1,0:T(8,128)(2,1)}, f32[3,384]{1,0:T(4,128)}) custom-call(s32[2]{0:T(128)} %pad_add_fusion.1.meta_ref, bf16[448,384]{1,0:T(8,128)(2,1)} %copy-done.4, bf16[2,64,1536]{2,1,0:T(8,128)(2,1)} %bitcast.51), custom_call_target="tpu_custom_call" | custom-call | flops 56623104 | bytes 737280 | tf_op jit(solution)/shard_map/held_backward/pallas_call | solution.py:164
  57.0 0.0 copy-start.5
  57.0 2.3 %collective-permute-done.2.x_ref = bf16[448,384]{1,0:T(8,128)(2,1)S(1)} collective-permute-done((bf16[448,384]{1,0:T(8,128)(2,1)S(1)}, bf16[448,384]{1,0:T(8,128)(2,1)S(1)}, u32[]{:S(2)}, u32[]{:S(2)}) %collective-permute-start.2) | collective-permute-done | bytes 344096 | tf_op jit(solution)/shard_map/ppermute | solution.py:19
  59.2 0.0 copy-start.2
  59.2 0.7 copy-done.2
  60.0 4.4 %held_backward.5 = (bf16[64,384]{1,0:T(8,128)(2,1)}, bf16[2,192,384]{2,1,0:T(8,128)(2,1)}, f32[3,384]{1,0:T(4,128)}) custom-call(s32[2]{0:T(128)} %pad_add_fusion.1.meta_ref, bf16[448,384]{1,0:T(8,128)(2,1)} %copy-done.2, bf16[2,64,1536]{2,1,0:T(8,128)(2,1)} %bitcast.52), custom_call_target="tpu_custom_call" | custom-call | flops 56623104 | bytes 737280 | tf_op jit(solution)/shard_map/held_backward/pallas_call | solution.py:164
  64.3 0.0 copy-start.6
  64.3 2.3 %collective-permute-done.3.x_ref = bf16[448,384]{1,0:T(8,128)(2,1)S(1)} collective-permute-done((bf16[448,384]{1,0:T(8,128)(2,1)S(1)}, bf16[448,384]{1,0:T(8,128)(2,1)S(1)}, u32[]{:S(2)}, u32[]{:S(2)}) %collective-permute-start.3) | collective-permute-done | bytes 344096 | tf_op jit(solution)/shard_map/ppermute | solution.py:19
  66.6 0.0 copy-start.1
  66.6 0.7 copy-done.1
  67.3 4.4 %held_backward.6 = (bf16[64,384]{1,0:T(8,128)(2,1)}, bf16[2,192,384]{2,1,0:T(8,128)(2,1)}, f32[3,384]{1,0:T(4,128)}) custom-call(s32[2]{0:T(128)} %pad_add_fusion.1.meta_ref, bf16[448,384]{1,0:T(8,128)(2,1)} %copy-done.1, bf16[2,64,1536]{2,1,0:T(8,128)(2,1)} %bitcast.53), custom_call_target="tpu_custom_call" | custom-call | flops 56623104 | bytes 737280 | tf_op jit(solution)/shard_map/held_backward/pallas_call | solution.py:164
  71.7 0.0 copy-start.7
  71.7 1.5 %collective-permute-done.4.x_ref = bf16[448,384]{1,0:T(8,128)(2,1)S(1)} collective-permute-done((bf16[448,384]{1,0:T(8,128)(2,1)S(1)}, bf16[448,384]{1,0:T(8,128)(2,1)S(1)}, u32[]{:S(2)}, u32[]{:S(2)}) %collective-permute-start.4) | collective-permute-done | bytes 344096 | tf_op jit(solution)/shard_map/ppermute | solution.py:19
  73.2 0.0 copy-start.3
  73.2 0.7 copy-done.3
  74.0 4.4 %held_backward.7 = (bf16[64,384]{1,0:T(8,128)(2,1)}, bf16[2,192,384]{2,1,0:T(8,128)(2,1)}, f32[3,384]{1,0:T(4,128)}) custom-call(s32[2]{0:T(128)} %pad_add_fusion.1.meta_ref, bf16[448,384]{1,0:T(8,128)(2,1)} %copy-done.3, bf16[2,64,1536]{2,1,0:T(8,128)(2,1)} %bitcast.54), custom_call_target="tpu_custom_call" | custom-call | flops 56623104 | bytes 737280 | tf_op jit(solution)/shard_map/held_backward/pallas_call | solution.py:164
  78.4 0.0 copy-start.8
  78.4 0.0 copy-start.9
  78.4 0.0 copy-done.10
  78.4 0.8 maximum_add_fusion
  79.2 1.6 %collective-permute-start.5 = (f32[3,1536]{1,0:T(4,128)S(1)}, f32[3,1536]{1,0:T(4,128)S(1)}, u32[]{:S(2)}, u32[]{:S(2)}) collective-permute-start(f32[3,1536]{1,0:T(4,128)S(1)} %maximum_add_fusion), channel_id=1, source_target_pairs={{0,16},{16,0},{1,17},{17,1},{2,18},{18,2},{3,19},{19,3},{4,20},{20... | collective-permute-start | bytes 55304 | tf_op jit(solution)/shard_map/ppermute | solution.py:19
  80.8 1.4 %bitcast_dynamic-update-slice_fusion.7 = bf16[1,1,2,64,1536]{4,3,2,1,0:T(8,128)(2,1)} fusion(bf16[1,1,2,64,1536]{4,3,2,1,0:T(8,128)(2,1)} %bitcast.61, bf16[64,384]{1,0:T(8,128)(2,1)} %get-tuple-element.27), kind=kLoop, calls=%fused_computation.20 | loop fusion | bytes 98304 | tf_op jit(solution)/shard_map/dynamic_update_slice | solution.py:220
  82.2 1.4 %bitcast_dynamic-update-slice_fusion.6 = bf16[1,1,2,64,1536]{4,3,2,1,0:T(8,128)(2,1)} fusion(bf16[1,1,2,64,1536]{4,3,2,1,0:T(8,128)(2,1)} %bitcast_dynamic-update-slice_fusion.7, bf16[64,384]{1,0:T(8,128)(2,1)} %get-tuple-element.28), kind=kLoop, calls=%fused_computation.19 | loop fusion | bytes 98304 | tf_op jit(solution)/shard_map/dynamic_update_slice | solution.py:220
  83.6 1.4 %bitcast_dynamic-update-slice_fusion.5 = bf16[1,1,2,64,1536]{4,3,2,1,0:T(8,128)(2,1)} fusion(bf16[1,1,2,64,1536]{4,3,2,1,0:T(8,128)(2,1)} %bitcast_dynamic-update-slice_fusion.6, bf16[64,384]{1,0:T(8,128)(2,1)} %get-tuple-element.29), kind=kLoop, calls=%fused_computation.18 | loop fusion | bytes 98304 | tf_op jit(solution)/shard_map/dynamic_update_slice | solution.py:220
  85.0 0.0 copy-done.5
  85.0 0.7 bitcast_dynamic-update-slice_fusion.3
  85.8 0.0 copy-done.6
  85.8 0.7 bitcast_dynamic-update-slice_fusion.2
  86.5 0.0 copy-done.7
  86.5 0.7 bitcast_dynamic-update-slice_fusion.1
  87.3 0.0 copy-done.8
  87.3 0.7 bitcast_dynamic-update-slice_fusion
  88.0 0.0 copy-done.9
  88.0 0.6 bitcast_dynamic-update-slice_fusion.4
  88.7 0.0 collective-permute-done.5
  88.7 0.6 copy.14
  (5 shorter events, 0.1 us)
Async XLA Ops:
  0.6 9.6 %copy-start = (bf16[1,1,3,192,1536]{4,3,2,1,0:T(8,128)(2,1)S(1)}, bf16[1,1,3,192,1536]{4,3,2,1,0:T(8,128)(2,1)}, u32[]{:S(2)}) copy-start(bf16[1,1,3,192,1536]{4,3,2,1,0:T(8,128)(2,1)} %param.6) | copy-start | bytes 5308420
  0.6 17.3 %collective-permute-start.1 = (bf16[2,16,6144]{2,1,0:T(8,128)(2,1)}, bf16[2,16,6144]{2,1,0:T(8,128)(2,1)S(1)}, u32[]{:S(2)}, u32[]{:S(2)}) collective-permute-start(bf16[2,16,6144]{2,1,0:T(8,128)(2,1)} %bitcast.60), channel_id=1, source_target_pairs={{0,12},{4,0},{8,4},{12,8},{1,13},{5,1},{9,5},{13,9},{2,14},{6,2},{... | collective-permute-start | bytes 1179656 | tf_op jit(solution)/shard_map/ppermute | solution.py:19
  11.2 40.7 %collective-permute-start = (bf16[448,384]{1,0:T(8,128)(2,1)}, bf16[448,384]{1,0:T(8,128)(2,1)S(1)}, u32[]{:S(2)}, u32[]{:S(2)}) collective-permute-start(bf16[448,384]{1,0:T(8,128)(2,1)} %pad_maximum_fusion), channel_id=1, source_target_pairs={{0,8},{4,12},{8,0},{12,4},{1,9},{5,13},{9,1},{13,5},{2,10},{6,14},... | collective-permute-start | bytes 1032200 | tf_op jit(solution)/shard_map/ppermute | solution.py:19
  11.2 48.0 %collective-permute-start.2 = (bf16[448,384]{1,0:T(8,128)(2,1)S(1)}, bf16[448,384]{1,0:T(8,128)(2,1)S(1)}, u32[]{:S(2)}, u32[]{:S(2)}) collective-permute-start(bf16[448,384]{1,0:T(8,128)(2,1)S(1)} %pad_maximum_fusion.1), channel_id=1, source_target_pairs={{0,8},{4,12},{8,0},{12,4},{1,9},{5,13},{9,1},{13,5},{2,10},{6,14},... | collective-permute-start | bytes 1032200 | tf_op jit(solution)/shard_map/ppermute | solution.py:19
  14.2 52.4 %collective-permute-start.3 = (bf16[448,384]{1,0:T(8,128)(2,1)S(1)}, bf16[448,384]{1,0:T(8,128)(2,1)S(1)}, u32[]{:S(2)}, u32[]{:S(2)}) collective-permute-start(bf16[448,384]{1,0:T(8,128)(2,1)S(1)} %pad_maximum_fusion.2), channel_id=1, source_target_pairs={{0,8},{4,12},{8,0},{12,4},{1,9},{5,13},{9,1},{13,5},{2,10},{6,14},... | collective-permute-start | bytes 1032200 | tf_op jit(solution)/shard_map/ppermute | solution.py:19
  14.3 58.9 %collective-permute-start.4 = (bf16[448,384]{1,0:T(8,128)(2,1)S(1)}, bf16[448,384]{1,0:T(8,128)(2,1)S(1)}, u32[]{:S(2)}, u32[]{:S(2)}) collective-permute-start(bf16[448,384]{1,0:T(8,128)(2,1)S(1)} %pad_maximum_fusion.3), channel_id=1, source_target_pairs={{0,8},{4,12},{8,0},{12,4},{1,9},{5,13},{9,1},{13,5},{2,10},{6,14},... | collective-permute-start | bytes 1032200 | tf_op jit(solution)/shard_map/ppermute | solution.py:19
  19.1 10.9 %all-to-all-start = ((bf16[4,2,16,1536]{3,2,1,0:T(8,128)(2,1)}), bf16[4,2,16,1536]{3,2,1,0:T(8,128)(2,1)S(1)}, u32[]{:S(2)}, u32[]{:S(2)}) async-start(bf16[4,2,16,1536]{3,2,1,0:T(8,128)(2,1)} %copy.12), calls=%async_computation | async-start | bytes 786432 | tf_op jit(solution)/shard_map/all_to_all | solution.py:209
  41.6 36.8 %copy-start.10 = (f32[3,1536]{1,0:T(4,128)S(1)}, f32[3,1536]{1,0:T(4,128)}, u32[]{:S(2)}) copy-start(f32[3,1536]{1,0:T(4,128)} %get-tuple-element.36) | copy-start | bytes 55300
  51.9 0.7 copy-start.4
  57.0 28.1 %copy-start.5 = (bf16[2,192,384]{2,1,0:T(8,128)(2,1)S(1)}, bf16[2,192,384]{2,1,0:T(8,128)(2,1)}, u32[]{:S(2)}) copy-start(bf16[2,192,384]{2,1,0:T(8,128)(2,1)} %get-tuple-element.32) | copy-start | bytes 884740
  59.2 0.7 copy-start.2
  64.3 21.4 %copy-start.6 = (bf16[2,192,384]{2,1,0:T(8,128)(2,1)S(1)}, bf16[2,192,384]{2,1,0:T(8,128)(2,1)}, u32[]{:S(2)}) copy-start(bf16[2,192,384]{2,1,0:T(8,128)(2,1)} %get-tuple-element.33) | copy-start | bytes 884740
  66.6 0.7 copy-start.1
  71.7 14.8 %copy-start.7 = (bf16[2,192,384]{2,1,0:T(8,128)(2,1)S(1)}, bf16[2,192,384]{2,1,0:T(8,128)(2,1)}, u32[]{:S(2)}) copy-start(bf16[2,192,384]{2,1,0:T(8,128)(2,1)} %get-tuple-element.34) | copy-start | bytes 884740
  73.2 0.7 copy-start.3
  78.4 8.9 %copy-start.8 = (bf16[2,192,384]{2,1,0:T(8,128)(2,1)S(1)}, bf16[2,192,384]{2,1,0:T(8,128)(2,1)}, u32[]{:S(2)}) copy-start(bf16[2,192,384]{2,1,0:T(8,128)(2,1)} %get-tuple-element.35) | copy-start | bytes 884740
  78.4 9.7 %copy-start.9 = (bf16[64,384]{1,0:T(8,128)(2,1)S(1)}, bf16[64,384]{1,0:T(8,128)(2,1)}, u32[]{:S(2)}) copy-start(bf16[64,384]{1,0:T(8,128)(2,1)} %get-tuple-element.30) | copy-start | bytes 147460
  79.2 9.5 %collective-permute-start.5 = (f32[3,1536]{1,0:T(4,128)S(1)}, f32[3,1536]{1,0:T(4,128)S(1)}, u32[]{:S(2)}, u32[]{:S(2)}) collective-permute-start(f32[3,1536]{1,0:T(4,128)S(1)} %maximum_add_fusion), channel_id=1, source_target_pairs={{0,16},{16,0},{1,17},{17,1},{2,18},{18,2},{3,19},{19,3},{4,20},{20... | collective-permute-start | bytes 55304 | tf_op jit(solution)/shard_map/ppermute | solution.py:19

commit v8 on v7

--- a/solution.py
+++ b/solution.py
@@ -1,3 +1,4 @@
+import functools
 import math
 
 import jax
@@ -61,18 +62,19 @@
         return self.fn(cols)
 
 
-def store_into(qg_ref, kv_ref, sum_ref, add):
+def store_into(qg_ref, kv_ref, sum_ref, add, shift=0):
     f32 = jnp.float32
 
     def store(cols, dq, dk, dv):
-        qg_ref[:, cols] = dq
-        kv_ref[0, :, cols] = dk
-        kv_ref[1, :, cols] = dv
+        out = pl.ds(pl.multiple_of(cols.start + shift, HD), HD) if shift else cols
+        qg_ref[:, out] = dq
+        kv_ref[0, :, out] = dk
+        kv_ref[1, :, out] = dv
         for row, value in enumerate((dq, dk, dv)):
             total = jnp.sum(value.astype(f32), axis=0, keepdims=True)
             if add:
-                total = sum_ref[pl.ds(row, 1), cols] + total
-            sum_ref[pl.ds(row, 1), cols] = total
+                total = sum_ref[pl.ds(row, 1), out] + total
+            sum_ref[pl.ds(row, 1), out] = total
 
     return store
 
@@ -174,6 +176,64 @@
     )(meta, part, grads)
 
 
+def held_last_kernel(count, meta_ref, x_ref, g_ref, *refs):
+    prev_q, prev_kv = refs[:count], refs[count:2 * count]
+    qg_ref, kv_ref, sum_ref = refs[2 * count + 2:]
+    offset = meta_ref[0]
+    rows, width = g_ref.shape
+    keys = (x_ref.shape[0] - rows) // 2
+    for c in range(count):
+        cols = pl.ds(c * width, width)
+        qg_ref[:, cols] = prev_q[c][...]
+        kv_ref[:, :, cols] = prev_kv[c][...]
+    load = Loader(
+        lambda cols: (x_ref[pl.ds(0, rows), cols], x_ref[pl.ds(rows, keys), cols],
+                      x_ref[pl.ds(rows + keys, keys), cols], g_ref[:, cols]),
+        rows, keys, width // HD,
+    )
+    head_loop(offset, load, store_into(qg_ref, kv_ref, sum_ref, add=False, shift=count * width))
+
+
+def held_last_backward(part, grads, offset, pick, chunk, earlier, qg, kv):
+    rows = grads.shape[1]
+    width = part.shape[1]
+    keys = (part.shape[0] - rows) // 2
+    feats = qg.shape[-1]
+    count = len(earlier)
+    vmem_q = pl.BlockSpec((rows, width), lambda i, m: (0, 0))
+    vmem_kv = pl.BlockSpec((2, keys, width), lambda i, m: (0, 0, 0))
+    grid_spec = pltpu.PrefetchScalarGridSpec(
+        num_scalar_prefetch=1,
+        grid=(1,),
+        in_specs=[
+            pl.BlockSpec((part.shape[0], width), lambda i, m: (0, 0)),
+            pl.BlockSpec((None, rows, width), lambda i, m: (m[1], 0, chunk)),
+        ] + [vmem_q] * count + [vmem_kv] * count + [
+            pl.BlockSpec(memory_space=pl.ANY),
+            pl.BlockSpec(memory_space=pl.ANY),
+        ],
+        out_specs=(
+            pl.BlockSpec((None, rows, feats), lambda i, m: (1, 0, 0)),
+            pl.BlockSpec((None, 2, keys, feats), lambda i, m: (1, 0, 0, 0)),
+            pl.BlockSpec((3, feats), lambda i, m: (0, 0)),
+        ),
+    )
+    meta = jnp.stack([offset, 1 - pick]).astype(jnp.int32)
+    first_alias = 2 + 2 * count + 1
+    return pl.pallas_call(
+        functools.partial(held_last_kernel, count),
+        out_shape=(
+            jax.ShapeDtypeStruct(qg.shape, qg.dtype),
+            jax.ShapeDtypeStruct(kv.shape, kv.dtype),
+            jax.ShapeDtypeStruct((3, feats), jnp.float32),
+        ),
+        grid_spec=grid_spec,
+        input_output_aliases={first_alias: 0, first_alias + 1: 1},
+        cost_estimate=kernel_cost(rows, keys, width),
+        name="held_last_backward",
+    )(meta, part, grads, *[e[0] for e in earlier], *[e[1] for e in earlier], qg, kv)
+
+
 def chunk_count(heads):
     for count in range(min(MAX_CHUNKS, heads), 0, -1):
         if heads % count == 0:
@@ -214,12 +274,13 @@
     first_part, qg, kv, column_sums = lax.optimization_barrier((fetched[0], qg, kv, column_sums))
     fetched = [first_part] + fetched[1:]
     held_parts = [
-        held_backward(fetched[c], regrouped, section_offsets[1], pick, c) for c in range(chunks)
+        held_backward(fetched[c], regrouped, section_offsets[1], pick, c) for c in range(chunks - 1)
     ]
-    for c, (part_q, part_kv, _) in enumerate(held_parts):
-        qg = lax.dynamic_update_slice(qg, part_q[None], (1, 0, c * width))
-        kv = lax.dynamic_update_slice(kv, part_kv[None], (1, 0, 0, c * width))
-    column_sums = column_sums + jnp.concatenate([part[2] for part in held_parts], axis=1)
+    qg, kv, last_sums = held_last_backward(
+        fetched[-1], regrouped, section_offsets[1], pick, chunks - 1, held_parts, qg, kv
+    )
+    last_sums = last_sums[:, (chunks - 1) * width:]
+    column_sums = column_sums + jnp.concatenate([part[2] for part in held_parts] + [last_sums], axis=1)
     query_grad = qg
     key_value_grad = kv
     if lax.axis_size("dp") == 2:

time: 89.9 us -> 89.4 us (level)
  waiting for transfers between devices: 20.6 us -> 28.7 us
  local copies, waits for them, and re-layouts: 16.5 us -> 8.62 us
  other arithmetic: 4.23 us -> 2.6 us
  Pallas kernels: 28.4 us -> 29.3 us
    ppermute x6, waiting for transfers between devices: 16.3 us -> 24.3 us  [from_behind(): return lax.ppermute(value, axis, pairs)]
    dynamic_update_slice x8 -> x0, local copies, waits for them, and re-layouts: 7.87 us -> none  [the longest x4 4.89 us: body(): qg = lax.dynamic_update_slice(qg, part_q[None], (1, 0, c * width))]
    pallas_call x0 -> x1, Pallas kernels: none -> 5.24 us  [held_last_backward(): pl.pallas_call(functools.partial(held_last_kernel, count), out_shape=(jax...]
    pallas_call x4 -> x3, Pallas kernels: 17.6 us -> 13.2 us  [held_backward(): pl.pallas_call(held_kernel, out_shape=(jax.ShapeDtypeStruct((rows, width)...]
    unnamed x23 -> x17, local copies, waits for them, and re-layouts: 3.55 us -> 2.86 us
  transfers between devices with their start and end apart: 7 -> 7, of which waited for: 5 -> 5; matrix products, arithmetic and copies ran while one was open for 18% -> 9% of each run, Pallas kernels for 27% -> 27%
where the time goes in v8:
time: 89.4 us; the launch traced here: 88.9 us
  Pallas kernels  29.3 us (33%)
  waiting for transfers between devices  28.7 us (32%)
  starting transfers between devices  16.2 us (18%)
  local copies, waits for them, and re-layouts  8.62 us (10%)
  between operations  3.38 us (4%)
  other arithmetic  2.6 us (3%)
    ppermute x6, waiting for transfers between devices, from_behind(): return lax.ppermute(value, axis, pairs)  24.3 us
    pallas_call x3, Pallas kernels, held_backward(): pl.pallas_call(held_kernel, out_shape=(jax.ShapeDtypeStruct((rows, width)...  13.2 us
    ppermute x6, starting transfers between devices, from_behind(): return lax.ppermute(value, axis, pairs)  12.8 us
    pallas_call x1, Pallas kernels, kept_backward(): pl.pallas_call(kept_kernel, out_shape=out_shape, grid_spec=grid_spec, cos...  10.9 us
    pallas_call x1, Pallas kernels, held_last_backward(): pl.pallas_call(functools.partial(held_last_kernel, count), out_shape=(jax...  5.24 us
    all_to_all x1, waiting for transfers between devices, body(): lax.all_to_all(split, 'tensor', split_axis=0, concat_axis=0, tiled=True)  4.42 us
    all_to_all x1, starting transfers between devices, body(): lax.all_to_all(split, 'tensor', split_axis=0, concat_axis=0, tiled=True)  3.46 us
    unnamed x17, local copies, waits for them, and re-layouts  2.86 us
  transfers between devices with their start and end apart: 7, of which 5 were waited for; matrix products, arithmetic and copies ran while one was open for 9% of the time, Pallas kernels for 27%

profile of v8, /device:TPU:0, one launch (start us, length us, event | category | flops | bytes accessed | tf_op | source)
XLA Modules:
  0.0 88.9 jit_solution(2292069967537572768)
XLA Ops:
  0.6 0.0 copy-start
  0.6 5.1 %collective-permute-start.1 = (bf16[2,16,6144]{2,1,0:T(8,128)(2,1)}, bf16[2,16,6144]{2,1,0:T(8,128)(2,1)S(1)}, u32[]{:S(2)}, u32[]{:S(2)}) collective-permute-start(bf16[2,16,6144]{2,1,0:T(8,128)(2,1)} %bitcast.45), channel_id=1, source_target_pairs={{0,12},{4,0},{8,4},{12,8},{1,13},{5,1},{9,5},{13,9},{2,14},{6,2},{... | collective-permute-start | bytes 1179656 | tf_op jit(solution)/shard_map/ppermute | solution.py:20
  5.7 0.8 constant_dynamic-slice_fusion
  6.6 0.5 slice.65
  8.4 1.1 %slice.64 = bf16[1,1,1,192,1536]{4,3,2,1,0:T(8,128)(2,1)S(1)} slice(bf16[1,1,3,192,1536]{4,3,2,1,0:T(8,128)(2,1)} %param.6), slice={[0:1], [0:1], [0:1], [0:192], [0:1536]} | slice | bytes 1179648 | tf_op jit(solution)/shard_map/slice | solution.py:256
  10.1 0.1 dynamic-slice_bitcast_fusion
  10.2 0.0 copy-done
  10.2 0.1 slice_bitcast_fusion.1
  10.4 0.1 collective-permute-start
  10.6 3.0 %collective-permute-start.2 = (bf16[448,384]{1,0:T(8,128)(2,1)S(1)}, bf16[448,384]{1,0:T(8,128)(2,1)S(1)}, u32[]{:S(2)}, u32[]{:S(2)}) collective-permute-start(bf16[448,384]{1,0:T(8,128)(2,1)S(1)} %pad_maximum_fusion.1), channel_id=1, source_target_pairs={{0,8},{4,12},{8,0},{12,4},{1,9},{5,13},{9,1},{13,5},{2,10},{6,14},... | collective-permute-start | bytes 1032200 | tf_op jit(solution)/shard_map/ppermute | solution.py:20
  13.6 0.1 collective-permute-start.3
  13.7 3.0 %collective-permute-start.4 = (bf16[448,384]{1,0:T(8,128)(2,1)S(1)}, bf16[448,384]{1,0:T(8,128)(2,1)S(1)}, u32[]{:S(2)}, u32[]{:S(2)}) collective-permute-start(bf16[448,384]{1,0:T(8,128)(2,1)S(1)} %pad_maximum_fusion.3), channel_id=1, source_target_pairs={{0,8},{4,12},{8,0},{12,4},{1,9},{5,13},{9,1},{13,5},{2,10},{6,14},... | collective-permute-start | bytes 1032200 | tf_op jit(solution)/shard_map/ppermute | solution.py:20
  17.3 0.0 collective-permute-done.1
  17.3 0.3 reshape.26
  17.6 0.8 copy.14
  18.4 3.5 %all-to-all-start = ((bf16[4,2,16,1536]{3,2,1,0:T(8,128)(2,1)}), bf16[4,2,16,1536]{3,2,1,0:T(8,128)(2,1)S(1)}, u32[]{:S(2)}, u32[]{:S(2)}) async-start(bf16[4,2,16,1536]{3,2,1,0:T(8,128)(2,1)} %copy.14), calls=%async_computation | async-start | bytes 786432 | tf_op jit(solution)/shard_map/all_to_all | solution.py:269
  21.9 0.5 fusion.1
  22.4 1.2 %pad_add_fusion.1.meta_ref = s32[2]{0:T(128)} fusion(s32[1]{0:T(128)} %bitcast.33, s32[1]{0:T(128)} %bitcast.13), kind=kLoop, calls=%fused_computation.18 | loop fusion | flops 2 | bytes 16 | tf_op jit(solution)/shard_map/stack | solution.py:137
  23.7 1.2 %pad_add_fusion.meta_ref = s32[2]{0:T(128)} fusion(s32[1]{0:T(128)} %bitcast.1, s32[1]{0:T(128)} %bitcast), kind=kLoop, calls=%fused_computation.17 | loop fusion | flops 2 | bytes 16 | tf_op jit(solution)/shard_map/stack | solution.py:221
  24.9 4.4 %all-to-all-done = bf16[4,2,16,1536]{3,2,1,0:T(8,128)(2,1)S(1)} async-done(((bf16[4,2,16,1536]{3,2,1,0:T(8,128)(2,1)}), bf16[4,2,16,1536]{3,2,1,0:T(8,128)(2,1)S(1)}, u32[]{:S(2)}, u32[]{:S(2)}) %all-to-all-start) | async-done | bytes 393248 | tf_op jit(solution)/shard_map/all_to_all | solution.py:269
  29.3 0.8 copy.15
  30.1 10.9 %kept_backward.1 = (bf16[2,64,1536]{2,1,0:T(8,128)(2,1)}, bf16[2,2,192,1536]{3,2,1,0:T(8,128)(2,1)}, f32[3,1536]{1,0:T(4,128)}) custom-call(s32[2]{0:T(128)} %pad_add_fusion.1.meta_ref, bf16[3,192,1536]{2,1,0:T(8,128)(2,1)} %bitcast.41, bf16[2,64,1536]{2,1,0:T(8,128)(2,1)} %bitcast.34), custom_call_target="tpu_custom_call" | custom-call | flops 226492416 | bytes 2949120 | tf_op jit(solution)/shard_map/kept_backward/pallas_call | solution.py:138
  41.0 18.1 %collective-permute-done.2.x_ref = bf16[448,384]{1,0:T(8,128)(2,1)S(1)} collective-permute-done((bf16[448,384]{1,0:T(8,128)(2,1)S(1)}, bf16[448,384]{1,0:T(8,128)(2,1)S(1)}, u32[]{:S(2)}, u32[]{:S(2)}) %collective-permute-start.2) | collective-permute-done | bytes 344096 | tf_op jit(solution)/shard_map/ppermute | solution.py:20
  59.1 0.0 copy-start.2
  59.1 0.7 copy-done.2
  59.8 4.4 %held_backward.3 = (bf16[64,384]{1,0:T(8,128)(2,1)}, bf16[2,192,384]{2,1,0:T(8,128)(2,1)}, f32[3,384]{1,0:T(4,128)}) custom-call(s32[2]{0:T(128)} %pad_add_fusion.meta_ref, bf16[448,384]{1,0:T(8,128)(2,1)} %copy-done.2, bf16[2,64,1536]{2,1,0:T(8,128)(2,1)} %bitcast.35), custom_call_target="tpu_custom_call" | custom-call | flops 56623104 | bytes 737280 | tf_op jit(solution)/shard_map/held_backward/pallas_call | solution.py:166
  64.2 2.3 %collective-permute-done.3.x_ref = bf16[448,384]{1,0:T(8,128)(2,1)S(1)} collective-permute-done((bf16[448,384]{1,0:T(8,128)(2,1)S(1)}, bf16[448,384]{1,0:T(8,128)(2,1)S(1)}, u32[]{:S(2)}, u32[]{:S(2)}) %collective-permute-start.3) | collective-permute-done | bytes 344096 | tf_op jit(solution)/shard_map/ppermute | solution.py:20
  66.4 0.0 copy-start.1
  66.4 0.7 copy-done.1
  67.2 4.4 %held_backward.4 = (bf16[64,384]{1,0:T(8,128)(2,1)}, bf16[2,192,384]{2,1,0:T(8,128)(2,1)}, f32[3,384]{1,0:T(4,128)}) custom-call(s32[2]{0:T(128)} %pad_add_fusion.meta_ref, bf16[448,384]{1,0:T(8,128)(2,1)} %copy-done.1, bf16[2,64,1536]{2,1,0:T(8,128)(2,1)} %bitcast.36), custom_call_target="tpu_custom_call" | custom-call | flops 56623104 | bytes 737280 | tf_op jit(solution)/shard_map/held_backward/pallas_call | solution.py:166
  71.6 1.6 %collective-permute-done.4.x_ref = bf16[448,384]{1,0:T(8,128)(2,1)S(1)} collective-permute-done((bf16[448,384]{1,0:T(8,128)(2,1)S(1)}, bf16[448,384]{1,0:T(8,128)(2,1)S(1)}, u32[]{:S(2)}, u32[]{:S(2)}) %collective-permute-start.4) | collective-permute-done | bytes 344096 | tf_op jit(solution)/shard_map/ppermute | solution.py:20
  73.2 0.0 copy-start.3
  73.2 0.7 copy-done.3
  73.9 4.4 %held_backward.5 = (bf16[64,384]{1,0:T(8,128)(2,1)}, bf16[2,192,384]{2,1,0:T(8,128)(2,1)}, f32[3,384]{1,0:T(4,128)}) custom-call(s32[2]{0:T(128)} %pad_add_fusion.meta_ref, bf16[448,384]{1,0:T(8,128)(2,1)} %copy-done.3, bf16[2,64,1536]{2,1,0:T(8,128)(2,1)} %bitcast.37), custom_call_target="tpu_custom_call" | custom-call | flops 56623104 | bytes 737280 | tf_op jit(solution)/shard_map/held_backward/pallas_call | solution.py:166
  78.4 0.0 collective-permute-done.x_ref
  78.4 0.0 copy-start.4
  78.4 0.0 copy-start.5
  78.4 0.0 copy-start.6
  78.4 0.0 copy-start.7
  78.4 5.2 %held_last_backward.1 = (bf16[2,64,1536]{2,1,0:T(8,128)(2,1)}, bf16[2,2,192,1536]{3,2,1,0:T(8,128)(2,1)}, f32[3,1536]{1,0:T(4,128)}) custom-call(s32[2]{0:T(128)} %pad_add_fusion.meta_ref, bf16[448,384]{1,0:T(8,128)(2,1)} %collective-permute-done.x_ref, bf16[2,64,1536]{2,1,0:T(8,128)(2,1)} %bitcast.38, ...), custom_call_target="tpu_custom_call", output_to_operand_aliasing={{0}: (9, {}), {1}: (10, {})} | custom-call | flops 56623104 | bytes 737280 | tf_op jit(solution)/shard_map/held_last_backward/pallas_call | solution.py:223
  83.6 0.7 slice.80
  84.3 0.0 copy-done.4
  84.3 0.0 copy-done.5
  84.3 0.0 copy-done.6
  84.3 0.0 copy-done.7
  84.4 1.6 %collective-permute-start.5 = (f32[3,1536]{1,0:T(4,128)S(1)}, f32[3,1536]{1,0:T(4,128)S(1)}, u32[]{:S(2)}, u32[]{:S(2)}) collective-permute-start(f32[3,1536]{1,0:T(4,128)S(1)} %maximum_add_fusion), channel_id=1, source_target_pairs={{0,16},{16,0},{1,17},{17,1},{2,18},{18,2},{3,19},{19,3},{4,20},{20... | collective-permute-start | bytes 55304 | tf_op jit(solution)/shard_map/ppermute | solution.py:20
  85.9 2.3 %collective-permute-done.5 = f32[3,1536]{1,0:T(4,128)S(1)} collective-permute-done((f32[3,1536]{1,0:T(4,128)S(1)}, f32[3,1536]{1,0:T(4,128)S(1)}, u32[]{:S(2)}, u32[]{:S(2)}) %collective-permute-start.5) | collective-permute-done | bytes 18464 | tf_op jit(solution)/shard_map/ppermute | solution.py:20
  88.3 0.6 copy.16
  (7 shorter events, 0.2 us)
Async XLA Ops:
  0.6 9.6 %copy-start = (bf16[1,1,3,192,1536]{4,3,2,1,0:T(8,128)(2,1)S(1)}, bf16[1,1,3,192,1536]{4,3,2,1,0:T(8,128)(2,1)}, u32[]{:S(2)}) copy-start(bf16[1,1,3,192,1536]{4,3,2,1,0:T(8,128)(2,1)} %param.6) | copy-start | bytes 5308420
  0.6 16.7 %collective-permute-start.1 = (bf16[2,16,6144]{2,1,0:T(8,128)(2,1)}, bf16[2,16,6144]{2,1,0:T(8,128)(2,1)S(1)}, u32[]{:S(2)}, u32[]{:S(2)}) collective-permute-start(bf16[2,16,6144]{2,1,0:T(8,128)(2,1)} %bitcast.45), channel_id=1, source_target_pairs={{0,12},{4,0},{8,4},{12,8},{1,13},{5,1},{9,5},{13,9},{2,14},{6,2},{... | collective-permute-start | bytes 1179656 | tf_op jit(solution)/shard_map/ppermute | solution.py:20
  10.4 67.9 %collective-permute-start = (bf16[448,384]{1,0:T(8,128)(2,1)S(1)}, bf16[448,384]{1,0:T(8,128)(2,1)}, u32[]{:S(2)}, u32[]{:S(2)}) collective-permute-start(bf16[448,384]{1,0:T(8,128)(2,1)S(1)} %pad_maximum_fusion), channel_id=1, source_target_pairs={{0,8},{4,12},{8,0},{12,4},{1,9},{5,13},{9,1},{13,5},{2,10},{6,14},... | collective-permute-start | bytes 1032200 | tf_op jit(solution)/shard_map/ppermute | solution.py:20
  10.6 48.5 %collective-permute-start.2 = (bf16[448,384]{1,0:T(8,128)(2,1)S(1)}, bf16[448,384]{1,0:T(8,128)(2,1)S(1)}, u32[]{:S(2)}, u32[]{:S(2)}) collective-permute-start(bf16[448,384]{1,0:T(8,128)(2,1)S(1)} %pad_maximum_fusion.1), channel_id=1, source_target_pairs={{0,8},{4,12},{8,0},{12,4},{1,9},{5,13},{9,1},{13,5},{2,10},{6,14},... | collective-permute-start | bytes 1032200 | tf_op jit(solution)/shard_map/ppermute | solution.py:20
  13.6 52.9 %collective-permute-start.3 = (bf16[448,384]{1,0:T(8,128)(2,1)S(1)}, bf16[448,384]{1,0:T(8,128)(2,1)S(1)}, u32[]{:S(2)}, u32[]{:S(2)}) collective-permute-start(bf16[448,384]{1,0:T(8,128)(2,1)S(1)} %pad_maximum_fusion.2), channel_id=1, source_target_pairs={{0,8},{4,12},{8,0},{12,4},{1,9},{5,13},{9,1},{13,5},{2,10},{6,14},... | collective-permute-start | bytes 1032200 | tf_op jit(solution)/shard_map/ppermute | solution.py:20
  13.7 59.5 %collective-permute-start.4 = (bf16[448,384]{1,0:T(8,128)(2,1)S(1)}, bf16[448,384]{1,0:T(8,128)(2,1)S(1)}, u32[]{:S(2)}, u32[]{:S(2)}) collective-permute-start(bf16[448,384]{1,0:T(8,128)(2,1)S(1)} %pad_maximum_fusion.3), channel_id=1, source_target_pairs={{0,8},{4,12},{8,0},{12,4},{1,9},{5,13},{9,1},{13,5},{2,10},{6,14},... | collective-permute-start | bytes 1032200 | tf_op jit(solution)/shard_map/ppermute | solution.py:20
  18.4 10.9 %all-to-all-start = ((bf16[4,2,16,1536]{3,2,1,0:T(8,128)(2,1)}), bf16[4,2,16,1536]{3,2,1,0:T(8,128)(2,1)S(1)}, u32[]{:S(2)}, u32[]{:S(2)}) async-start(bf16[4,2,16,1536]{3,2,1,0:T(8,128)(2,1)} %copy.14), calls=%async_computation | async-start | bytes 786432 | tf_op jit(solution)/shard_map/all_to_all | solution.py:269
  59.1 0.7 copy-start.2
  66.4 0.7 copy-start.1
  73.2 0.7 copy-start.3
  78.4 6.0 %copy-start.4 = (f32[3,1536]{1,0:T(4,128)S(1)}, f32[3,1536]{1,0:T(4,128)}, u32[]{:S(2)}) copy-start(f32[3,1536]{1,0:T(4,128)} %get-tuple-element.36) | copy-start | bytes 55300
  78.4 6.0 %copy-start.5 = (f32[3,384]{1,0:T(4,128)S(1)}, f32[3,384]{1,0:T(4,128)}, u32[]{:S(2)}) copy-start(f32[3,384]{1,0:T(4,128)} %get-tuple-element.37) | copy-start | bytes 13828
  78.4 6.0 %copy-start.6 = (f32[3,384]{1,0:T(4,128)S(1)}, f32[3,384]{1,0:T(4,128)}, u32[]{:S(2)}) copy-start(f32[3,384]{1,0:T(4,128)} %get-tuple-element.38) | copy-start | bytes 13828
  78.4 6.0 %copy-start.7 = (f32[3,384]{1,0:T(4,128)S(1)}, f32[3,384]{1,0:T(4,128)}, u32[]{:S(2)}) copy-start(f32[3,384]{1,0:T(4,128)} %get-tuple-element.39) | copy-start | bytes 13828
  84.4 3.9 %collective-permute-start.5 = (f32[3,1536]{1,0:T(4,128)S(1)}, f32[3,1536]{1,0:T(4,128)S(1)}, u32[]{:S(2)}, u32[]{:S(2)}) collective-permute-start(f32[3,1536]{1,0:T(4,128)S(1)} %maximum_add_fusion), channel_id=1, source_target_pairs={{0,16},{16,0},{1,17},{17,1},{2,18},{18,2},{3,19},{19,3},{4,20},{20... | collective-permute-start | bytes 55304 | tf_op jit(solution)/shard_map/ppermute | solution.py:20

commit v9 on v7

--- a/solution.py
+++ b/solution.py
@@ -1,3 +1,4 @@
+import functools
 import math
 
 import jax
@@ -142,9 +143,11 @@
     )(meta, stash, grads)
 
 
-def held_backward(part, grads, offset, pick, chunk):
+def held_backward(part, grads, offset, pick, lo):
     rows = grads.shape[1]
     width = part.shape[1]
+    assert lo % width == 0
+    chunk = lo // width
     keys = (part.shape[0] - rows) // 2
     bf16 = jnp.bfloat16
     grid_spec = pltpu.PrefetchScalarGridSpec(
@@ -174,6 +177,69 @@
     )(meta, part, grads)
 
 
+def assemble_kernel(bounds, *refs):
+    count = len(bounds)
+    q_parts, kv_parts, sum_parts = refs[:count], refs[count:2 * count], refs[2 * count:3 * count]
+    kept_sums = refs[3 * count]
+    qg_ref, kv_ref, sum_ref = refs[3 * count + 3:]
+    for c, (lo, hi) in enumerate(bounds):
+        qg_ref[:, lo:hi] = q_parts[c][...]
+        kv_ref[:, :, lo:hi] = kv_parts[c][...]
+        sum_ref[:, lo:hi] = kept_sums[:, lo:hi] + sum_parts[c][...]
+
+
+def assemble(bounds, held_parts, kept_sums, qg, kv):
+    rows, feats = qg.shape[1], qg.shape[2]
+    keys = kv.shape[2]
+    whole = lambda shape: pl.BlockSpec(shape, lambda i: (0,) * len(shape))
+    in_specs = (
+        [whole(part[0].shape) for part in held_parts]
+        + [whole(part[1].shape) for part in held_parts]
+        + [whole(part[2].shape) for part in held_parts]
+        + [whole(kept_sums.shape), pl.BlockSpec(memory_space=pl.ANY), pl.BlockSpec(memory_space=pl.ANY)]
+    )
+    count = len(held_parts)
+    first_alias = 3 * count + 1
+    return pl.pallas_call(
+        functools.partial(assemble_kernel, tuple(bounds)),
+        out_shape=(
+            jax.ShapeDtypeStruct(qg.shape, qg.dtype),
+            jax.ShapeDtypeStruct(kv.shape, kv.dtype),
+            jax.ShapeDtypeStruct(kept_sums.shape, kept_sums.dtype),
+        ),
+        grid=(1,),
+        in_specs=in_specs,
+        out_specs=(
+            pl.BlockSpec((None, rows, feats), lambda i: (1, 0, 0)),
+            pl.BlockSpec((None, 2, keys, feats), lambda i: (1, 0, 0, 0)),
+            whole(kept_sums.shape),
+        ),
+        input_output_aliases={first_alias: 0, first_alias + 1: 1},
+        cost_estimate=pl.CostEstimate(flops=0, transcendentals=0, bytes_accessed=4 * 2 * feats * (rows + 2 * keys)),
+        name="assemble_held",
+    )(*[p[0] for p in held_parts], *[p[1] for p in held_parts], *[p[2] for p in held_parts], kept_sums, qg, kv)
+
+
+def chunk_bounds(heads):
+    sizes = [heads // 3, heads // 3, heads // 6]
+    sizes.append(heads - sum(sizes))
+    if min(sizes) < 1:
+        sizes = [heads]
+    bounds, lo = [], 0
+    for size in sizes:
+        if lo % size:
+            return [(c * HD, (c + 1) * HD) for c in range(heads)] if heads <= 4 else chunk_bounds_even(heads)
+        bounds.append((lo * HD, (lo + size) * HD))
+        lo += size
+    return bounds
+
+
+def chunk_bounds_even(heads):
+    count = next(n for n in (4, 3, 2, 1) if heads % n == 0)
+    size = heads // count
+    return [(c * size * HD, (c + 1) * size * HD) for c in range(count)]
+
+
 def chunk_count(heads):
     for count in range(min(MAX_CHUNKS, heads), 0, -1):
         if heads % count == 0:
@@ -194,12 +260,10 @@
     rows = sent_grad.shape[3] * lax.axis_size("tensor")
     held = held_qkv[0, 0]
     held_q = lax.dynamic_slice_in_dim(held[0], owner_offset, rows, 0)
-    chunks = chunk_count(heads)
-    width = feats // chunks
+    bounds = chunk_bounds_even(heads)
     fetched = []
-    for c in range(chunks):
-        cols = slice(c * width, (c + 1) * width)
-        part = jnp.concatenate([held_q[:, cols], held[1, :, cols], held[2, :, cols]], axis=0)
+    for lo, hi in bounds:
+        part = jnp.concatenate([held_q[:, lo:hi], held[1, :, lo:hi], held[2, :, lo:hi]], axis=0)
         fetched.append(from_behind(part, "pipe", half_way))
 
     arrived = from_behind(sent_grad[0, 0], "pipe", -1)
@@ -213,13 +277,13 @@
     qg, kv, column_sums = kept_backward(kept_qkv[0, 0], regrouped, section_offsets[0], pick)
     first_part, qg, kv, column_sums = lax.optimization_barrier((fetched[0], qg, kv, column_sums))
     fetched = [first_part] + fetched[1:]
+    first_part, qg, kv, column_sums = lax.optimization_barrier((fetched[0], qg, kv, column_sums))
+    fetched = [first_part] + fetched[1:]
     held_parts = [
-        held_backward(fetched[c], regrouped, section_offsets[1], pick, c) for c in range(chunks)
+        held_backward(part, regrouped, section_offsets[1], pick, lo)
+        for (lo, _), part in zip(bounds, fetched)
     ]
-    for c, (part_q, part_kv, _) in enumerate(held_parts):
-        qg = lax.dynamic_update_slice(qg, part_q[None], (1, 0, c * width))
-        kv = lax.dynamic_update_slice(kv, part_kv[None], (1, 0, 0, c * width))
-    column_sums = column_sums + jnp.concatenate([part[2] for part in held_parts], axis=1)
+    qg, kv, column_sums = assemble(bounds, held_parts, column_sums, qg, kv)
     query_grad = qg
     key_value_grad = kv
     if lax.axis_size("dp") == 2:

time: 89.9 us -> 86.8 us (0.966)
  local copies, waits for them, and re-layouts: 16.5 us -> 8.58 us
  waiting for transfers between devices: 20.6 us -> 23.3 us
  Pallas kernels: 28.4 us -> 30.9 us
    dynamic_update_slice x8 -> x0, local copies, waits for them, and re-layouts: 7.87 us -> none  [the longest x4 4.89 us: body(): qg = lax.dynamic_update_slice(qg, part_q[None], (1, 0, c * width))]
    ppermute x6, waiting for transfers between devices: 16.3 us -> 18.9 us  [from_behind(): return lax.ppermute(value, axis, pairs)]
    pallas_call x0 -> x1, Pallas kernels: none -> 2.5 us  [assemble(): pl.pallas_call(functools.partial(assemble_kernel, tuple(bounds)), out_sha...]
    unnamed x23 -> x11, local copies, waits for them, and re-layouts: 3.55 us -> 3.5 us
  transfers between devices with their start and end apart: 7 -> 7, of which waited for: 5 -> 6; matrix products, arithmetic and copies ran while one was open for 18% -> 10% of each run, Pallas kernels for 27% -> 28%
where the time goes in v9:
time: 86.8 us; the launch traced here: 86.2 us
  Pallas kernels  30.9 us (36%)
  waiting for transfers between devices  23.3 us (27%)
  starting transfers between devices  16.1 us (19%)
  local copies, waits for them, and re-layouts  8.58 us (10%)
  other arithmetic  4.07 us (5%)
  between operations  3.32 us (4%)
    ppermute x6, waiting for transfers between devices, from_behind(): return lax.ppermute(value, axis, pairs)  18.9 us
    pallas_call x4, Pallas kernels, held_backward(): pl.pallas_call(held_kernel, out_shape=(jax.ShapeDtypeStruct((rows, width)...  17.5 us
    ppermute x6, starting transfers between devices, from_behind(): return lax.ppermute(value, axis, pairs)  12.7 us
    pallas_call x1, Pallas kernels, kept_backward(): pl.pallas_call(kept_kernel, out_shape=out_shape, grid_spec=grid_spec, cos...  10.9 us
    all_to_all x1, waiting for transfers between devices, body(): lax.all_to_all(split, 'tensor', split_axis=0, concat_axis=0, tiled=True)  4.39 us
    unnamed x11, local copies, waits for them, and re-layouts  3.5 us
    all_to_all x1, starting transfers between devices, body(): lax.all_to_all(split, 'tensor', split_axis=0, concat_axis=0, tiled=True)  3.46 us
    pallas_call x1, Pallas kernels, assemble(): pl.pallas_call(functools.partial(assemble_kernel, tuple(bounds)), out_sha...  2.5 us
  transfers between devices with their start and end apart: 7, of which 6 were waited for; matrix products, arithmetic and copies ran while one was open for 10% of the time, Pallas kernels for 28%

profile of v9, /device:TPU:0, one launch (start us, length us, event | category | flops | bytes accessed | tf_op | source)
XLA Modules:
  0.0 86.2 jit_solution(3011975457197888334)
XLA Ops:
  0.6 0.0 copy-start
  0.6 5.1 %collective-permute-start.1 = (bf16[2,16,6144]{2,1,0:T(8,128)(2,1)}, bf16[2,16,6144]{2,1,0:T(8,128)(2,1)S(1)}, u32[]{:S(2)}, u32[]{:S(2)}) collective-permute-start(bf16[2,16,6144]{2,1,0:T(8,128)(2,1)} %bitcast.45), channel_id=1, source_target_pairs={{0,12},{4,0},{8,4},{12,8},{1,13},{5,1},{9,5},{13,9},{2,14},{6,2},{... | collective-permute-start | bytes 1179656 | tf_op jit(solution)/shard_map/ppermute | solution.py:20
  5.7 0.8 constant_dynamic-slice_fusion
  6.6 0.5 slice.62
  8.4 1.1 %slice.61 = bf16[1,1,1,192,1536]{4,3,2,1,0:T(8,128)(2,1)S(1)} slice(bf16[1,1,3,192,1536]{4,3,2,1,0:T(8,128)(2,1)} %param.6), slice={[0:1], [0:1], [0:1], [0:192], [0:1536]} | slice | bytes 1179648 | tf_op jit(solution)/shard_map/slice | solution.py:262
  10.1 0.1 dynamic-slice_bitcast_fusion
  10.2 0.0 copy-done
  10.2 0.1 slice_bitcast_fusion.1
  10.4 0.8 pad_maximum_fusion
  11.1 0.0 collective-permute-start
  11.2 3.0 %collective-permute-start.2 = (bf16[448,384]{1,0:T(8,128)(2,1)S(1)}, bf16[448,384]{1,0:T(8,128)(2,1)S(1)}, u32[]{:S(2)}, u32[]{:S(2)}) collective-permute-start(bf16[448,384]{1,0:T(8,128)(2,1)S(1)} %pad_maximum_fusion.1), channel_id=1, source_target_pairs={{0,8},{4,12},{8,0},{12,4},{1,9},{5,13},{9,1},{13,5},{2,10},{6,14},... | collective-permute-start | bytes 1032200 | tf_op jit(solution)/shard_map/ppermute | solution.py:20
  14.2 0.1 collective-permute-start.3
  14.3 3.0 %collective-permute-start.4 = (bf16[448,384]{1,0:T(8,128)(2,1)S(1)}, bf16[448,384]{1,0:T(8,128)(2,1)S(1)}, u32[]{:S(2)}, u32[]{:S(2)}) collective-permute-start(bf16[448,384]{1,0:T(8,128)(2,1)S(1)} %pad_maximum_fusion.3), channel_id=1, source_target_pairs={{0,8},{4,12},{8,0},{12,4},{1,9},{5,13},{9,1},{13,5},{2,10},{6,14},... | collective-permute-start | bytes 1032200 | tf_op jit(solution)/shard_map/ppermute | solution.py:20
  18.0 0.0 collective-permute-done.1
  18.0 0.3 reshape.26
  18.3 0.8 copy.14
  19.1 3.5 %all-to-all-start = ((bf16[4,2,16,1536]{3,2,1,0:T(8,128)(2,1)}), bf16[4,2,16,1536]{3,2,1,0:T(8,128)(2,1)S(1)}, u32[]{:S(2)}, u32[]{:S(2)}) async-start(bf16[4,2,16,1536]{3,2,1,0:T(8,128)(2,1)} %copy.14), calls=%async_computation | async-start | bytes 786432 | tf_op jit(solution)/shard_map/all_to_all | solution.py:273
  22.5 0.5 fusion.1
  23.1 1.2 %pad_add_fusion.1.meta_ref = s32[2]{0:T(128)} fusion(s32[1]{0:T(128)} %bitcast.33, s32[1]{0:T(128)} %bitcast.7), kind=kLoop, calls=%fused_computation.17 | loop fusion | flops 2 | bytes 16 | tf_op jit(solution)/shard_map/stack | solution.py:136
  24.3 1.2 %pad_add_fusion.meta_ref = s32[2]{0:T(128)} fusion(s32[1]{0:T(128)} %bitcast.1, s32[1]{0:T(128)} %bitcast), kind=kLoop, calls=%fused_computation.16 | loop fusion | flops 2 | bytes 16 | tf_op jit(solution)/shard_map/stack | solution.py:166
  25.5 4.4 %all-to-all-done = bf16[4,2,16,1536]{3,2,1,0:T(8,128)(2,1)S(1)} async-done(((bf16[4,2,16,1536]{3,2,1,0:T(8,128)(2,1)}), bf16[4,2,16,1536]{3,2,1,0:T(8,128)(2,1)S(1)}, u32[]{:S(2)}, u32[]{:S(2)}) %all-to-all-start) | async-done | bytes 393248 | tf_op jit(solution)/shard_map/all_to_all | solution.py:273
  29.9 0.8 copy.15
  30.7 10.9 %kept_backward.1 = (bf16[2,64,1536]{2,1,0:T(8,128)(2,1)}, bf16[2,2,192,1536]{3,2,1,0:T(8,128)(2,1)}, f32[3,1536]{1,0:T(4,128)}) custom-call(s32[2]{0:T(128)} %pad_add_fusion.1.meta_ref, bf16[3,192,1536]{2,1,0:T(8,128)(2,1)} %bitcast.41, bf16[2,64,1536]{2,1,0:T(8,128)(2,1)} %bitcast.34), custom_call_target="tpu_custom_call" | custom-call | flops 226492416 | bytes 2949120 | tf_op jit(solution)/shard_map/kept_backward/pallas_call | solution.py:137
  41.6 10.3 %collective-permute-done.x_ref = bf16[448,384]{1,0:T(8,128)(2,1)S(1)} collective-permute-done((bf16[448,384]{1,0:T(8,128)(2,1)}, bf16[448,384]{1,0:T(8,128)(2,1)S(1)}, u32[]{:S(2)}, u32[]{:S(2)}) %collective-permute-start) | collective-permute-done | bytes 344096 | tf_op jit(solution)/shard_map/ppermute | solution.py:20
  51.9 0.0 copy-start.4
  51.9 0.7 copy-done.4
  52.6 4.4 %held_backward.4 = (bf16[64,384]{1,0:T(8,128)(2,1)}, bf16[2,192,384]{2,1,0:T(8,128)(2,1)}, f32[3,384]{1,0:T(4,128)}) custom-call(s32[2]{0:T(128)} %pad_add_fusion.meta_ref, bf16[448,384]{1,0:T(8,128)(2,1)} %copy-done.4, bf16[2,64,1536]{2,1,0:T(8,128)(2,1)} %bitcast.35), custom_call_target="tpu_custom_call" | custom-call | flops 56623104 | bytes 737280 | tf_op jit(solution)/shard_map/held_backward/pallas_call | solution.py:167
  56.9 2.3 %collective-permute-done.2.x_ref = bf16[448,384]{1,0:T(8,128)(2,1)S(1)} collective-permute-done((bf16[448,384]{1,0:T(8,128)(2,1)S(1)}, bf16[448,384]{1,0:T(8,128)(2,1)S(1)}, u32[]{:S(2)}, u32[]{:S(2)}) %collective-permute-start.2) | collective-permute-done | bytes 344096 | tf_op jit(solution)/shard_map/ppermute | solution.py:20
  59.2 0.0 copy-start.2
  59.2 0.7 copy-done.2
  60.0 4.4 %held_backward.5 = (bf16[64,384]{1,0:T(8,128)(2,1)}, bf16[2,192,384]{2,1,0:T(8,128)(2,1)}, f32[3,384]{1,0:T(4,128)}) custom-call(s32[2]{0:T(128)} %pad_add_fusion.meta_ref, bf16[448,384]{1,0:T(8,128)(2,1)} %copy-done.2, bf16[2,64,1536]{2,1,0:T(8,128)(2,1)} %bitcast.36), custom_call_target="tpu_custom_call" | custom-call | flops 56623104 | bytes 737280 | tf_op jit(solution)/shard_map/held_backward/pallas_call | solution.py:167
  64.3 2.3 %collective-permute-done.3.x_ref = bf16[448,384]{1,0:T(8,128)(2,1)S(1)} collective-permute-done((bf16[448,384]{1,0:T(8,128)(2,1)S(1)}, bf16[448,384]{1,0:T(8,128)(2,1)S(1)}, u32[]{:S(2)}, u32[]{:S(2)}) %collective-permute-start.3) | collective-permute-done | bytes 344096 | tf_op jit(solution)/shard_map/ppermute | solution.py:20
  66.6 0.0 copy-start.1
  66.6 0.7 copy-done.1
  67.3 4.4 %held_backward.6 = (bf16[64,384]{1,0:T(8,128)(2,1)}, bf16[2,192,384]{2,1,0:T(8,128)(2,1)}, f32[3,384]{1,0:T(4,128)}) custom-call(s32[2]{0:T(128)} %pad_add_fusion.meta_ref, bf16[448,384]{1,0:T(8,128)(2,1)} %copy-done.1, bf16[2,64,1536]{2,1,0:T(8,128)(2,1)} %bitcast.37), custom_call_target="tpu_custom_call" | custom-call | flops 56623104 | bytes 737280 | tf_op jit(solution)/shard_map/held_backward/pallas_call | solution.py:167
  71.7 1.5 %collective-permute-done.4.x_ref = bf16[448,384]{1,0:T(8,128)(2,1)S(1)} collective-permute-done((bf16[448,384]{1,0:T(8,128)(2,1)S(1)}, bf16[448,384]{1,0:T(8,128)(2,1)S(1)}, u32[]{:S(2)}, u32[]{:S(2)}) %collective-permute-start.4) | collective-permute-done | bytes 344096 | tf_op jit(solution)/shard_map/ppermute | solution.py:20
  73.2 0.0 copy-start.3
  73.2 0.7 copy-done.3
  73.9 4.4 %held_backward.7 = (bf16[64,384]{1,0:T(8,128)(2,1)}, bf16[2,192,384]{2,1,0:T(8,128)(2,1)}, f32[3,384]{1,0:T(4,128)}) custom-call(s32[2]{0:T(128)} %pad_add_fusion.meta_ref, bf16[448,384]{1,0:T(8,128)(2,1)} %copy-done.3, bf16[2,64,1536]{2,1,0:T(8,128)(2,1)} %bitcast.38), custom_call_target="tpu_custom_call" | custom-call | flops 56623104 | bytes 737280 | tf_op jit(solution)/shard_map/held_backward/pallas_call | solution.py:167
  78.3 2.5 %assemble_held.1 = (bf16[2,64,1536]{2,1,0:T(8,128)(2,1)}, bf16[2,2,192,1536]{3,2,1,0:T(8,128)(2,1)}, f32[3,1536]{1,0:T(4,128)}) custom-call(bf16[64,384]{1,0:T(8,128)(2,1)} %get-tuple-element.29.refs_0_, bf16[64,384]{1,0:T(8,128)(2,1)} %get-tuple-element.30.refs_1_, ...), custom_call_target="tpu_custom_call", output_to_operand_aliasing={{0}: (13, {}), {1}: (14, {})} | custom-call | bytes 5505024 | tf_op jit(solution)/shard_map/assemble_held/pallas_call | solution.py:203
  80.8 1.5 %collective-permute-start.5 = (f32[3,1536]{1,0:T(4,128)}, f32[3,1536]{1,0:T(4,128)S(1)}, u32[]{:S(2)}, u32[]{:S(2)}) collective-permute-start(f32[3,1536]{1,0:T(4,128)} %get-tuple-element.46), channel_id=1, source_target_pairs={{0,16},{16,0},{1,17},{17,1},{2,18},{18,2},{3,19},{19,3},{4,20},{20... | collective-permute-start | bytes 55304 | tf_op jit(solution)/shard_map/ppermute | solution.py:20
  82.3 2.5 %collective-permute-done.5 = f32[3,1536]{1,0:T(4,128)S(1)} collective-permute-done((f32[3,1536]{1,0:T(4,128)}, f32[3,1536]{1,0:T(4,128)S(1)}, u32[]{:S(2)}, u32[]{:S(2)}) %collective-permute-start.5) | collective-permute-done | bytes 18464 | tf_op jit(solution)/shard_map/ppermute | solution.py:20
  84.9 0.7 add_bitcast_fusion
  85.6 0.6 copy.16
  (4 shorter events, 0.1 us)
Async XLA Ops:
  0.6 9.6 %copy-start = (bf16[1,1,3,192,1536]{4,3,2,1,0:T(8,128)(2,1)S(1)}, bf16[1,1,3,192,1536]{4,3,2,1,0:T(8,128)(2,1)}, u32[]{:S(2)}) copy-start(bf16[1,1,3,192,1536]{4,3,2,1,0:T(8,128)(2,1)} %param.6) | copy-start | bytes 5308420
  0.6 17.3 %collective-permute-start.1 = (bf16[2,16,6144]{2,1,0:T(8,128)(2,1)}, bf16[2,16,6144]{2,1,0:T(8,128)(2,1)S(1)}, u32[]{:S(2)}, u32[]{:S(2)}) collective-permute-start(bf16[2,16,6144]{2,1,0:T(8,128)(2,1)} %bitcast.45), channel_id=1, source_target_pairs={{0,12},{4,0},{8,4},{12,8},{1,13},{5,1},{9,5},{13,9},{2,14},{6,2},{... | collective-permute-start | bytes 1179656 | tf_op jit(solution)/shard_map/ppermute | solution.py:20
  11.1 40.7 %collective-permute-start = (bf16[448,384]{1,0:T(8,128)(2,1)}, bf16[448,384]{1,0:T(8,128)(2,1)S(1)}, u32[]{:S(2)}, u32[]{:S(2)}) collective-permute-start(bf16[448,384]{1,0:T(8,128)(2,1)} %pad_maximum_fusion), channel_id=1, source_target_pairs={{0,8},{4,12},{8,0},{12,4},{1,9},{5,13},{9,1},{13,5},{2,10},{6,14},... | collective-permute-start | bytes 1032200 | tf_op jit(solution)/shard_map/ppermute | solution.py:20
  11.2 48.1 %collective-permute-start.2 = (bf16[448,384]{1,0:T(8,128)(2,1)S(1)}, bf16[448,384]{1,0:T(8,128)(2,1)S(1)}, u32[]{:S(2)}, u32[]{:S(2)}) collective-permute-start(bf16[448,384]{1,0:T(8,128)(2,1)S(1)} %pad_maximum_fusion.1), channel_id=1, source_target_pairs={{0,8},{4,12},{8,0},{12,4},{1,9},{5,13},{9,1},{13,5},{2,10},{6,14},... | collective-permute-start | bytes 1032200 | tf_op jit(solution)/shard_map/ppermute | solution.py:20
  14.2 52.4 %collective-permute-start.3 = (bf16[448,384]{1,0:T(8,128)(2,1)S(1)}, bf16[448,384]{1,0:T(8,128)(2,1)S(1)}, u32[]{:S(2)}, u32[]{:S(2)}) collective-permute-start(bf16[448,384]{1,0:T(8,128)(2,1)S(1)} %pad_maximum_fusion.2), channel_id=1, source_target_pairs={{0,8},{4,12},{8,0},{12,4},{1,9},{5,13},{9,1},{13,5},{2,10},{6,14},... | collective-permute-start | bytes 1032200 | tf_op jit(solution)/shard_map/ppermute | solution.py:20
  14.3 58.9 %collective-permute-start.4 = (bf16[448,384]{1,0:T(8,128)(2,1)S(1)}, bf16[448,384]{1,0:T(8,128)(2,1)S(1)}, u32[]{:S(2)}, u32[]{:S(2)}) collective-permute-start(bf16[448,384]{1,0:T(8,128)(2,1)S(1)} %pad_maximum_fusion.3), channel_id=1, source_target_pairs={{0,8},{4,12},{8,0},{12,4},{1,9},{5,13},{9,1},{13,5},{2,10},{6,14},... | collective-permute-start | bytes 1032200 | tf_op jit(solution)/shard_map/ppermute | solution.py:20
  19.1 10.9 %all-to-all-start = ((bf16[4,2,16,1536]{3,2,1,0:T(8,128)(2,1)}), bf16[4,2,16,1536]{3,2,1,0:T(8,128)(2,1)S(1)}, u32[]{:S(2)}, u32[]{:S(2)}) async-start(bf16[4,2,16,1536]{3,2,1,0:T(8,128)(2,1)} %copy.14), calls=%async_computation | async-start | bytes 786432 | tf_op jit(solution)/shard_map/all_to_all | solution.py:273
  51.9 0.7 copy-start.4
  59.2 0.7 copy-start.2
  66.6 0.7 copy-start.1
  73.2 0.7 copy-start.3
  80.8 4.0 %collective-permute-start.5 = (f32[3,1536]{1,0:T(4,128)}, f32[3,1536]{1,0:T(4,128)S(1)}, u32[]{:S(2)}, u32[]{:S(2)}) collective-permute-start(f32[3,1536]{1,0:T(4,128)} %get-tuple-element.46), channel_id=1, source_target_pairs={{0,16},{16,0},{1,17},{17,1},{2,18},{18,2},{3,19},{19,3},{4,20},{20... | collective-permute-start | bytes 55304 | tf_op jit(solution)/shard_map/ppermute | solution.py:20

commit v10 on v9

--- a/solution.py
+++ b/solution.py
@@ -177,6 +177,33 @@
     )(meta, part, grads)
 
 
+def pack_kernel(count, half, bounds, off_ref, x_ref, *out_refs):
+    owner = (lax.axis_index("pipe") + count - half) % count
+    start = pl.multiple_of(off_ref[owner, 1], 16)
+    rows = out_refs[0].shape[0] - 2 * x_ref.shape[1]
+    keys = x_ref.shape[1]
+    for (lo, hi), out_ref in zip(bounds, out_refs):
+        out_ref[pl.ds(0, rows), :] = x_ref[0, pl.ds(start, rows), lo:hi]
+        out_ref[pl.ds(rows, keys), :] = x_ref[1, :, lo:hi]
+        out_ref[pl.ds(rows + keys, keys), :] = x_ref[2, :, lo:hi]
+
+
+def pack_held(held, offsets, rows, count, half, bounds):
+    keys = held.shape[1]
+    out_shape = tuple(
+        jax.ShapeDtypeStruct((rows + 2 * keys, hi - lo), held.dtype) for lo, hi in bounds
+    )
+    vmem = pl.BlockSpec(memory_space=pltpu.VMEM)
+    return pl.pallas_call(
+        functools.partial(pack_kernel, count, half, tuple(bounds)),
+        out_shape=out_shape,
+        in_specs=[pl.BlockSpec(memory_space=pltpu.SMEM), vmem],
+        out_specs=tuple(vmem for _ in bounds),
+        cost_estimate=pl.CostEstimate(flops=0, transcendentals=0, bytes_accessed=4 * held.size),
+        name="pack_held",
+    )(offsets, held)
+
+
 def assemble_kernel(bounds, *refs):
     count = len(bounds)
     q_parts, kv_parts, sum_parts = refs[:count], refs[count:2 * count], refs[2 * count:3 * count]
@@ -255,16 +282,10 @@
     keys = kept_qkv.shape[-2]
     heads = feats // HD
 
-    owner = (section_index + section_count - half_way) % section_count
-    owner_offset = lax.dynamic_index_in_dim(offsets[0], owner, 0, keepdims=False)[1]
     rows = sent_grad.shape[3] * lax.axis_size("tensor")
-    held = held_qkv[0, 0]
-    held_q = lax.dynamic_slice_in_dim(held[0], owner_offset, rows, 0)
     bounds = chunk_bounds_even(heads)
-    fetched = []
-    for lo, hi in bounds:
-        part = jnp.concatenate([held_q[:, lo:hi], held[1, :, lo:hi], held[2, :, lo:hi]], axis=0)
-        fetched.append(from_behind(part, "pipe", half_way))
+    parts = pack_held(held_qkv[0, 0], offsets[0], rows, section_count, half_way, bounds)
+    fetched = [from_behind(part, "pipe", half_way) for part in parts]
 
     arrived = from_behind(sent_grad[0, 0], "pipe", -1)
     tensor_count = lax.axis_size("tensor")

time: 86.8 us -> 95 us (1.094)
  the two profiles are of different devices: /device:TPU:0 before, /device:TPU:8 now
where the time goes in v10:
time: 95 us; the launch traced here: 94.4 us
  waiting for transfers between devices  37.2 us (39%)
  Pallas kernels  33.5 us (35%)
  starting transfers between devices  11 us (12%)
  local copies, waits for them, and re-layouts  8.1 us (9%)
  other arithmetic  3.19 us (3%)
  between operations  1.32 us (1%)
    ppermute x6, waiting for transfers between devices, from_behind(): return lax.ppermute(value, axis, pairs)  32.9 us
    pallas_call x4, Pallas kernels, held_backward(): pl.pallas_call(held_kernel, out_shape=(jax.ShapeDtypeStruct((rows, width)...  17.5 us
    pallas_call x1, Pallas kernels, kept_backward(): pl.pallas_call(kept_kernel, out_shape=out_shape, grid_spec=grid_spec, cos...  10.9 us
    ppermute x6, starting transfers between devices, from_behind(): return lax.ppermute(value, axis, pairs)  7.57 us
    all_to_all x1, waiting for transfers between devices, body(): lax.all_to_all(split, 'tensor', split_axis=0, concat_axis=0, tiled=True)  4.39 us
    unnamed x9, local copies, waits for them, and re-layouts  3.57 us
    all_to_all x1, starting transfers between devices, body(): lax.all_to_all(split, 'tensor', split_axis=0, concat_axis=0, tiled=True)  3.46 us
    pallas_call x1, Pallas kernels, pack_held(): pl.pallas_call(functools.partial(pack_kernel, count, half, tuple(bounds))...  2.62 us
  transfers between devices with their start and end apart: 7, of which 3 were waited for; matrix products, arithmetic and copies ran while one was open for 7% of the time, Pallas kernels for 28%

profile of v10, /device:TPU:8, one launch (start us, length us, event | category | flops | bytes accessed | tf_op | source)
XLA Modules:
  0.0 94.4 jit_solution(3299819813846645547)
XLA Ops:
  0.6 0.1 collective-permute-start.1
  0.7 1.3 %copy.16.off_ref = s32[4,2]{1,0:T(4,128)} copy(s32[4,2]{0,1:T(2,128)} %bitcast.27) | data formatting | bytes 64 | tf_op jit(solution)/shard_map/squeeze | solution.py:297
  2.0 2.6 %pack_held.1 = (bf16[448,384]{1,0:T(8,128)(2,1)}, bf16[448,384]{1,0:T(8,128)(2,1)}, bf16[448,384]{1,0:T(8,128)(2,1)}, bf16[448,384]{1,0:T(8,128)(2,1)}) custom-call(s32[4,2]{1,0:T(4,128)} %copy.16.off_ref, bf16[3,192,1536]{2,1,0:T(8,128)(2,1)} %bitcast.23), custom_call_target="tpu_custom_call" | custom-call | bytes 3538944 | tf_op jit(solution)/shard_map/pack_held/pallas_call | solution.py:197
  4.7 3.0 %collective-permute-start = (bf16[448,384]{1,0:T(8,128)(2,1)}, bf16[448,384]{1,0:T(8,128)(2,1)S(1)}, u32[]{:S(2)}, u32[]{:S(2)}) collective-permute-start(bf16[448,384]{1,0:T(8,128)(2,1)} %get-tuple-element.29), channel_id=1, source_target_pairs={{0,8},{4,12},{8,0},{12,4},{1,9},{5,13},{9,1},{13,5},{2,10},{6,14},... | collective-permute-start | bytes 1032200 | tf_op jit(solution)/shard_map/ppermute | solution.py:20
  7.7 0.0 collective-permute-start.2
  7.7 2.9 %collective-permute-start.3 = (bf16[448,384]{1,0:T(8,128)(2,1)}, bf16[448,384]{1,0:T(8,128)(2,1)S(1)}, u32[]{:S(2)}, u32[]{:S(2)}) collective-permute-start(bf16[448,384]{1,0:T(8,128)(2,1)} %get-tuple-element.37), channel_id=1, source_target_pairs={{0,8},{4,12},{8,0},{12,4},{1,9},{5,13},{9,1},{13,5},{2,10},{6,14},... | collective-permute-start | bytes 1032200 | tf_op jit(solution)/shard_map/ppermute | solution.py:20
  10.6 0.0 collective-permute-start.4
  11.3 0.8 constant_dynamic-slice_fusion
  12.1 30.3 %collective-permute-done.1 = bf16[2,16,6144]{2,1,0:T(8,128)(2,1)S(1)} collective-permute-done((bf16[2,16,6144]{2,1,0:T(8,128)(2,1)}, bf16[2,16,6144]{2,1,0:T(8,128)(2,1)S(1)}, u32[]{:S(2)}, u32[]{:S(2)}) %collective-permute-start.1) | collective-permute-done | bytes 393248 | tf_op jit(solution)/shard_map/ppermute | solution.py:20
  42.4 0.3 reshape.19
  42.7 0.8 copy.17
  43.5 3.5 %all-to-all-start = ((bf16[4,2,16,1536]{3,2,1,0:T(8,128)(2,1)}), bf16[4,2,16,1536]{3,2,1,0:T(8,128)(2,1)S(1)}, u32[]{:S(2)}, u32[]{:S(2)}) async-start(bf16[4,2,16,1536]{3,2,1,0:T(8,128)(2,1)} %copy.17), calls=%async_computation | async-start | bytes 786432 | tf_op jit(solution)/shard_map/all_to_all | solution.py:294
  47.0 0.6 fusion
  47.5 1.2 %pad_add_fusion.1.meta_ref = s32[2]{0:T(128)} fusion(s32[1]{0:T(128)} %bitcast.15, s32[1]{0:T(128)} %bitcast.4), kind=kLoop, calls=%fused_computation.2 | loop fusion | flops 2 | bytes 16 | tf_op jit(solution)/shard_map/stack | solution.py:136
  48.7 1.2 %pad_add_fusion.meta_ref = s32[2]{0:T(128)} fusion(s32[1]{0:T(128)} %bitcast.1, s32[1]{0:T(128)} %bitcast), kind=kLoop, calls=%fused_computation.1 | loop fusion | flops 2 | bytes 16 | tf_op jit(solution)/shard_map/stack | solution.py:166
  50.0 4.4 %all-to-all-done = bf16[4,2,16,1536]{3,2,1,0:T(8,128)(2,1)S(1)} async-done(((bf16[4,2,16,1536]{3,2,1,0:T(8,128)(2,1)}), bf16[4,2,16,1536]{3,2,1,0:T(8,128)(2,1)S(1)}, u32[]{:S(2)}, u32[]{:S(2)}) %all-to-all-start) | async-done | bytes 393248 | tf_op jit(solution)/shard_map/all_to_all | solution.py:294
  54.4 0.8 copy.18
  55.1 10.9 %kept_backward.1 = (bf16[2,64,1536]{2,1,0:T(8,128)(2,1)}, bf16[2,2,192,1536]{3,2,1,0:T(8,128)(2,1)}, f32[3,1536]{1,0:T(4,128)}) custom-call(s32[2]{0:T(128)} %pad_add_fusion.1.meta_ref, bf16[3,192,1536]{2,1,0:T(8,128)(2,1)} %bitcast.22, bf16[2,64,1536]{2,1,0:T(8,128)(2,1)} %bitcast.16), custom_call_target="tpu_custom_call" | custom-call | flops 226492416 | bytes 2949120 | tf_op jit(solution)/shard_map/kept_backward/pallas_call | solution.py:137
  66.0 0.0 collective-permute-done.x_ref
  66.0 0.0 copy-start.3
  66.0 0.7 copy-done.3
  66.8 4.4 %held_backward.4 = (bf16[64,384]{1,0:T(8,128)(2,1)}, bf16[2,192,384]{2,1,0:T(8,128)(2,1)}, f32[3,384]{1,0:T(4,128)}) custom-call(s32[2]{0:T(128)} %pad_add_fusion.meta_ref, bf16[448,384]{1,0:T(8,128)(2,1)} %copy-done.3, bf16[2,64,1536]{2,1,0:T(8,128)(2,1)} %bitcast.17), custom_call_target="tpu_custom_call" | custom-call | flops 56623104 | bytes 737280 | tf_op jit(solution)/shard_map/held_backward/pallas_call | solution.py:167
  71.2 0.0 collective-permute-done.2.x_ref
  71.2 0.0 copy-start.2
  71.2 0.7 copy-done.2
  71.9 4.4 %held_backward.5 = (bf16[64,384]{1,0:T(8,128)(2,1)}, bf16[2,192,384]{2,1,0:T(8,128)(2,1)}, f32[3,384]{1,0:T(4,128)}) custom-call(s32[2]{0:T(128)} %pad_add_fusion.meta_ref, bf16[448,384]{1,0:T(8,128)(2,1)} %copy-done.2, bf16[2,64,1536]{2,1,0:T(8,128)(2,1)} %bitcast.18), custom_call_target="tpu_custom_call" | custom-call | flops 56623104 | bytes 737280 | tf_op jit(solution)/shard_map/held_backward/pallas_call | solution.py:167
  76.3 0.0 collective-permute-done.3.x_ref
  76.3 0.0 copy-start.1
  76.3 0.7 copy-done.1
  77.0 4.4 %held_backward.6 = (bf16[64,384]{1,0:T(8,128)(2,1)}, bf16[2,192,384]{2,1,0:T(8,128)(2,1)}, f32[3,384]{1,0:T(4,128)}) custom-call(s32[2]{0:T(128)} %pad_add_fusion.meta_ref, bf16[448,384]{1,0:T(8,128)(2,1)} %copy-done.1, bf16[2,64,1536]{2,1,0:T(8,128)(2,1)} %bitcast.19), custom_call_target="tpu_custom_call" | custom-call | flops 56623104 | bytes 737280 | tf_op jit(solution)/shard_map/held_backward/pallas_call | solution.py:167
  81.4 0.0 collective-permute-done.4.x_ref
  81.4 0.0 copy-start
  81.4 0.7 copy-done
  82.1 4.4 %held_backward.7 = (bf16[64,384]{1,0:T(8,128)(2,1)}, bf16[2,192,384]{2,1,0:T(8,128)(2,1)}, f32[3,384]{1,0:T(4,128)}) custom-call(s32[2]{0:T(128)} %pad_add_fusion.meta_ref, bf16[448,384]{1,0:T(8,128)(2,1)} %copy-done, bf16[2,64,1536]{2,1,0:T(8,128)(2,1)} %bitcast.20), custom_call_target="tpu_custom_call" | custom-call | flops 56623104 | bytes 737280 | tf_op jit(solution)/shard_map/held_backward/pallas_call | solution.py:167
  86.5 2.5 %assemble_held.1 = (bf16[2,64,1536]{2,1,0:T(8,128)(2,1)}, bf16[2,2,192,1536]{3,2,1,0:T(8,128)(2,1)}, f32[3,1536]{1,0:T(4,128)}) custom-call(bf16[64,384]{1,0:T(8,128)(2,1)} %get-tuple-element.34.refs_0_, bf16[64,384]{1,0:T(8,128)(2,1)} %get-tuple-element.36.refs_1_, ...), custom_call_target="tpu_custom_call", output_to_operand_aliasing={{0}: (13, {}), {1}: (14, {})} | custom-call | bytes 5505024 | tf_op jit(solution)/shard_map/assemble_held/pallas_call | solution.py:230
  89.0 1.5 %collective-permute-start.5 = (f32[3,1536]{1,0:T(4,128)}, f32[3,1536]{1,0:T(4,128)S(1)}, u32[]{:S(2)}, u32[]{:S(2)}) collective-permute-start(f32[3,1536]{1,0:T(4,128)} %get-tuple-element.54), channel_id=1, source_target_pairs={{0,16},{16,0},{1,17},{17,1},{2,18},{18,2},{3,19},{19,3},{4,20},{20... | collective-permute-start | bytes 55304 | tf_op jit(solution)/shard_map/ppermute | solution.py:20
  90.5 2.5 %collective-permute-done.5 = f32[3,1536]{1,0:T(4,128)S(1)} collective-permute-done((f32[3,1536]{1,0:T(4,128)}, f32[3,1536]{1,0:T(4,128)S(1)}, u32[]{:S(2)}, u32[]{:S(2)}) %collective-permute-start.5) | collective-permute-done | bytes 18464 | tf_op jit(solution)/shard_map/ppermute | solution.py:20
  93.1 0.7 add_bitcast_fusion
  93.8 0.6 copy.19
Async XLA Ops:
  0.6 41.8 %collective-permute-start.1 = (bf16[2,16,6144]{2,1,0:T(8,128)(2,1)}, bf16[2,16,6144]{2,1,0:T(8,128)(2,1)S(1)}, u32[]{:S(2)}, u32[]{:S(2)}) collective-permute-start(bf16[2,16,6144]{2,1,0:T(8,128)(2,1)} %bitcast.28), channel_id=1, source_target_pairs={{0,12},{4,0},{8,4},{12,8},{1,13},{5,1},{9,5},{13,9},{2,14},{6,2},{... | collective-permute-start | bytes 1179656 | tf_op jit(solution)/shard_map/ppermute | solution.py:20
  4.7 61.4 %collective-permute-start = (bf16[448,384]{1,0:T(8,128)(2,1)}, bf16[448,384]{1,0:T(8,128)(2,1)S(1)}, u32[]{:S(2)}, u32[]{:S(2)}) collective-permute-start(bf16[448,384]{1,0:T(8,128)(2,1)} %get-tuple-element.29), channel_id=1, source_target_pairs={{0,8},{4,12},{8,0},{12,4},{1,9},{5,13},{9,1},{13,5},{2,10},{6,14},... | collective-permute-start | bytes 1032200 | tf_op jit(solution)/shard_map/ppermute | solution.py:20
  7.7 63.5 %collective-permute-start.2 = (bf16[448,384]{1,0:T(8,128)(2,1)}, bf16[448,384]{1,0:T(8,128)(2,1)S(1)}, u32[]{:S(2)}, u32[]{:S(2)}) collective-permute-start(bf16[448,384]{1,0:T(8,128)(2,1)} %get-tuple-element.35), channel_id=1, source_target_pairs={{0,8},{4,12},{8,0},{12,4},{1,9},{5,13},{9,1},{13,5},{2,10},{6,14},... | collective-permute-start | bytes 1032200 | tf_op jit(solution)/shard_map/ppermute | solution.py:20
  7.7 68.6 %collective-permute-start.3 = (bf16[448,384]{1,0:T(8,128)(2,1)}, bf16[448,384]{1,0:T(8,128)(2,1)S(1)}, u32[]{:S(2)}, u32[]{:S(2)}) collective-permute-start(bf16[448,384]{1,0:T(8,128)(2,1)} %get-tuple-element.37), channel_id=1, source_target_pairs={{0,8},{4,12},{8,0},{12,4},{1,9},{5,13},{9,1},{13,5},{2,10},{6,14},... | collective-permute-start | bytes 1032200 | tf_op jit(solution)/shard_map/ppermute | solution.py:20
  10.6 70.8 %collective-permute-start.4 = (bf16[448,384]{1,0:T(8,128)(2,1)}, bf16[448,384]{1,0:T(8,128)(2,1)S(1)}, u32[]{:S(2)}, u32[]{:S(2)}) collective-permute-start(bf16[448,384]{1,0:T(8,128)(2,1)} %get-tuple-element.39), channel_id=1, source_target_pairs={{0,8},{4,12},{8,0},{12,4},{1,9},{5,13},{9,1},{13,5},{2,10},{6,14},... | collective-permute-start | bytes 1032200 | tf_op jit(solution)/shard_map/ppermute | solution.py:20
  43.5 10.9 %all-to-all-start = ((bf16[4,2,16,1536]{3,2,1,0:T(8,128)(2,1)}), bf16[4,2,16,1536]{3,2,1,0:T(8,128)(2,1)S(1)}, u32[]{:S(2)}, u32[]{:S(2)}) async-start(bf16[4,2,16,1536]{3,2,1,0:T(8,128)(2,1)} %copy.17), calls=%async_computation | async-start | bytes 786432 | tf_op jit(solution)/shard_map/all_to_all | solution.py:294
  66.0 0.7 copy-start.3
  71.2 0.7 copy-start.2
  76.3 0.7 copy-start.1
  81.4 0.7 copy-start
  89.0 4.0 %collective-permute-start.5 = (f32[3,1536]{1,0:T(4,128)}, f32[3,1536]{1,0:T(4,128)S(1)}, u32[]{:S(2)}, u32[]{:S(2)}) collective-permute-start(f32[3,1536]{1,0:T(4,128)} %get-tuple-element.54), channel_id=1, source_target_pairs={{0,16},{16,0},{1,17},{17,1},{2,18},{18,2},{3,19},{19,3},{4,20},{20... | collective-permute-start | bytes 55304 | tf_op jit(solution)/shard_map/ppermute | solution.py:20

commit v11 on v9

--- a/solution.py
+++ b/solution.py
@@ -179,45 +179,40 @@
 
 def assemble_kernel(bounds, *refs):
     count = len(bounds)
-    q_parts, kv_parts, sum_parts = refs[:count], refs[count:2 * count], refs[2 * count:3 * count]
-    kept_sums = refs[3 * count]
-    qg_ref, kv_ref, sum_ref = refs[3 * count + 3:]
+    q_parts, kv_parts = refs[:count], refs[count:2 * count]
+    qg_ref, kv_ref = refs[2 * count + 2:]
     for c, (lo, hi) in enumerate(bounds):
         qg_ref[:, lo:hi] = q_parts[c][...]
         kv_ref[:, :, lo:hi] = kv_parts[c][...]
-        sum_ref[:, lo:hi] = kept_sums[:, lo:hi] + sum_parts[c][...]
-
-
-def assemble(bounds, held_parts, kept_sums, qg, kv):
+
+
+def assemble(bounds, held_parts, qg, kv):
     rows, feats = qg.shape[1], qg.shape[2]
     keys = kv.shape[2]
     whole = lambda shape: pl.BlockSpec(shape, lambda i: (0,) * len(shape))
     in_specs = (
         [whole(part[0].shape) for part in held_parts]
         + [whole(part[1].shape) for part in held_parts]
-        + [whole(part[2].shape) for part in held_parts]
-        + [whole(kept_sums.shape), pl.BlockSpec(memory_space=pl.ANY), pl.BlockSpec(memory_space=pl.ANY)]
+        + [pl.BlockSpec(memory_space=pl.ANY), pl.BlockSpec(memory_space=pl.ANY)]
     )
     count = len(held_parts)
-    first_alias = 3 * count + 1
+    first_alias = 2 * count
     return pl.pallas_call(
         functools.partial(assemble_kernel, tuple(bounds)),
         out_shape=(
             jax.ShapeDtypeStruct(qg.shape, qg.dtype),
             jax.ShapeDtypeStruct(kv.shape, kv.dtype),
-            jax.ShapeDtypeStruct(kept_sums.shape, kept_sums.dtype),
         ),
         grid=(1,),
         in_specs=in_specs,
         out_specs=(
             pl.BlockSpec((None, rows, feats), lambda i: (1, 0, 0)),
             pl.BlockSpec((None, 2, keys, feats), lambda i: (1, 0, 0, 0)),
-            whole(kept_sums.shape),
         ),
         input_output_aliases={first_alias: 0, first_alias + 1: 1},
-        cost_estimate=pl.CostEstimate(flops=0, transcendentals=0, bytes_accessed=4 * 2 * feats * (rows + 2 * keys)),
+        cost_estimate=pl.CostEstimate(flops=0, transcendentals=0, bytes_accessed=4 * feats * (rows + 2 * keys)),
         name="assemble_held",
-    )(*[p[0] for p in held_parts], *[p[1] for p in held_parts], *[p[2] for p in held_parts], kept_sums, qg, kv)
+    )(*[p[0] for p in held_parts], *[p[1] for p in held_parts], qg, kv)
 
 
 def chunk_bounds(heads):
@@ -283,7 +278,8 @@
         held_backward(part, regrouped, section_offsets[1], pick, lo)
         for (lo, _), part in zip(bounds, fetched)
     ]
-    qg, kv, column_sums = assemble(bounds, held_parts, column_sums, qg, kv)
+    column_sums = column_sums + jnp.concatenate([part[2] for part in held_parts], axis=1)
+    qg, kv = assemble(bounds, held_parts, qg, kv)
     query_grad = qg
     key_value_grad = kv
     if lax.axis_size("dp") == 2:

time: 86.8 us -> 84.4 us (0.972)
  waiting for transfers between devices: 23.3 us -> 20.7 us
    ppermute x6, waiting for transfers between devices: 18.9 us -> 16.3 us  [from_behind(): return lax.ppermute(value, axis, pairs)]
    unnamed x11 -> x15, local copies, waits for them, and re-layouts: 3.5 us -> 3.55 us
  transfers between devices with their start and end apart: 7 -> 7, of which waited for: 6 -> 5; matrix products, arithmetic and copies ran while one was open for 10% -> 10% of each run, Pallas kernels for 28% -> 32%
where the time goes in v11:
time: 84.4 us; the launch traced here: 83.8 us
  Pallas kernels  30.9 us (37%)
  waiting for transfers between devices  20.7 us (25%)
  starting transfers between devices  16.2 us (19%)
  local copies, waits for them, and re-layouts  8.62 us (10%)
  other arithmetic  4.13 us (5%)
  between operations  3.33 us (4%)
    pallas_call x4, Pallas kernels, held_backward(): pl.pallas_call(held_kernel, out_shape=(jax.ShapeDtypeStruct((rows, width)...  17.5 us
    ppermute x6, waiting for transfers between devices, from_behind(): return lax.ppermute(value, axis, pairs)  16.3 us
    ppermute x6, starting transfers between devices, from_behind(): return lax.ppermute(value, axis, pairs)  12.7 us
    pallas_call x1, Pallas kernels, kept_backward(): pl.pallas_call(kept_kernel, out_shape=out_shape, grid_spec=grid_spec, cos...  10.9 us
    all_to_all x1, waiting for transfers between devices, body(): lax.all_to_all(split, 'tensor', split_axis=0, concat_axis=0, tiled=True)  4.34 us
    unnamed x15, local copies, waits for them, and re-layouts  3.55 us
    all_to_all x1, starting transfers between devices, body(): lax.all_to_all(split, 'tensor', split_axis=0, concat_axis=0, tiled=True)  3.46 us
    pallas_call x1, Pallas kernels, assemble(): pl.pallas_call(functools.partial(assemble_kernel, tuple(bounds)), out_sha...  2.51 us
  transfers between devices with their start and end apart: 7, of which 5 were waited for; matrix products, arithmetic and copies ran while one was open for 10% of the time, Pallas kernels for 32%

profile of v11, /device:TPU:0, one launch (start us, length us, event | category | flops | bytes accessed | tf_op | source)
XLA Modules:
  0.0 83.8 jit_solution(9452703940610593727)
XLA Ops:
  0.6 0.0 copy-start
  0.6 5.1 %collective-permute-start.1 = (bf16[2,16,6144]{2,1,0:T(8,128)(2,1)}, bf16[2,16,6144]{2,1,0:T(8,128)(2,1)S(1)}, u32[]{:S(2)}, u32[]{:S(2)}) collective-permute-start(bf16[2,16,6144]{2,1,0:T(8,128)(2,1)} %bitcast.45), channel_id=1, source_target_pairs={{0,12},{4,0},{8,4},{12,8},{1,13},{5,1},{9,5},{13,9},{2,14},{6,2},{... | collective-permute-start | bytes 1179656 | tf_op jit(solution)/shard_map/ppermute | solution.py:20
  5.7 0.8 constant_dynamic-slice_fusion
  6.6 0.5 slice.62
  8.4 1.1 %slice.61 = bf16[1,1,1,192,1536]{4,3,2,1,0:T(8,128)(2,1)S(1)} slice(bf16[1,1,3,192,1536]{4,3,2,1,0:T(8,128)(2,1)} %param.6), slice={[0:1], [0:1], [0:1], [0:192], [0:1536]} | slice | bytes 1179648 | tf_op jit(solution)/shard_map/slice | solution.py:257
  10.1 0.1 dynamic-slice_bitcast_fusion
  10.2 0.0 copy-done
  10.2 0.1 slice_bitcast_fusion.1
  10.4 0.8 pad_maximum_fusion
  11.2 0.0 collective-permute-start
  11.2 3.0 %collective-permute-start.2 = (bf16[448,384]{1,0:T(8,128)(2,1)S(1)}, bf16[448,384]{1,0:T(8,128)(2,1)S(1)}, u32[]{:S(2)}, u32[]{:S(2)}) collective-permute-start(bf16[448,384]{1,0:T(8,128)(2,1)S(1)} %pad_maximum_fusion.1), channel_id=1, source_target_pairs={{0,8},{4,12},{8,0},{12,4},{1,9},{5,13},{9,1},{13,5},{2,10},{6,14},... | collective-permute-start | bytes 1032200 | tf_op jit(solution)/shard_map/ppermute | solution.py:20
  14.2 0.1 collective-permute-start.3
  14.3 3.0 %collective-permute-start.4 = (bf16[448,384]{1,0:T(8,128)(2,1)S(1)}, bf16[448,384]{1,0:T(8,128)(2,1)S(1)}, u32[]{:S(2)}, u32[]{:S(2)}) collective-permute-start(bf16[448,384]{1,0:T(8,128)(2,1)S(1)} %pad_maximum_fusion.3), channel_id=1, source_target_pairs={{0,8},{4,12},{8,0},{12,4},{1,9},{5,13},{9,1},{13,5},{2,10},{6,14},... | collective-permute-start | bytes 1032200 | tf_op jit(solution)/shard_map/ppermute | solution.py:20
  18.0 0.0 collective-permute-done.1
  18.0 0.3 reshape.26
  18.3 0.8 copy.14
  19.1 3.5 %all-to-all-start = ((bf16[4,2,16,1536]{3,2,1,0:T(8,128)(2,1)}), bf16[4,2,16,1536]{3,2,1,0:T(8,128)(2,1)S(1)}, u32[]{:S(2)}, u32[]{:S(2)}) async-start(bf16[4,2,16,1536]{3,2,1,0:T(8,128)(2,1)} %copy.14), calls=%async_computation | async-start | bytes 786432 | tf_op jit(solution)/shard_map/all_to_all | solution.py:268
  22.5 0.5 fusion.1
  23.1 1.2 %pad_add_fusion.1.meta_ref = s32[2]{0:T(128)} fusion(s32[1]{0:T(128)} %bitcast.33, s32[1]{0:T(128)} %bitcast.7), kind=kLoop, calls=%fused_computation.18 | loop fusion | flops 2 | bytes 16 | tf_op jit(solution)/shard_map/stack | solution.py:136
  24.3 1.3 %pad_add_fusion.meta_ref = s32[2]{0:T(128)} fusion(s32[1]{0:T(128)} %bitcast.1, s32[1]{0:T(128)} %bitcast), kind=kLoop, calls=%fused_computation.17 | loop fusion | flops 2 | bytes 16 | tf_op jit(solution)/shard_map/stack | solution.py:166
  25.6 4.3 %all-to-all-done = bf16[4,2,16,1536]{3,2,1,0:T(8,128)(2,1)S(1)} async-done(((bf16[4,2,16,1536]{3,2,1,0:T(8,128)(2,1)}), bf16[4,2,16,1536]{3,2,1,0:T(8,128)(2,1)S(1)}, u32[]{:S(2)}, u32[]{:S(2)}) %all-to-all-start) | async-done | bytes 393248 | tf_op jit(solution)/shard_map/all_to_all | solution.py:268
  29.9 0.8 copy.15
  30.7 10.9 %kept_backward.1 = (bf16[2,64,1536]{2,1,0:T(8,128)(2,1)}, bf16[2,2,192,1536]{3,2,1,0:T(8,128)(2,1)}, f32[3,1536]{1,0:T(4,128)}) custom-call(s32[2]{0:T(128)} %pad_add_fusion.1.meta_ref, bf16[3,192,1536]{2,1,0:T(8,128)(2,1)} %bitcast.41, bf16[2,64,1536]{2,1,0:T(8,128)(2,1)} %bitcast.34), custom_call_target="tpu_custom_call" | custom-call | flops 226492416 | bytes 2949120 | tf_op jit(solution)/shard_map/kept_backward/pallas_call | solution.py:137
  41.6 0.0 copy-start.5
  41.6 10.3 %collective-permute-done.x_ref = bf16[448,384]{1,0:T(8,128)(2,1)S(1)} collective-permute-done((bf16[448,384]{1,0:T(8,128)(2,1)}, bf16[448,384]{1,0:T(8,128)(2,1)S(1)}, u32[]{:S(2)}, u32[]{:S(2)}) %collective-permute-start) | collective-permute-done | bytes 344096 | tf_op jit(solution)/shard_map/ppermute | solution.py:20
  51.9 0.0 copy-start.4
  51.9 0.7 copy-done.4
  52.6 4.4 %held_backward.4 = (bf16[64,384]{1,0:T(8,128)(2,1)}, bf16[2,192,384]{2,1,0:T(8,128)(2,1)}, f32[3,384]{1,0:T(4,128)}) custom-call(s32[2]{0:T(128)} %pad_add_fusion.meta_ref, bf16[448,384]{1,0:T(8,128)(2,1)} %copy-done.4, bf16[2,64,1536]{2,1,0:T(8,128)(2,1)} %bitcast.35), custom_call_target="tpu_custom_call" | custom-call | flops 56623104 | bytes 737280 | tf_op jit(solution)/shard_map/held_backward/pallas_call | solution.py:167
  57.0 0.0 copy-start.6
  57.0 2.3 %collective-permute-done.2.x_ref = bf16[448,384]{1,0:T(8,128)(2,1)S(1)} collective-permute-done((bf16[448,384]{1,0:T(8,128)(2,1)S(1)}, bf16[448,384]{1,0:T(8,128)(2,1)S(1)}, u32[]{:S(2)}, u32[]{:S(2)}) %collective-permute-start.2) | collective-permute-done | bytes 344096 | tf_op jit(solution)/shard_map/ppermute | solution.py:20
  59.2 0.0 copy-start.2
  59.2 0.7 copy-done.2
  60.0 4.4 %held_backward.5 = (bf16[64,384]{1,0:T(8,128)(2,1)}, bf16[2,192,384]{2,1,0:T(8,128)(2,1)}, f32[3,384]{1,0:T(4,128)}) custom-call(s32[2]{0:T(128)} %pad_add_fusion.meta_ref, bf16[448,384]{1,0:T(8,128)(2,1)} %copy-done.2, bf16[2,64,1536]{2,1,0:T(8,128)(2,1)} %bitcast.36), custom_call_target="tpu_custom_call" | custom-call | flops 56623104 | bytes 737280 | tf_op jit(solution)/shard_map/held_backward/pallas_call | solution.py:167
  64.3 2.3 %collective-permute-done.3.x_ref = bf16[448,384]{1,0:T(8,128)(2,1)S(1)} collective-permute-done((bf16[448,384]{1,0:T(8,128)(2,1)S(1)}, bf16[448,384]{1,0:T(8,128)(2,1)S(1)}, u32[]{:S(2)}, u32[]{:S(2)}) %collective-permute-start.3) | collective-permute-done | bytes 344096 | tf_op jit(solution)/shard_map/ppermute | solution.py:20
  66.6 0.0 copy-start.1
  66.6 0.7 copy-done.1
  67.3 4.4 %held_backward.6 = (bf16[64,384]{1,0:T(8,128)(2,1)}, bf16[2,192,384]{2,1,0:T(8,128)(2,1)}, f32[3,384]{1,0:T(4,128)}) custom-call(s32[2]{0:T(128)} %pad_add_fusion.meta_ref, bf16[448,384]{1,0:T(8,128)(2,1)} %copy-done.1, bf16[2,64,1536]{2,1,0:T(8,128)(2,1)} %bitcast.37), custom_call_target="tpu_custom_call" | custom-call | flops 56623104 | bytes 737280 | tf_op jit(solution)/shard_map/held_backward/pallas_call | solution.py:167
  71.7 1.5 %collective-permute-done.4.x_ref = bf16[448,384]{1,0:T(8,128)(2,1)S(1)} collective-permute-done((bf16[448,384]{1,0:T(8,128)(2,1)S(1)}, bf16[448,384]{1,0:T(8,128)(2,1)S(1)}, u32[]{:S(2)}, u32[]{:S(2)}) %collective-permute-start.4) | collective-permute-done | bytes 344096 | tf_op jit(solution)/shard_map/ppermute | solution.py:20
  73.2 0.0 copy-start.3
  73.2 0.7 copy-done.3
  74.0 4.4 %held_backward.7 = (bf16[64,384]{1,0:T(8,128)(2,1)}, bf16[2,192,384]{2,1,0:T(8,128)(2,1)}, f32[3,384]{1,0:T(4,128)}) custom-call(s32[2]{0:T(128)} %pad_add_fusion.meta_ref, bf16[448,384]{1,0:T(8,128)(2,1)} %copy-done.3, bf16[2,64,1536]{2,1,0:T(8,128)(2,1)} %bitcast.38), custom_call_target="tpu_custom_call" | custom-call | flops 56623104 | bytes 737280 | tf_op jit(solution)/shard_map/held_backward/pallas_call | solution.py:167
  78.3 0.0 copy-done.5
  78.4 0.0 copy-done.6
  78.4 0.7 maximum_add_fusion
  79.1 1.6 %collective-permute-start.5 = (f32[3,1536]{1,0:T(4,128)S(1)}, f32[3,1536]{1,0:T(4,128)S(1)}, u32[]{:S(2)}, u32[]{:S(2)}) collective-permute-start(f32[3,1536]{1,0:T(4,128)S(1)} %maximum_add_fusion), channel_id=1, source_target_pairs={{0,16},{16,0},{1,17},{17,1},{2,18},{18,2},{3,19},{19,3},{4,20},{20... | collective-permute-start | bytes 55304 | tf_op jit(solution)/shard_map/ppermute | solution.py:20
  80.7 2.5 %assemble_held.1 = (bf16[2,64,1536]{2,1,0:T(8,128)(2,1)}, bf16[2,2,192,1536]{3,2,1,0:T(8,128)(2,1)}) custom-call(bf16[64,384]{1,0:T(8,128)(2,1)} %get-tuple-element.28.refs_0_, bf16[64,384]{1,0:T(8,128)(2,1)} %get-tuple-element.29.refs_1_, bf16[64,384]{1,0:T(8,128)(2,1)} %get-tuple-element.30.refs_2_, ...), custom_call_target="tpu_custom_call", output_to_operand_aliasing={{0}: (8, {}), {1}: (9, {})} | custom-call | bytes 2752512 | tf_op jit(solution)/shard_map/assemble_held/pallas_call | solution.py:200
  83.2 0.0 collective-permute-done.5
  83.2 0.6 copy.16
  (5 shorter events, 0.1 us)
Async XLA Ops:
  0.6 9.6 %copy-start = (bf16[1,1,3,192,1536]{4,3,2,1,0:T(8,128)(2,1)S(1)}, bf16[1,1,3,192,1536]{4,3,2,1,0:T(8,128)(2,1)}, u32[]{:S(2)}) copy-start(bf16[1,1,3,192,1536]{4,3,2,1,0:T(8,128)(2,1)} %param.6) | copy-start | bytes 5308420
  0.6 17.3 %collective-permute-start.1 = (bf16[2,16,6144]{2,1,0:T(8,128)(2,1)}, bf16[2,16,6144]{2,1,0:T(8,128)(2,1)S(1)}, u32[]{:S(2)}, u32[]{:S(2)}) collective-permute-start(bf16[2,16,6144]{2,1,0:T(8,128)(2,1)} %bitcast.45), channel_id=1, source_target_pairs={{0,12},{4,0},{8,4},{12,8},{1,13},{5,1},{9,5},{13,9},{2,14},{6,2},{... | collective-permute-start | bytes 1179656 | tf_op jit(solution)/shard_map/ppermute | solution.py:20
  11.2 40.7 %collective-permute-start = (bf16[448,384]{1,0:T(8,128)(2,1)}, bf16[448,384]{1,0:T(8,128)(2,1)S(1)}, u32[]{:S(2)}, u32[]{:S(2)}) collective-permute-start(bf16[448,384]{1,0:T(8,128)(2,1)} %pad_maximum_fusion), channel_id=1, source_target_pairs={{0,8},{4,12},{8,0},{12,4},{1,9},{5,13},{9,1},{13,5},{2,10},{6,14},... | collective-permute-start | bytes 1032200 | tf_op jit(solution)/shard_map/ppermute | solution.py:20
  11.2 48.0 %collective-permute-start.2 = (bf16[448,384]{1,0:T(8,128)(2,1)S(1)}, bf16[448,384]{1,0:T(8,128)(2,1)S(1)}, u32[]{:S(2)}, u32[]{:S(2)}) collective-permute-start(bf16[448,384]{1,0:T(8,128)(2,1)S(1)} %pad_maximum_fusion.1), channel_id=1, source_target_pairs={{0,8},{4,12},{8,0},{12,4},{1,9},{5,13},{9,1},{13,5},{2,10},{6,14},... | collective-permute-start | bytes 1032200 | tf_op jit(solution)/shard_map/ppermute | solution.py:20
  14.2 52.4 %collective-permute-start.3 = (bf16[448,384]{1,0:T(8,128)(2,1)S(1)}, bf16[448,384]{1,0:T(8,128)(2,1)S(1)}, u32[]{:S(2)}, u32[]{:S(2)}) collective-permute-start(bf16[448,384]{1,0:T(8,128)(2,1)S(1)} %pad_maximum_fusion.2), channel_id=1, source_target_pairs={{0,8},{4,12},{8,0},{12,4},{1,9},{5,13},{9,1},{13,5},{2,10},{6,14},... | collective-permute-start | bytes 1032200 | tf_op jit(solution)/shard_map/ppermute | solution.py:20
  14.3 58.9 %collective-permute-start.4 = (bf16[448,384]{1,0:T(8,128)(2,1)S(1)}, bf16[448,384]{1,0:T(8,128)(2,1)S(1)}, u32[]{:S(2)}, u32[]{:S(2)}) collective-permute-start(bf16[448,384]{1,0:T(8,128)(2,1)S(1)} %pad_maximum_fusion.3), channel_id=1, source_target_pairs={{0,8},{4,12},{8,0},{12,4},{1,9},{5,13},{9,1},{13,5},{2,10},{6,14},... | collective-permute-start | bytes 1032200 | tf_op jit(solution)/shard_map/ppermute | solution.py:20
  19.1 10.9 %all-to-all-start = ((bf16[4,2,16,1536]{3,2,1,0:T(8,128)(2,1)}), bf16[4,2,16,1536]{3,2,1,0:T(8,128)(2,1)S(1)}, u32[]{:S(2)}, u32[]{:S(2)}) async-start(bf16[4,2,16,1536]{3,2,1,0:T(8,128)(2,1)} %copy.14), calls=%async_computation | async-start | bytes 786432 | tf_op jit(solution)/shard_map/all_to_all | solution.py:268
  41.6 36.7 %copy-start.5 = (f32[3,1536]{1,0:T(4,128)S(1)}, f32[3,1536]{1,0:T(4,128)}, u32[]{:S(2)}) copy-start(f32[3,1536]{1,0:T(4,128)} %get-tuple-element.40) | copy-start | bytes 55300
  51.9 0.7 copy-start.4
  57.0 21.4 %copy-start.6 = (f32[3,384]{1,0:T(4,128)S(1)}, f32[3,384]{1,0:T(4,128)}, u32[]{:S(2)}) copy-start(f32[3,384]{1,0:T(4,128)} %get-tuple-element.41) | copy-start | bytes 13828
  59.2 0.7 copy-start.2
  66.6 0.7 copy-start.1
  73.2 0.7 copy-start.3
  79.1 4.1 %collective-permute-start.5 = (f32[3,1536]{1,0:T(4,128)S(1)}, f32[3,1536]{1,0:T(4,128)S(1)}, u32[]{:S(2)}, u32[]{:S(2)}) collective-permute-start(f32[3,1536]{1,0:T(4,128)S(1)} %maximum_add_fusion), channel_id=1, source_target_pairs={{0,16},{16,0},{1,17},{17,1},{2,18},{18,2},{3,19},{19,3},{4,20},{20... | collective-permute-start | bytes 55304 | tf_op jit(solution)/shard_map/ppermute | solution.py:20

commit v12 on v11

--- a/solution.py
+++ b/solution.py
@@ -150,17 +150,18 @@
     chunk = lo // width
     keys = (part.shape[0] - rows) // 2
     bf16 = jnp.bfloat16
+    first = lo // HD
     grid_spec = pltpu.PrefetchScalarGridSpec(
         num_scalar_prefetch=1,
-        grid=(1,),
+        grid=(width // HD,),
         in_specs=[
-            pl.BlockSpec((part.shape[0], width), lambda i, m: (0, 0)),
-            pl.BlockSpec((None, rows, width), lambda i, m: (m[1], 0, chunk)),
+            pl.BlockSpec((part.shape[0], HD), lambda i, m: (0, i)),
+            pl.BlockSpec((None, rows, HD), lambda i, m: (m[1], 0, first + i)),
         ],
         out_specs=(
-            pl.BlockSpec((rows, width), lambda i, m: (0, 0)),
-            pl.BlockSpec((2, keys, width), lambda i, m: (0, 0, 0)),
-            pl.BlockSpec((3, width), lambda i, m: (0, 0)),
+            pl.BlockSpec((rows, HD), lambda i, m: (0, i)),
+            pl.BlockSpec((2, keys, HD), lambda i, m: (0, 0, i)),
+            pl.BlockSpec((3, HD), lambda i, m: (0, i)),
         ),
     )
     meta = jnp.stack([offset, 1 - pick]).astype(jnp.int32)

time: 84.4 us -> 84.8 us (level)
  Pallas kernels: 30.9 us -> 32.1 us
  waiting for transfers between devices: 20.7 us -> 19.8 us
    pallas_call x4, Pallas kernels: 17.5 us -> 18.7 us  [held_backward(): pl.pallas_call(held_kernel, out_shape=(jax.ShapeDtypeStruct((rows, width)...]
    ppermute x6, waiting for transfers between devices: 16.3 us -> 15.4 us  [from_behind(): return lax.ppermute(value, axis, pairs)]
  transfers between devices with their start and end apart: 7 -> 7, of which waited for: 5 -> 5; matrix products, arithmetic and copies ran while one was open for 10% -> 10% of each run, Pallas kernels for 32% -> 33%
where the time goes in v12:
time: 84.8 us; the launch traced here: 84.1 us
  Pallas kernels  32.1 us (38%)
  waiting for transfers between devices  19.8 us (23%)
  starting transfers between devices  16.2 us (19%)
  local copies, waits for them, and re-layouts  8.62 us (10%)
  other arithmetic  4.14 us (5%)
  between operations  3.33 us (4%)
    pallas_call x4, Pallas kernels, held_backward(): pl.pallas_call(held_kernel, out_shape=(jax.ShapeDtypeStruct((rows, width)...  18.7 us
    ppermute x6, waiting for transfers between devices, from_behind(): return lax.ppermute(value, axis, pairs)  15.4 us
    ppermute x6, starting transfers between devices, from_behind(): return lax.ppermute(value, axis, pairs)  12.7 us
    pallas_call x1, Pallas kernels, kept_backward(): pl.pallas_call(kept_kernel, out_shape=out_shape, grid_spec=grid_spec, cos...  10.9 us
    all_to_all x1, waiting for transfers between devices, body(): lax.all_to_all(split, 'tensor', split_axis=0, concat_axis=0, tiled=True)  4.34 us
    unnamed x15, local copies, waits for them, and re-layouts  3.55 us
    all_to_all x1, starting transfers between devices, body(): lax.all_to_all(split, 'tensor', split_axis=0, concat_axis=0, tiled=True)  3.46 us
    pallas_call x1, Pallas kernels, assemble(): pl.pallas_call(functools.partial(assemble_kernel, tuple(bounds)), out_sha...  2.51 us
  transfers between devices with their start and end apart: 7, of which 5 were waited for; matrix products, arithmetic and copies ran while one was open for 10% of the time, Pallas kernels for 33%

profile of v12, /device:TPU:0, one launch (start us, length us, event | category | flops | bytes accessed | tf_op | source)
XLA Modules:
  0.0 84.1 jit_solution(16138211427509699386)
XLA Ops:
  0.6 0.0 copy-start
  0.6 5.1 %collective-permute-start.1 = (bf16[2,16,6144]{2,1,0:T(8,128)(2,1)}, bf16[2,16,6144]{2,1,0:T(8,128)(2,1)S(1)}, u32[]{:S(2)}, u32[]{:S(2)}) collective-permute-start(bf16[2,16,6144]{2,1,0:T(8,128)(2,1)} %bitcast.45), channel_id=1, source_target_pairs={{0,12},{4,0},{8,4},{12,8},{1,13},{5,1},{9,5},{13,9},{2,14},{6,2},{... | collective-permute-start | bytes 1179656 | tf_op jit(solution)/shard_map/ppermute | solution.py:20
  5.7 0.8 constant_dynamic-slice_fusion
  6.6 0.5 slice.62
  8.4 1.1 %slice.61 = bf16[1,1,1,192,1536]{4,3,2,1,0:T(8,128)(2,1)S(1)} slice(bf16[1,1,3,192,1536]{4,3,2,1,0:T(8,128)(2,1)} %param.6), slice={[0:1], [0:1], [0:1], [0:192], [0:1536]} | slice | bytes 1179648 | tf_op jit(solution)/shard_map/slice | solution.py:258
  10.1 0.1 dynamic-slice_bitcast_fusion
  10.2 0.0 copy-done
  10.2 0.1 slice_bitcast_fusion.1
  10.4 0.8 pad_maximum_fusion
  11.2 0.0 collective-permute-start
  11.2 3.0 %collective-permute-start.2 = (bf16[448,384]{1,0:T(8,128)(2,1)S(1)}, bf16[448,384]{1,0:T(8,128)(2,1)S(1)}, u32[]{:S(2)}, u32[]{:S(2)}) collective-permute-start(bf16[448,384]{1,0:T(8,128)(2,1)S(1)} %pad_maximum_fusion.1), channel_id=1, source_target_pairs={{0,8},{4,12},{8,0},{12,4},{1,9},{5,13},{9,1},{13,5},{2,10},{6,14},... | collective-permute-start | bytes 1032200 | tf_op jit(solution)/shard_map/ppermute | solution.py:20
  14.2 0.1 collective-permute-start.3
  14.3 3.0 %collective-permute-start.4 = (bf16[448,384]{1,0:T(8,128)(2,1)S(1)}, bf16[448,384]{1,0:T(8,128)(2,1)S(1)}, u32[]{:S(2)}, u32[]{:S(2)}) collective-permute-start(bf16[448,384]{1,0:T(8,128)(2,1)S(1)} %pad_maximum_fusion.3), channel_id=1, source_target_pairs={{0,8},{4,12},{8,0},{12,4},{1,9},{5,13},{9,1},{13,5},{2,10},{6,14},... | collective-permute-start | bytes 1032200 | tf_op jit(solution)/shard_map/ppermute | solution.py:20
  18.0 0.0 collective-permute-done.1
  18.0 0.3 reshape.26
  18.3 0.8 copy.14
  19.1 3.5 %all-to-all-start = ((bf16[4,2,16,1536]{3,2,1,0:T(8,128)(2,1)}), bf16[4,2,16,1536]{3,2,1,0:T(8,128)(2,1)S(1)}, u32[]{:S(2)}, u32[]{:S(2)}) async-start(bf16[4,2,16,1536]{3,2,1,0:T(8,128)(2,1)} %copy.14), calls=%async_computation | async-start | bytes 786432 | tf_op jit(solution)/shard_map/all_to_all | solution.py:269
  22.5 0.5 fusion.1
  23.1 1.2 %pad_add_fusion.1.meta_ref = s32[2]{0:T(128)} fusion(s32[1]{0:T(128)} %bitcast.33, s32[1]{0:T(128)} %bitcast.7), kind=kLoop, calls=%fused_computation.18 | loop fusion | flops 2 | bytes 16 | tf_op jit(solution)/shard_map/stack | solution.py:136
  24.3 1.3 %pad_add_fusion.meta_ref = s32[2]{0:T(128)} fusion(s32[1]{0:T(128)} %bitcast.1, s32[1]{0:T(128)} %bitcast), kind=kLoop, calls=%fused_computation.17 | loop fusion | flops 2 | bytes 16 | tf_op jit(solution)/shard_map/stack | solution.py:167
  25.6 4.3 %all-to-all-done = bf16[4,2,16,1536]{3,2,1,0:T(8,128)(2,1)S(1)} async-done(((bf16[4,2,16,1536]{3,2,1,0:T(8,128)(2,1)}), bf16[4,2,16,1536]{3,2,1,0:T(8,128)(2,1)S(1)}, u32[]{:S(2)}, u32[]{:S(2)}) %all-to-all-start) | async-done | bytes 393248 | tf_op jit(solution)/shard_map/all_to_all | solution.py:269
  29.9 0.8 copy.15
  30.7 10.9 %kept_backward.1 = (bf16[2,64,1536]{2,1,0:T(8,128)(2,1)}, bf16[2,2,192,1536]{3,2,1,0:T(8,128)(2,1)}, f32[3,1536]{1,0:T(4,128)}) custom-call(s32[2]{0:T(128)} %pad_add_fusion.1.meta_ref, bf16[3,192,1536]{2,1,0:T(8,128)(2,1)} %bitcast.41, bf16[2,64,1536]{2,1,0:T(8,128)(2,1)} %bitcast.34), custom_call_target="tpu_custom_call" | custom-call | flops 226492416 | bytes 2949120 | tf_op jit(solution)/shard_map/kept_backward/pallas_call | solution.py:137
  41.6 0.0 copy-start.5
  41.6 10.3 %collective-permute-done.x_ref = bf16[448,384]{1,0:T(8,128)(2,1)S(1)} collective-permute-done((bf16[448,384]{1,0:T(8,128)(2,1)}, bf16[448,384]{1,0:T(8,128)(2,1)S(1)}, u32[]{:S(2)}, u32[]{:S(2)}) %collective-permute-start) | collective-permute-done | bytes 344096 | tf_op jit(solution)/shard_map/ppermute | solution.py:20
  51.9 0.0 copy-start.4
  51.9 0.7 copy-done.4
  52.6 4.7 %held_backward.4 = (bf16[64,384]{1,0:T(8,128)(2,1)}, bf16[2,192,384]{2,1,0:T(8,128)(2,1)}, f32[3,384]{1,0:T(4,128)}) custom-call(s32[2]{0:T(128)} %pad_add_fusion.meta_ref, bf16[448,384]{1,0:T(8,128)(2,1)} %copy-done.4, bf16[2,64,1536]{2,1,0:T(8,128)(2,1)} %bitcast.35), custom_call_target="tpu_custom_call" | custom-call | flops 56623104 | bytes 737280 | tf_op jit(solution)/shard_map/held_backward/pallas_call | solution.py:168
  57.3 0.0 copy-start.6
  57.3 2.0 %collective-permute-done.2.x_ref = bf16[448,384]{1,0:T(8,128)(2,1)S(1)} collective-permute-done((bf16[448,384]{1,0:T(8,128)(2,1)S(1)}, bf16[448,384]{1,0:T(8,128)(2,1)S(1)}, u32[]{:S(2)}, u32[]{:S(2)}) %collective-permute-start.2) | collective-permute-done | bytes 344096 | tf_op jit(solution)/shard_map/ppermute | solution.py:20
  59.2 0.0 copy-start.2
  59.2 0.7 copy-done.2
  60.0 4.7 %held_backward.5 = (bf16[64,384]{1,0:T(8,128)(2,1)}, bf16[2,192,384]{2,1,0:T(8,128)(2,1)}, f32[3,384]{1,0:T(4,128)}) custom-call(s32[2]{0:T(128)} %pad_add_fusion.meta_ref, bf16[448,384]{1,0:T(8,128)(2,1)} %copy-done.2, bf16[2,64,1536]{2,1,0:T(8,128)(2,1)} %bitcast.36), custom_call_target="tpu_custom_call" | custom-call | flops 56623104 | bytes 737280 | tf_op jit(solution)/shard_map/held_backward/pallas_call | solution.py:168
  64.6 2.0 %collective-permute-done.3.x_ref = bf16[448,384]{1,0:T(8,128)(2,1)S(1)} collective-permute-done((bf16[448,384]{1,0:T(8,128)(2,1)S(1)}, bf16[448,384]{1,0:T(8,128)(2,1)S(1)}, u32[]{:S(2)}, u32[]{:S(2)}) %collective-permute-start.3) | collective-permute-done | bytes 344096 | tf_op jit(solution)/shard_map/ppermute | solution.py:20
  66.6 0.0 copy-start.1
  66.6 0.7 copy-done.1
  67.3 4.7 %held_backward.6 = (bf16[64,384]{1,0:T(8,128)(2,1)}, bf16[2,192,384]{2,1,0:T(8,128)(2,1)}, f32[3,384]{1,0:T(4,128)}) custom-call(s32[2]{0:T(128)} %pad_add_fusion.meta_ref, bf16[448,384]{1,0:T(8,128)(2,1)} %copy-done.1, bf16[2,64,1536]{2,1,0:T(8,128)(2,1)} %bitcast.37), custom_call_target="tpu_custom_call" | custom-call | flops 56623104 | bytes 737280 | tf_op jit(solution)/shard_map/held_backward/pallas_call | solution.py:168
  72.0 1.2 %collective-permute-done.4.x_ref = bf16[448,384]{1,0:T(8,128)(2,1)S(1)} collective-permute-done((bf16[448,384]{1,0:T(8,128)(2,1)S(1)}, bf16[448,384]{1,0:T(8,128)(2,1)S(1)}, u32[]{:S(2)}, u32[]{:S(2)}) %collective-permute-start.4) | collective-permute-done | bytes 344096 | tf_op jit(solution)/shard_map/ppermute | solution.py:20
  73.2 0.0 copy-start.3
  73.2 0.7 copy-done.3
  74.0 4.7 %held_backward.7 = (bf16[64,384]{1,0:T(8,128)(2,1)}, bf16[2,192,384]{2,1,0:T(8,128)(2,1)}, f32[3,384]{1,0:T(4,128)}) custom-call(s32[2]{0:T(128)} %pad_add_fusion.meta_ref, bf16[448,384]{1,0:T(8,128)(2,1)} %copy-done.3, bf16[2,64,1536]{2,1,0:T(8,128)(2,1)} %bitcast.38), custom_call_target="tpu_custom_call" | custom-call | flops 56623104 | bytes 737280 | tf_op jit(solution)/shard_map/held_backward/pallas_call | solution.py:168
  78.6 0.0 copy-done.5
  78.6 0.0 copy-done.6
  78.6 0.7 maximum_add_fusion
  79.4 1.6 %collective-permute-start.5 = (f32[3,1536]{1,0:T(4,128)S(1)}, f32[3,1536]{1,0:T(4,128)S(1)}, u32[]{:S(2)}, u32[]{:S(2)}) collective-permute-start(f32[3,1536]{1,0:T(4,128)S(1)} %maximum_add_fusion), channel_id=1, source_target_pairs={{0,16},{16,0},{1,17},{17,1},{2,18},{18,2},{3,19},{19,3},{4,20},{20... | collective-permute-start | bytes 55304 | tf_op jit(solution)/shard_map/ppermute | solution.py:20
  81.0 2.5 %assemble_held.1 = (bf16[2,64,1536]{2,1,0:T(8,128)(2,1)}, bf16[2,2,192,1536]{3,2,1,0:T(8,128)(2,1)}) custom-call(bf16[64,384]{1,0:T(8,128)(2,1)} %get-tuple-element.28.refs_0_, bf16[64,384]{1,0:T(8,128)(2,1)} %get-tuple-element.29.refs_1_, bf16[64,384]{1,0:T(8,128)(2,1)} %get-tuple-element.30.refs_2_, ...), custom_call_target="tpu_custom_call", output_to_operand_aliasing={{0}: (8, {}), {1}: (9, {})} | custom-call | bytes 2752512 | tf_op jit(solution)/shard_map/assemble_held/pallas_call | solution.py:201
  83.5 0.0 collective-permute-done.5
  83.5 0.6 copy.16
  (5 shorter events, 0.1 us)
Async XLA Ops:
  0.6 9.6 %copy-start = (bf16[1,1,3,192,1536]{4,3,2,1,0:T(8,128)(2,1)S(1)}, bf16[1,1,3,192,1536]{4,3,2,1,0:T(8,128)(2,1)}, u32[]{:S(2)}) copy-start(bf16[1,1,3,192,1536]{4,3,2,1,0:T(8,128)(2,1)} %param.6) | copy-start | bytes 5308420
  0.6 17.3 %collective-permute-start.1 = (bf16[2,16,6144]{2,1,0:T(8,128)(2,1)}, bf16[2,16,6144]{2,1,0:T(8,128)(2,1)S(1)}, u32[]{:S(2)}, u32[]{:S(2)}) collective-permute-start(bf16[2,16,6144]{2,1,0:T(8,128)(2,1)} %bitcast.45), channel_id=1, source_target_pairs={{0,12},{4,0},{8,4},{12,8},{1,13},{5,1},{9,5},{13,9},{2,14},{6,2},{... | collective-permute-start | bytes 1179656 | tf_op jit(solution)/shard_map/ppermute | solution.py:20
  11.2 40.7 %collective-permute-start = (bf16[448,384]{1,0:T(8,128)(2,1)}, bf16[448,384]{1,0:T(8,128)(2,1)S(1)}, u32[]{:S(2)}, u32[]{:S(2)}) collective-permute-start(bf16[448,384]{1,0:T(8,128)(2,1)} %pad_maximum_fusion), channel_id=1, source_target_pairs={{0,8},{4,12},{8,0},{12,4},{1,9},{5,13},{9,1},{13,5},{2,10},{6,14},... | collective-permute-start | bytes 1032200 | tf_op jit(solution)/shard_map/ppermute | solution.py:20
  11.2 48.0 %collective-permute-start.2 = (bf16[448,384]{1,0:T(8,128)(2,1)S(1)}, bf16[448,384]{1,0:T(8,128)(2,1)S(1)}, u32[]{:S(2)}, u32[]{:S(2)}) collective-permute-start(bf16[448,384]{1,0:T(8,128)(2,1)S(1)} %pad_maximum_fusion.1), channel_id=1, source_target_pairs={{0,8},{4,12},{8,0},{12,4},{1,9},{5,13},{9,1},{13,5},{2,10},{6,14},... | collective-permute-start | bytes 1032200 | tf_op jit(solution)/shard_map/ppermute | solution.py:20
  14.2 52.4 %collective-permute-start.3 = (bf16[448,384]{1,0:T(8,128)(2,1)S(1)}, bf16[448,384]{1,0:T(8,128)(2,1)S(1)}, u32[]{:S(2)}, u32[]{:S(2)}) collective-permute-start(bf16[448,384]{1,0:T(8,128)(2,1)S(1)} %pad_maximum_fusion.2), channel_id=1, source_target_pairs={{0,8},{4,12},{8,0},{12,4},{1,9},{5,13},{9,1},{13,5},{2,10},{6,14},... | collective-permute-start | bytes 1032200 | tf_op jit(solution)/shard_map/ppermute | solution.py:20
  14.3 58.9 %collective-permute-start.4 = (bf16[448,384]{1,0:T(8,128)(2,1)S(1)}, bf16[448,384]{1,0:T(8,128)(2,1)S(1)}, u32[]{:S(2)}, u32[]{:S(2)}) collective-permute-start(bf16[448,384]{1,0:T(8,128)(2,1)S(1)} %pad_maximum_fusion.3), channel_id=1, source_target_pairs={{0,8},{4,12},{8,0},{12,4},{1,9},{5,13},{9,1},{13,5},{2,10},{6,14},... | collective-permute-start | bytes 1032200 | tf_op jit(solution)/shard_map/ppermute | solution.py:20
  19.1 10.9 %all-to-all-start = ((bf16[4,2,16,1536]{3,2,1,0:T(8,128)(2,1)}), bf16[4,2,16,1536]{3,2,1,0:T(8,128)(2,1)S(1)}, u32[]{:S(2)}, u32[]{:S(2)}) async-start(bf16[4,2,16,1536]{3,2,1,0:T(8,128)(2,1)} %copy.14), calls=%async_computation | async-start | bytes 786432 | tf_op jit(solution)/shard_map/all_to_all | solution.py:269
  41.6 37.0 %copy-start.5 = (f32[3,1536]{1,0:T(4,128)S(1)}, f32[3,1536]{1,0:T(4,128)}, u32[]{:S(2)}) copy-start(f32[3,1536]{1,0:T(4,128)} %get-tuple-element.40) | copy-start | bytes 55300
  51.9 0.7 copy-start.4
  57.3 21.4 %copy-start.6 = (f32[3,384]{1,0:T(4,128)S(1)}, f32[3,384]{1,0:T(4,128)}, u32[]{:S(2)}) copy-start(f32[3,384]{1,0:T(4,128)} %get-tuple-element.41) | copy-start | bytes 13828
  59.2 0.7 copy-start.2
  66.6 0.7 copy-start.1
  73.2 0.7 copy-start.3
  79.4 4.1 %collective-permute-start.5 = (f32[3,1536]{1,0:T(4,128)S(1)}, f32[3,1536]{1,0:T(4,128)S(1)}, u32[]{:S(2)}, u32[]{:S(2)}) collective-permute-start(f32[3,1536]{1,0:T(4,128)S(1)} %maximum_add_fusion), channel_id=1, source_target_pairs={{0,16},{16,0},{1,17},{17,1},{2,18},{18,2},{3,19},{19,3},{4,20},{20... | collective-permute-start | bytes 55304 | tf_op jit(solution)/shard_map/ppermute | solution.py:20

commit v13 on v11

--- a/solution.py
+++ b/solution.py
@@ -180,36 +180,33 @@
 def assemble_kernel(bounds, *refs):
     count = len(bounds)
     q_parts, kv_parts = refs[:count], refs[count:2 * count]
-    qg_ref, kv_ref = refs[2 * count + 2:]
+    qg_ref, kv_ref, sems = refs[2 * count + 2:]
+    copies = []
     for c, (lo, hi) in enumerate(bounds):
-        qg_ref[:, lo:hi] = q_parts[c][...]
-        kv_ref[:, :, lo:hi] = kv_parts[c][...]
+        cols = pl.ds(lo, hi - lo)
+        copies.append(pltpu.make_async_copy(q_parts[c], qg_ref.at[1, :, cols], sems.at[2 * c]))
+        copies.append(pltpu.make_async_copy(kv_parts[c], kv_ref.at[1, :, :, cols], sems.at[2 * c + 1]))
+    for copy in copies:
+        copy.start()
+    for copy in copies:
+        copy.wait()
 
 
 def assemble(bounds, held_parts, qg, kv):
     rows, feats = qg.shape[1], qg.shape[2]
     keys = kv.shape[2]
-    whole = lambda shape: pl.BlockSpec(shape, lambda i: (0,) * len(shape))
-    in_specs = (
-        [whole(part[0].shape) for part in held_parts]
-        + [whole(part[1].shape) for part in held_parts]
-        + [pl.BlockSpec(memory_space=pl.ANY), pl.BlockSpec(memory_space=pl.ANY)]
-    )
     count = len(held_parts)
-    first_alias = 2 * count
+    anywhere = pl.BlockSpec(memory_space=pl.ANY)
     return pl.pallas_call(
         functools.partial(assemble_kernel, tuple(bounds)),
         out_shape=(
             jax.ShapeDtypeStruct(qg.shape, qg.dtype),
             jax.ShapeDtypeStruct(kv.shape, kv.dtype),
         ),
-        grid=(1,),
-        in_specs=in_specs,
-        out_specs=(
-            pl.BlockSpec((None, rows, feats), lambda i: (1, 0, 0)),
-            pl.BlockSpec((None, 2, keys, feats), lambda i: (1, 0, 0, 0)),
-        ),
-        input_output_aliases={first_alias: 0, first_alias + 1: 1},
+        in_specs=[anywhere] * (2 * count + 2),
+        out_specs=(anywhere, anywhere),
+        scratch_shapes=[pltpu.SemaphoreType.DMA((2 * count,))],
+        input_output_aliases={2 * count: 0, 2 * count + 1: 1},
         cost_estimate=pl.CostEstimate(flops=0, transcendentals=0, bytes_accessed=4 * feats * (rows + 2 * keys)),
         name="assemble_held",
     )(*[p[0] for p in held_parts], *[p[1] for p in held_parts], qg, kv)

time: 84.4 us -> 125 us (1.48)
  Pallas kernels: 30.9 us -> 71.2 us
    pallas_call x1, Pallas kernels: 2.51 us -> 42.9 us  [assemble(): pl.pallas_call(functools.partial(assemble_kernel, tuple(bounds)), out_sha...]
  transfers between devices with their start and end apart: 7 -> 7, of which waited for: 5 -> 5; matrix products, arithmetic and copies ran while one was open for 10% -> 7% of each run, Pallas kernels for 32% -> 54%
where the time goes in v13:
time: 125 us; the launch traced here: 124 us
  Pallas kernels  71.2 us (57%)
  waiting for transfers between devices  20.7 us (17%)
  starting transfers between devices  16.2 us (13%)
  local copies, waits for them, and re-layouts  8.62 us (7%)
  other arithmetic  4.14 us (3%)
  between operations  3.35 us (3%)
    pallas_call x1, Pallas kernels, assemble(): pl.pallas_call(functools.partial(assemble_kernel, tuple(bounds)), out_sha...  42.9 us
    pallas_call x4, Pallas kernels, held_backward(): pl.pallas_call(held_kernel, out_shape=(jax.ShapeDtypeStruct((rows, width)...  17.5 us
    ppermute x6, waiting for transfers between devices, from_behind(): return lax.ppermute(value, axis, pairs)  16.3 us
    ppermute x6, starting transfers between devices, from_behind(): return lax.ppermute(value, axis, pairs)  12.7 us
    pallas_call x1, Pallas kernels, kept_backward(): pl.pallas_call(kept_kernel, out_shape=out_shape, grid_spec=grid_spec, cos...  10.9 us
    all_to_all x1, waiting for transfers between devices, body(): lax.all_to_all(split, 'tensor', split_axis=0, concat_axis=0, tiled=True)  4.34 us
    unnamed x15, local copies, waits for them, and re-layouts  3.55 us
    all_to_all x1, starting transfers between devices, body(): lax.all_to_all(split, 'tensor', split_axis=0, concat_axis=0, tiled=True)  3.46 us
  transfers between devices with their start and end apart: 7, of which 5 were waited for; matrix products, arithmetic and copies ran while one was open for 7% of the time, Pallas kernels for 54%

profile of v13, /device:TPU:0, one launch (start us, length us, event | category | flops | bytes accessed | tf_op | source)
XLA Modules:
  0.0 124.2 jit_solution(17551268785368303983)
XLA Ops:
  0.6 0.0 copy-start
  0.6 5.1 %collective-permute-start.1 = (bf16[2,16,6144]{2,1,0:T(8,128)(2,1)}, bf16[2,16,6144]{2,1,0:T(8,128)(2,1)S(1)}, u32[]{:S(2)}, u32[]{:S(2)}) collective-permute-start(bf16[2,16,6144]{2,1,0:T(8,128)(2,1)} %bitcast.45), channel_id=1, source_target_pairs={{0,12},{4,0},{8,4},{12,8},{1,13},{5,1},{9,5},{13,9},{2,14},{6,2},{... | collective-permute-start | bytes 1179656 | tf_op jit(solution)/shard_map/ppermute | solution.py:20
  5.7 0.8 constant_dynamic-slice_fusion
  6.6 0.5 slice.62
  8.4 1.1 slice.61
  10.1 0.1 dynamic-slice_bitcast_fusion
  10.2 0.0 copy-done
  10.2 0.1 slice_bitcast_fusion.1
  10.4 0.8 pad_maximum_fusion
  11.2 0.0 collective-permute-start
  11.2 3.0 %collective-permute-start.2 = (bf16[448,384]{1,0:T(8,128)(2,1)S(1)}, bf16[448,384]{1,0:T(8,128)(2,1)S(1)}, u32[]{:S(2)}, u32[]{:S(2)}) collective-permute-start(bf16[448,384]{1,0:T(8,128)(2,1)S(1)} %pad_maximum_fusion.1), channel_id=1, source_target_pairs={{0,8},{4,12},{8,0},{12,4},{1,9},{5,13},{9,1},{13,5},{2,10},{6,14},... | collective-permute-start | bytes 1032200 | tf_op jit(solution)/shard_map/ppermute | solution.py:20
  14.2 0.1 collective-permute-start.3
  14.3 3.0 %collective-permute-start.4 = (bf16[448,384]{1,0:T(8,128)(2,1)S(1)}, bf16[448,384]{1,0:T(8,128)(2,1)S(1)}, u32[]{:S(2)}, u32[]{:S(2)}) collective-permute-start(bf16[448,384]{1,0:T(8,128)(2,1)S(1)} %pad_maximum_fusion.3), channel_id=1, source_target_pairs={{0,8},{4,12},{8,0},{12,4},{1,9},{5,13},{9,1},{13,5},{2,10},{6,14},... | collective-permute-start | bytes 1032200 | tf_op jit(solution)/shard_map/ppermute | solution.py:20
  18.0 0.0 collective-permute-done.1
  18.0 0.3 reshape.26
  18.3 0.8 copy.14
  19.1 3.5 %all-to-all-start = ((bf16[4,2,16,1536]{3,2,1,0:T(8,128)(2,1)}), bf16[4,2,16,1536]{3,2,1,0:T(8,128)(2,1)S(1)}, u32[]{:S(2)}, u32[]{:S(2)}) async-start(bf16[4,2,16,1536]{3,2,1,0:T(8,128)(2,1)} %copy.14), calls=%async_computation | async-start | bytes 786432 | tf_op jit(solution)/shard_map/all_to_all | solution.py:265
  22.5 0.5 fusion.1
  23.1 1.2 pad_add_fusion.1.meta_ref
  24.3 1.3 %pad_add_fusion.meta_ref = s32[2]{0:T(128)} fusion(s32[1]{0:T(128)} %bitcast.1, s32[1]{0:T(128)} %bitcast), kind=kLoop, calls=%fused_computation.17 | loop fusion | flops 2 | bytes 16 | tf_op jit(solution)/shard_map/stack | solution.py:166
  25.6 4.3 %all-to-all-done = bf16[4,2,16,1536]{3,2,1,0:T(8,128)(2,1)S(1)} async-done(((bf16[4,2,16,1536]{3,2,1,0:T(8,128)(2,1)}), bf16[4,2,16,1536]{3,2,1,0:T(8,128)(2,1)S(1)}, u32[]{:S(2)}, u32[]{:S(2)}) %all-to-all-start) | async-done | bytes 393248 | tf_op jit(solution)/shard_map/all_to_all | solution.py:265
  29.9 0.8 copy.15
  30.7 10.9 %kept_backward.1 = (bf16[2,64,1536]{2,1,0:T(8,128)(2,1)}, bf16[2,2,192,1536]{3,2,1,0:T(8,128)(2,1)}, f32[3,1536]{1,0:T(4,128)}) custom-call(s32[2]{0:T(128)} %pad_add_fusion.1.meta_ref, bf16[3,192,1536]{2,1,0:T(8,128)(2,1)} %bitcast.41, bf16[2,64,1536]{2,1,0:T(8,128)(2,1)} %bitcast.34), custom_call_target="tpu_custom_call" | custom-call | flops 226492416 | bytes 2949120 | tf_op jit(solution)/shard_map/kept_backward/pallas_call | solution.py:137
  41.6 0.0 copy-start.5
  41.6 10.3 %collective-permute-done.x_ref = bf16[448,384]{1,0:T(8,128)(2,1)S(1)} collective-permute-done((bf16[448,384]{1,0:T(8,128)(2,1)}, bf16[448,384]{1,0:T(8,128)(2,1)S(1)}, u32[]{:S(2)}, u32[]{:S(2)}) %collective-permute-start) | collective-permute-done | bytes 344096 | tf_op jit(solution)/shard_map/ppermute | solution.py:20
  51.9 0.0 copy-start.4
  51.9 0.7 copy-done.4
  52.6 4.4 %held_backward.4 = (bf16[64,384]{1,0:T(8,128)(2,1)}, bf16[2,192,384]{2,1,0:T(8,128)(2,1)}, f32[3,384]{1,0:T(4,128)}) custom-call(s32[2]{0:T(128)} %pad_add_fusion.meta_ref, bf16[448,384]{1,0:T(8,128)(2,1)} %copy-done.4, bf16[2,64,1536]{2,1,0:T(8,128)(2,1)} %bitcast.35), custom_call_target="tpu_custom_call" | custom-call | flops 56623104 | bytes 737280 | tf_op jit(solution)/shard_map/held_backward/pallas_call | solution.py:167
  57.0 0.0 copy-start.6
  57.0 2.3 %collective-permute-done.2.x_ref = bf16[448,384]{1,0:T(8,128)(2,1)S(1)} collective-permute-done((bf16[448,384]{1,0:T(8,128)(2,1)S(1)}, bf16[448,384]{1,0:T(8,128)(2,1)S(1)}, u32[]{:S(2)}, u32[]{:S(2)}) %collective-permute-start.2) | collective-permute-done | bytes 344096 | tf_op jit(solution)/shard_map/ppermute | solution.py:20
  59.2 0.0 copy-start.2
  59.2 0.7 copy-done.2
  60.0 4.4 %held_backward.5 = (bf16[64,384]{1,0:T(8,128)(2,1)}, bf16[2,192,384]{2,1,0:T(8,128)(2,1)}, f32[3,384]{1,0:T(4,128)}) custom-call(s32[2]{0:T(128)} %pad_add_fusion.meta_ref, bf16[448,384]{1,0:T(8,128)(2,1)} %copy-done.2, bf16[2,64,1536]{2,1,0:T(8,128)(2,1)} %bitcast.36), custom_call_target="tpu_custom_call" | custom-call | flops 56623104 | bytes 737280 | tf_op jit(solution)/shard_map/held_backward/pallas_call | solution.py:167
  64.3 2.3 %collective-permute-done.3.x_ref = bf16[448,384]{1,0:T(8,128)(2,1)S(1)} collective-permute-done((bf16[448,384]{1,0:T(8,128)(2,1)S(1)}, bf16[448,384]{1,0:T(8,128)(2,1)S(1)}, u32[]{:S(2)}, u32[]{:S(2)}) %collective-permute-start.3) | collective-permute-done | bytes 344096 | tf_op jit(solution)/shard_map/ppermute | solution.py:20
  66.6 0.0 copy-start.1
  66.6 0.7 copy-done.1
  67.3 4.4 %held_backward.6 = (bf16[64,384]{1,0:T(8,128)(2,1)}, bf16[2,192,384]{2,1,0:T(8,128)(2,1)}, f32[3,384]{1,0:T(4,128)}) custom-call(s32[2]{0:T(128)} %pad_add_fusion.meta_ref, bf16[448,384]{1,0:T(8,128)(2,1)} %copy-done.1, bf16[2,64,1536]{2,1,0:T(8,128)(2,1)} %bitcast.37), custom_call_target="tpu_custom_call" | custom-call | flops 56623104 | bytes 737280 | tf_op jit(solution)/shard_map/held_backward/pallas_call | solution.py:167
  71.7 1.5 %collective-permute-done.4.x_ref = bf16[448,384]{1,0:T(8,128)(2,1)S(1)} collective-permute-done((bf16[448,384]{1,0:T(8,128)(2,1)S(1)}, bf16[448,384]{1,0:T(8,128)(2,1)S(1)}, u32[]{:S(2)}, u32[]{:S(2)}) %collective-permute-start.4) | collective-permute-done | bytes 344096 | tf_op jit(solution)/shard_map/ppermute | solution.py:20
  73.2 0.0 copy-start.3
  73.2 0.7 copy-done.3
  74.0 4.4 %held_backward.7 = (bf16[64,384]{1,0:T(8,128)(2,1)}, bf16[2,192,384]{2,1,0:T(8,128)(2,1)}, f32[3,384]{1,0:T(4,128)}) custom-call(s32[2]{0:T(128)} %pad_add_fusion.meta_ref, bf16[448,384]{1,0:T(8,128)(2,1)} %copy-done.3, bf16[2,64,1536]{2,1,0:T(8,128)(2,1)} %bitcast.38), custom_call_target="tpu_custom_call" | custom-call | flops 56623104 | bytes 737280 | tf_op jit(solution)/shard_map/held_backward/pallas_call | solution.py:167
  78.3 0.0 copy-done.5
  78.4 0.0 copy-done.6
  78.4 0.7 maximum_add_fusion
  79.1 1.6 %collective-permute-start.5 = (f32[3,1536]{1,0:T(4,128)S(1)}, f32[3,1536]{1,0:T(4,128)S(1)}, u32[]{:S(2)}, u32[]{:S(2)}) collective-permute-start(f32[3,1536]{1,0:T(4,128)S(1)} %maximum_add_fusion), channel_id=1, source_target_pairs={{0,16},{16,0},{1,17},{17,1},{2,18},{18,2},{3,19},{19,3},{4,20},{20... | collective-permute-start | bytes 55304 | tf_op jit(solution)/shard_map/ppermute | solution.py:20
  80.7 42.9 %assemble_held.1 = (bf16[2,64,1536]{2,1,0:T(8,128)(2,1)}, bf16[2,2,192,1536]{3,2,1,0:T(8,128)(2,1)}) custom-call(bf16[64,384]{1,0:T(8,128)(2,1)} %get-tuple-element.28.refs_0_, bf16[64,384]{1,0:T(8,128)(2,1)} %get-tuple-element.29.refs_1_, bf16[64,384]{1,0:T(8,128)(2,1)} %get-tuple-element.30.refs_2_, ...), custom_call_target="tpu_custom_call", output_to_operand_aliasing={{0}: (8, {}), {1}: (9, {})} | custom-call | bytes 2752512 | tf_op jit(solution)/shard_map/assemble_held/pallas_call | solution.py:200
  123.5 0.0 collective-permute-done.5
  123.6 0.6 copy.16
  (5 shorter events, 0.1 us)
Async XLA Ops:
  0.6 9.6 %copy-start = (bf16[1,1,3,192,1536]{4,3,2,1,0:T(8,128)(2,1)S(1)}, bf16[1,1,3,192,1536]{4,3,2,1,0:T(8,128)(2,1)}, u32[]{:S(2)}) copy-start(bf16[1,1,3,192,1536]{4,3,2,1,0:T(8,128)(2,1)} %param.6) | copy-start | bytes 5308420
  0.6 17.3 %collective-permute-start.1 = (bf16[2,16,6144]{2,1,0:T(8,128)(2,1)}, bf16[2,16,6144]{2,1,0:T(8,128)(2,1)S(1)}, u32[]{:S(2)}, u32[]{:S(2)}) collective-permute-start(bf16[2,16,6144]{2,1,0:T(8,128)(2,1)} %bitcast.45), channel_id=1, source_target_pairs={{0,12},{4,0},{8,4},{12,8},{1,13},{5,1},{9,5},{13,9},{2,14},{6,2},{... | collective-permute-start | bytes 1179656 | tf_op jit(solution)/shard_map/ppermute | solution.py:20
  11.2 40.7 %collective-permute-start = (bf16[448,384]{1,0:T(8,128)(2,1)}, bf16[448,384]{1,0:T(8,128)(2,1)S(1)}, u32[]{:S(2)}, u32[]{:S(2)}) collective-permute-start(bf16[448,384]{1,0:T(8,128)(2,1)} %pad_maximum_fusion), channel_id=1, source_target_pairs={{0,8},{4,12},{8,0},{12,4},{1,9},{5,13},{9,1},{13,5},{2,10},{6,14},... | collective-permute-start | bytes 1032200 | tf_op jit(solution)/shard_map/ppermute | solution.py:20
  11.2 48.0 %collective-permute-start.2 = (bf16[448,384]{1,0:T(8,128)(2,1)S(1)}, bf16[448,384]{1,0:T(8,128)(2,1)S(1)}, u32[]{:S(2)}, u32[]{:S(2)}) collective-permute-start(bf16[448,384]{1,0:T(8,128)(2,1)S(1)} %pad_maximum_fusion.1), channel_id=1, source_target_pairs={{0,8},{4,12},{8,0},{12,4},{1,9},{5,13},{9,1},{13,5},{2,10},{6,14},... | collective-permute-start | bytes 1032200 | tf_op jit(solution)/shard_map/ppermute | solution.py:20
  14.2 52.4 %collective-permute-start.3 = (bf16[448,384]{1,0:T(8,128)(2,1)S(1)}, bf16[448,384]{1,0:T(8,128)(2,1)S(1)}, u32[]{:S(2)}, u32[]{:S(2)}) collective-permute-start(bf16[448,384]{1,0:T(8,128)(2,1)S(1)} %pad_maximum_fusion.2), channel_id=1, source_target_pairs={{0,8},{4,12},{8,0},{12,4},{1,9},{5,13},{9,1},{13,5},{2,10},{6,14},... | collective-permute-start | bytes 1032200 | tf_op jit(solution)/shard_map/ppermute | solution.py:20
  14.3 58.9 %collective-permute-start.4 = (bf16[448,384]{1,0:T(8,128)(2,1)S(1)}, bf16[448,384]{1,0:T(8,128)(2,1)S(1)}, u32[]{:S(2)}, u32[]{:S(2)}) collective-permute-start(bf16[448,384]{1,0:T(8,128)(2,1)S(1)} %pad_maximum_fusion.3), channel_id=1, source_target_pairs={{0,8},{4,12},{8,0},{12,4},{1,9},{5,13},{9,1},{13,5},{2,10},{6,14},... | collective-permute-start | bytes 1032200 | tf_op jit(solution)/shard_map/ppermute | solution.py:20
  19.1 10.9 %all-to-all-start = ((bf16[4,2,16,1536]{3,2,1,0:T(8,128)(2,1)}), bf16[4,2,16,1536]{3,2,1,0:T(8,128)(2,1)S(1)}, u32[]{:S(2)}, u32[]{:S(2)}) async-start(bf16[4,2,16,1536]{3,2,1,0:T(8,128)(2,1)} %copy.14), calls=%async_computation | async-start | bytes 786432 | tf_op jit(solution)/shard_map/all_to_all | solution.py:265
  41.6 36.7 %copy-start.5 = (f32[3,1536]{1,0:T(4,128)S(1)}, f32[3,1536]{1,0:T(4,128)}, u32[]{:S(2)}) copy-start(f32[3,1536]{1,0:T(4,128)} %get-tuple-element.40) | copy-start | bytes 55300
  51.9 0.7 copy-start.4
  57.0 21.4 %copy-start.6 = (f32[3,384]{1,0:T(4,128)S(1)}, f32[3,384]{1,0:T(4,128)}, u32[]{:S(2)}) copy-start(f32[3,384]{1,0:T(4,128)} %get-tuple-element.41) | copy-start | bytes 13828
  59.2 0.7 copy-start.2
  66.6 0.7 copy-start.1
  73.2 0.7 copy-start.3
  79.1 44.5 %collective-permute-start.5 = (f32[3,1536]{1,0:T(4,128)S(1)}, f32[3,1536]{1,0:T(4,128)S(1)}, u32[]{:S(2)}, u32[]{:S(2)}) collective-permute-start(f32[3,1536]{1,0:T(4,128)S(1)} %maximum_add_fusion), channel_id=1, source_target_pairs={{0,16},{16,0},{1,17},{17,1},{2,18},{18,2},{3,19},{19,3},{4,20},{20... | collective-permute-start | bytes 55304 | tf_op jit(solution)/shard_map/ppermute | solution.py:20

commit v14 on v11

--- a/solution.py
+++ b/solution.py
@@ -20,7 +20,7 @@
     return lax.ppermute(value, axis, pairs)
 
 
-def head_backward(q, k, v, g, visible):
+def head_backward(q, k, v, g, visible, visible_t):
     f32, bf16 = jnp.float32, jnp.bfloat16
     scale = 1.0 / math.sqrt(HD)
     s = lax.dot_general(q, k, NT_DIMS, preferred_element_type=f32) * scale
@@ -28,14 +28,21 @@
     m = jnp.max(s, axis=1, keepdims=True)
     e = jnp.exp(s - m)
     p = e / jnp.sum(e, axis=1, keepdims=True)
-    p_low = p.astype(bf16)
-    ctx = jnp.dot(p_low, v, preferred_element_type=f32).astype(bf16)
-    delta = jnp.sum(g.astype(f32) * ctx.astype(f32), axis=1, keepdims=True)
     dp = lax.dot_general(g, v, NT_DIMS, preferred_element_type=f32)
+    delta = jnp.sum(p.astype(bf16).astype(f32) * dp, axis=1, keepdims=True)
     ds = (p * (dp - delta) * scale).astype(bf16)
     dq = jnp.dot(ds, k, preferred_element_type=f32).astype(bf16)
-    dk = jnp.dot(ds.T, q, preferred_element_type=f32).astype(bf16)
-    dv = jnp.dot(p_low.T, g, preferred_element_type=f32).astype(bf16)
+    st = lax.dot_general(k, q, NT_DIMS, preferred_element_type=f32) * scale
+    st = jnp.where(visible_t, st, MASK_FILL)
+    mt = jnp.max(st, axis=0, keepdims=True)
+    et = jnp.exp(st - mt)
+    pt = et / jnp.sum(et, axis=0, keepdims=True)
+    pt_low = pt.astype(bf16)
+    dpt = lax.dot_general(v, g, NT_DIMS, preferred_element_type=f32)
+    delta_t = jnp.sum(pt_low.astype(f32) * dpt, axis=0, keepdims=True)
+    dst = (pt * (dpt - delta_t) * scale).astype(bf16)
+    dk = jnp.dot(dst, q, preferred_element_type=f32).astype(bf16)
+    dv = jnp.dot(pt_low, g, preferred_element_type=f32).astype(bf16)
     return dq, dk, dv
 
 
@@ -44,11 +51,14 @@
     pos = offset + lax.broadcasted_iota(jnp.int32, (rows, keys), 0)
     col = lax.broadcasted_iota(jnp.int32, (rows, keys), 1)
     visible = col <= pos
+    pos_t = offset + lax.broadcasted_iota(jnp.int32, (keys, rows), 1)
+    col_t = lax.broadcasted_iota(jnp.int32, (keys, rows), 0)
+    visible_t = col_t <= pos_t
 
     def head(h, carry):
         cols = pl.ds(pl.multiple_of(h * HD, HD), HD)
         q, k, v, g = load(cols)
-        store(cols, *head_backward(q, k, v, g, visible))
+        store(cols, *head_backward(q, k, v, g, visible, visible_t))
         return carry
 
     lax.fori_loop(0, heads, head, 0, unroll=True)

time: 84.4 us -> 84.3 us (level)
  transfers between devices with their start and end apart: 7 -> 7, of which waited for: 5 -> 5; matrix products, arithmetic and copies ran while one was open for 10% -> 10% of each run, Pallas kernels for 32% -> 31%
where the time goes in v14:
time: 84.3 us; the launch traced here: 83.8 us
  Pallas kernels  30.2 us (36%)
  waiting for transfers between devices  21.3 us (25%)
  starting transfers between devices  16.2 us (19%)
  local copies, waits for them, and re-layouts  8.62 us (10%)
  other arithmetic  4.13 us (5%)
  between operations  3.33 us (4%)
    pallas_call x4, Pallas kernels, held_backward(): pl.pallas_call(held_kernel, out_shape=(jax.ShapeDtypeStruct((rows, width)...  17.2 us
    ppermute x6, waiting for transfers between devices, from_behind(): return lax.ppermute(value, axis, pairs)  16.9 us
    ppermute x6, starting transfers between devices, from_behind(): return lax.ppermute(value, axis, pairs)  12.7 us
    pallas_call x1, Pallas kernels, kept_backward(): pl.pallas_call(kept_kernel, out_shape=out_shape, grid_spec=grid_spec, cos...  10.5 us
    all_to_all x1, waiting for transfers between devices, body(): lax.all_to_all(split, 'tensor', split_axis=0, concat_axis=0, tiled=True)  4.34 us
    unnamed x15, local copies, waits for them, and re-layouts  3.55 us
    all_to_all x1, starting transfers between devices, body(): lax.all_to_all(split, 'tensor', split_axis=0, concat_axis=0, tiled=True)  3.46 us
    pallas_call x1, Pallas kernels, assemble(): pl.pallas_call(functools.partial(assemble_kernel, tuple(bounds)), out_sha...  2.51 us
  transfers between devices with their start and end apart: 7, of which 5 were waited for; matrix products, arithmetic and copies ran while one was open for 10% of the time, Pallas kernels for 31%

profile of v14, /device:TPU:0, one launch (start us, length us, event | category | flops | bytes accessed | tf_op | source)
XLA Modules:
  0.0 83.8 jit_solution(12108893495364702558)
XLA Ops:
  0.6 0.0 copy-start
  0.6 5.1 %collective-permute-start.1 = (bf16[2,16,6144]{2,1,0:T(8,128)(2,1)}, bf16[2,16,6144]{2,1,0:T(8,128)(2,1)S(1)}, u32[]{:S(2)}, u32[]{:S(2)}) collective-permute-start(bf16[2,16,6144]{2,1,0:T(8,128)(2,1)} %bitcast.45), channel_id=1, source_target_pairs={{0,12},{4,0},{8,4},{12,8},{1,13},{5,1},{9,5},{13,9},{2,14},{6,2},{... | collective-permute-start | bytes 1179656 | tf_op jit(solution)/shard_map/ppermute | solution.py:20
  5.7 0.8 constant_dynamic-slice_fusion
  6.6 0.5 slice.62
  8.4 1.1 %slice.61 = bf16[1,1,1,192,1536]{4,3,2,1,0:T(8,128)(2,1)S(1)} slice(bf16[1,1,3,192,1536]{4,3,2,1,0:T(8,128)(2,1)} %param.6), slice={[0:1], [0:1], [0:1], [0:192], [0:1536]} | slice | bytes 1179648 | tf_op jit(solution)/shard_map/slice | solution.py:267
  10.1 0.1 dynamic-slice_bitcast_fusion
  10.2 0.0 copy-done
  10.2 0.1 slice_bitcast_fusion.1
  10.4 0.8 pad_maximum_fusion
  11.2 0.0 collective-permute-start
  11.2 3.0 %collective-permute-start.2 = (bf16[448,384]{1,0:T(8,128)(2,1)S(1)}, bf16[448,384]{1,0:T(8,128)(2,1)S(1)}, u32[]{:S(2)}, u32[]{:S(2)}) collective-permute-start(bf16[448,384]{1,0:T(8,128)(2,1)S(1)} %pad_maximum_fusion.1), channel_id=1, source_target_pairs={{0,8},{4,12},{8,0},{12,4},{1,9},{5,13},{9,1},{13,5},{2,10},{6,14},... | collective-permute-start | bytes 1032200 | tf_op jit(solution)/shard_map/ppermute | solution.py:20
  14.2 0.1 collective-permute-start.3
  14.3 3.0 %collective-permute-start.4 = (bf16[448,384]{1,0:T(8,128)(2,1)S(1)}, bf16[448,384]{1,0:T(8,128)(2,1)S(1)}, u32[]{:S(2)}, u32[]{:S(2)}) collective-permute-start(bf16[448,384]{1,0:T(8,128)(2,1)S(1)} %pad_maximum_fusion.3), channel_id=1, source_target_pairs={{0,8},{4,12},{8,0},{12,4},{1,9},{5,13},{9,1},{13,5},{2,10},{6,14},... | collective-permute-start | bytes 1032200 | tf_op jit(solution)/shard_map/ppermute | solution.py:20
  18.0 0.0 collective-permute-done.1
  18.0 0.3 reshape.26
  18.3 0.8 copy.14
  19.1 3.5 %all-to-all-start = ((bf16[4,2,16,1536]{3,2,1,0:T(8,128)(2,1)}), bf16[4,2,16,1536]{3,2,1,0:T(8,128)(2,1)S(1)}, u32[]{:S(2)}, u32[]{:S(2)}) async-start(bf16[4,2,16,1536]{3,2,1,0:T(8,128)(2,1)} %copy.14), calls=%async_computation | async-start | bytes 786432 | tf_op jit(solution)/shard_map/all_to_all | solution.py:278
  22.5 0.5 fusion.1
  23.1 1.2 %pad_add_fusion.1.meta_ref = s32[2]{0:T(128)} fusion(s32[1]{0:T(128)} %bitcast.33, s32[1]{0:T(128)} %bitcast.7), kind=kLoop, calls=%fused_computation.18 | loop fusion | flops 2 | bytes 16 | tf_op jit(solution)/shard_map/stack | solution.py:146
  24.3 1.3 %pad_add_fusion.meta_ref = s32[2]{0:T(128)} fusion(s32[1]{0:T(128)} %bitcast.1, s32[1]{0:T(128)} %bitcast), kind=kLoop, calls=%fused_computation.17 | loop fusion | flops 2 | bytes 16 | tf_op jit(solution)/shard_map/stack | solution.py:176
  25.6 4.3 %all-to-all-done = bf16[4,2,16,1536]{3,2,1,0:T(8,128)(2,1)S(1)} async-done(((bf16[4,2,16,1536]{3,2,1,0:T(8,128)(2,1)}), bf16[4,2,16,1536]{3,2,1,0:T(8,128)(2,1)S(1)}, u32[]{:S(2)}, u32[]{:S(2)}) %all-to-all-start) | async-done | bytes 393248 | tf_op jit(solution)/shard_map/all_to_all | solution.py:278
  29.9 0.8 copy.15
  30.7 10.5 %kept_backward.1 = (bf16[2,64,1536]{2,1,0:T(8,128)(2,1)}, bf16[2,2,192,1536]{3,2,1,0:T(8,128)(2,1)}, f32[3,1536]{1,0:T(4,128)}) custom-call(s32[2]{0:T(128)} %pad_add_fusion.1.meta_ref, bf16[3,192,1536]{2,1,0:T(8,128)(2,1)} %bitcast.41, bf16[2,64,1536]{2,1,0:T(8,128)(2,1)} %bitcast.34), custom_call_target="tpu_custom_call" | custom-call | flops 226492416 | bytes 2949120 | tf_op jit(solution)/shard_map/kept_backward/pallas_call | solution.py:147
  41.2 0.0 copy-start.5
  41.2 10.6 %collective-permute-done.x_ref = bf16[448,384]{1,0:T(8,128)(2,1)S(1)} collective-permute-done((bf16[448,384]{1,0:T(8,128)(2,1)}, bf16[448,384]{1,0:T(8,128)(2,1)S(1)}, u32[]{:S(2)}, u32[]{:S(2)}) %collective-permute-start) | collective-permute-done | bytes 344096 | tf_op jit(solution)/shard_map/ppermute | solution.py:20
  51.9 0.0 copy-start.4
  51.9 0.7 copy-done.4
  52.6 4.3 %held_backward.4 = (bf16[64,384]{1,0:T(8,128)(2,1)}, bf16[2,192,384]{2,1,0:T(8,128)(2,1)}, f32[3,384]{1,0:T(4,128)}) custom-call(s32[2]{0:T(128)} %pad_add_fusion.meta_ref, bf16[448,384]{1,0:T(8,128)(2,1)} %copy-done.4, bf16[2,64,1536]{2,1,0:T(8,128)(2,1)} %bitcast.35), custom_call_target="tpu_custom_call" | custom-call | flops 56623104 | bytes 737280 | tf_op jit(solution)/shard_map/held_backward/pallas_call | solution.py:177
  56.9 0.0 copy-start.6
  56.9 2.4 %collective-permute-done.2.x_ref = bf16[448,384]{1,0:T(8,128)(2,1)S(1)} collective-permute-done((bf16[448,384]{1,0:T(8,128)(2,1)S(1)}, bf16[448,384]{1,0:T(8,128)(2,1)S(1)}, u32[]{:S(2)}, u32[]{:S(2)}) %collective-permute-start.2) | collective-permute-done | bytes 344096 | tf_op jit(solution)/shard_map/ppermute | solution.py:20
  59.2 0.0 copy-start.2
  59.2 0.7 copy-done.2
  60.0 4.3 %held_backward.5 = (bf16[64,384]{1,0:T(8,128)(2,1)}, bf16[2,192,384]{2,1,0:T(8,128)(2,1)}, f32[3,384]{1,0:T(4,128)}) custom-call(s32[2]{0:T(128)} %pad_add_fusion.meta_ref, bf16[448,384]{1,0:T(8,128)(2,1)} %copy-done.2, bf16[2,64,1536]{2,1,0:T(8,128)(2,1)} %bitcast.36), custom_call_target="tpu_custom_call" | custom-call | flops 56623104 | bytes 737280 | tf_op jit(solution)/shard_map/held_backward/pallas_call | solution.py:177
  64.3 2.3 %collective-permute-done.3.x_ref = bf16[448,384]{1,0:T(8,128)(2,1)S(1)} collective-permute-done((bf16[448,384]{1,0:T(8,128)(2,1)S(1)}, bf16[448,384]{1,0:T(8,128)(2,1)S(1)}, u32[]{:S(2)}, u32[]{:S(2)}) %collective-permute-start.3) | collective-permute-done | bytes 344096 | tf_op jit(solution)/shard_map/ppermute | solution.py:20
  66.6 0.0 copy-start.1
  66.6 0.7 copy-done.1
  67.3 4.3 %held_backward.6 = (bf16[64,384]{1,0:T(8,128)(2,1)}, bf16[2,192,384]{2,1,0:T(8,128)(2,1)}, f32[3,384]{1,0:T(4,128)}) custom-call(s32[2]{0:T(128)} %pad_add_fusion.meta_ref, bf16[448,384]{1,0:T(8,128)(2,1)} %copy-done.1, bf16[2,64,1536]{2,1,0:T(8,128)(2,1)} %bitcast.37), custom_call_target="tpu_custom_call" | custom-call | flops 56623104 | bytes 737280 | tf_op jit(solution)/shard_map/held_backward/pallas_call | solution.py:177
  71.6 1.6 %collective-permute-done.4.x_ref = bf16[448,384]{1,0:T(8,128)(2,1)S(1)} collective-permute-done((bf16[448,384]{1,0:T(8,128)(2,1)S(1)}, bf16[448,384]{1,0:T(8,128)(2,1)S(1)}, u32[]{:S(2)}, u32[]{:S(2)}) %collective-permute-start.4) | collective-permute-done | bytes 344096 | tf_op jit(solution)/shard_map/ppermute | solution.py:20
  73.2 0.0 copy-start.3
  73.2 0.7 copy-done.3
  74.0 4.3 %held_backward.7 = (bf16[64,384]{1,0:T(8,128)(2,1)}, bf16[2,192,384]{2,1,0:T(8,128)(2,1)}, f32[3,384]{1,0:T(4,128)}) custom-call(s32[2]{0:T(128)} %pad_add_fusion.meta_ref, bf16[448,384]{1,0:T(8,128)(2,1)} %copy-done.3, bf16[2,64,1536]{2,1,0:T(8,128)(2,1)} %bitcast.38), custom_call_target="tpu_custom_call" | custom-call | flops 56623104 | bytes 737280 | tf_op jit(solution)/shard_map/held_backward/pallas_call | solution.py:177
  78.3 0.0 copy-done.5
  78.3 0.0 copy-done.6
  78.3 0.7 maximum_add_fusion
  79.0 1.6 %collective-permute-start.5 = (f32[3,1536]{1,0:T(4,128)S(1)}, f32[3,1536]{1,0:T(4,128)S(1)}, u32[]{:S(2)}, u32[]{:S(2)}) collective-permute-start(f32[3,1536]{1,0:T(4,128)S(1)} %maximum_add_fusion), channel_id=1, source_target_pairs={{0,16},{16,0},{1,17},{17,1},{2,18},{18,2},{3,19},{19,3},{4,20},{20... | collective-permute-start | bytes 55304 | tf_op jit(solution)/shard_map/ppermute | solution.py:20
  80.6 2.5 %assemble_held.1 = (bf16[2,64,1536]{2,1,0:T(8,128)(2,1)}, bf16[2,2,192,1536]{3,2,1,0:T(8,128)(2,1)}) custom-call(bf16[64,384]{1,0:T(8,128)(2,1)} %get-tuple-element.28.refs_0_, bf16[64,384]{1,0:T(8,128)(2,1)} %get-tuple-element.29.refs_1_, bf16[64,384]{1,0:T(8,128)(2,1)} %get-tuple-element.30.refs_2_, ...), custom_call_target="tpu_custom_call", output_to_operand_aliasing={{0}: (8, {}), {1}: (9, {})} | custom-call | bytes 2752512 | tf_op jit(solution)/shard_map/assemble_held/pallas_call | solution.py:210
  83.1 0.0 collective-permute-done.5
  83.1 0.6 copy.16
  (5 shorter events, 0.1 us)
Async XLA Ops:
  0.6 9.6 %copy-start = (bf16[1,1,3,192,1536]{4,3,2,1,0:T(8,128)(2,1)S(1)}, bf16[1,1,3,192,1536]{4,3,2,1,0:T(8,128)(2,1)}, u32[]{:S(2)}) copy-start(bf16[1,1,3,192,1536]{4,3,2,1,0:T(8,128)(2,1)} %param.6) | copy-start | bytes 5308420
  0.6 17.3 %collective-permute-start.1 = (bf16[2,16,6144]{2,1,0:T(8,128)(2,1)}, bf16[2,16,6144]{2,1,0:T(8,128)(2,1)S(1)}, u32[]{:S(2)}, u32[]{:S(2)}) collective-permute-start(bf16[2,16,6144]{2,1,0:T(8,128)(2,1)} %bitcast.45), channel_id=1, source_target_pairs={{0,12},{4,0},{8,4},{12,8},{1,13},{5,1},{9,5},{13,9},{2,14},{6,2},{... | collective-permute-start | bytes 1179656 | tf_op jit(solution)/shard_map/ppermute | solution.py:20
  11.2 40.7 %collective-permute-start = (bf16[448,384]{1,0:T(8,128)(2,1)}, bf16[448,384]{1,0:T(8,128)(2,1)S(1)}, u32[]{:S(2)}, u32[]{:S(2)}) collective-permute-start(bf16[448,384]{1,0:T(8,128)(2,1)} %pad_maximum_fusion), channel_id=1, source_target_pairs={{0,8},{4,12},{8,0},{12,4},{1,9},{5,13},{9,1},{13,5},{2,10},{6,14},... | collective-permute-start | bytes 1032200 | tf_op jit(solution)/shard_map/ppermute | solution.py:20
  11.2 48.0 %collective-permute-start.2 = (bf16[448,384]{1,0:T(8,128)(2,1)S(1)}, bf16[448,384]{1,0:T(8,128)(2,1)S(1)}, u32[]{:S(2)}, u32[]{:S(2)}) collective-permute-start(bf16[448,384]{1,0:T(8,128)(2,1)S(1)} %pad_maximum_fusion.1), channel_id=1, source_target_pairs={{0,8},{4,12},{8,0},{12,4},{1,9},{5,13},{9,1},{13,5},{2,10},{6,14},... | collective-permute-start | bytes 1032200 | tf_op jit(solution)/shard_map/ppermute | solution.py:20
  14.2 52.4 %collective-permute-start.3 = (bf16[448,384]{1,0:T(8,128)(2,1)S(1)}, bf16[448,384]{1,0:T(8,128)(2,1)S(1)}, u32[]{:S(2)}, u32[]{:S(2)}) collective-permute-start(bf16[448,384]{1,0:T(8,128)(2,1)S(1)} %pad_maximum_fusion.2), channel_id=1, source_target_pairs={{0,8},{4,12},{8,0},{12,4},{1,9},{5,13},{9,1},{13,5},{2,10},{6,14},... | collective-permute-start | bytes 1032200 | tf_op jit(solution)/shard_map/ppermute | solution.py:20
  14.3 58.9 %collective-permute-start.4 = (bf16[448,384]{1,0:T(8,128)(2,1)S(1)}, bf16[448,384]{1,0:T(8,128)(2,1)S(1)}, u32[]{:S(2)}, u32[]{:S(2)}) collective-permute-start(bf16[448,384]{1,0:T(8,128)(2,1)S(1)} %pad_maximum_fusion.3), channel_id=1, source_target_pairs={{0,8},{4,12},{8,0},{12,4},{1,9},{5,13},{9,1},{13,5},{2,10},{6,14},... | collective-permute-start | bytes 1032200 | tf_op jit(solution)/shard_map/ppermute | solution.py:20
  19.1 10.9 %all-to-all-start = ((bf16[4,2,16,1536]{3,2,1,0:T(8,128)(2,1)}), bf16[4,2,16,1536]{3,2,1,0:T(8,128)(2,1)S(1)}, u32[]{:S(2)}, u32[]{:S(2)}) async-start(bf16[4,2,16,1536]{3,2,1,0:T(8,128)(2,1)} %copy.14), calls=%async_computation | async-start | bytes 786432 | tf_op jit(solution)/shard_map/all_to_all | solution.py:278
  41.2 37.1 %copy-start.5 = (f32[3,1536]{1,0:T(4,128)S(1)}, f32[3,1536]{1,0:T(4,128)}, u32[]{:S(2)}) copy-start(f32[3,1536]{1,0:T(4,128)} %get-tuple-element.40) | copy-start | bytes 55300
  51.9 0.7 copy-start.4
  56.9 21.4 %copy-start.6 = (f32[3,384]{1,0:T(4,128)S(1)}, f32[3,384]{1,0:T(4,128)}, u32[]{:S(2)}) copy-start(f32[3,384]{1,0:T(4,128)} %get-tuple-element.41) | copy-start | bytes 13828
  59.2 0.7 copy-start.2
  66.6 0.7 copy-start.1
  73.2 0.7 copy-start.3
  79.0 4.1 %collective-permute-start.5 = (f32[3,1536]{1,0:T(4,128)S(1)}, f32[3,1536]{1,0:T(4,128)S(1)}, u32[]{:S(2)}, u32[]{:S(2)}) collective-permute-start(f32[3,1536]{1,0:T(4,128)S(1)} %maximum_add_fusion), channel_id=1, source_target_pairs={{0,16},{16,0},{1,17},{17,1},{2,18},{18,2},{3,19},{19,3},{4,20},{20... | collective-permute-start | bytes 55304 | tf_op jit(solution)/shard_map/ppermute | solution.py:20

commit v15 on v11

--- a/solution.py
+++ b/solution.py
@@ -154,7 +154,7 @@
         num_scalar_prefetch=1,
         grid=(1,),
         in_specs=[
-            pl.BlockSpec((part.shape[0], width), lambda i, m: (0, 0)),
+            pl.BlockSpec(memory_space=pltpu.VMEM),
             pl.BlockSpec((None, rows, width), lambda i, m: (m[1], 0, chunk)),
         ],
         out_specs=(
@@ -174,7 +174,7 @@
         grid_spec=grid_spec,
         cost_estimate=kernel_cost(rows, keys, width),
         name="held_backward",
-    )(meta, part, grads)
+    )(meta, pltpu.with_memory_space_constraint(part, pltpu.VMEM), grads)
 
 
 def assemble_kernel(bounds, *refs):

time: 84.4 us -> 83.6 us (level)
  local copies, waits for them, and re-layouts: 8.62 us -> 5.74 us
  waiting for transfers between devices: 20.7 us -> 23.5 us
    unnamed x15 -> x7, local copies, waits for them, and re-layouts: 3.55 us -> 0.64 us
    ppermute x6, waiting for transfers between devices: 16.3 us -> 19 us  [from_behind(): return lax.ppermute(value, axis, pairs)]
  transfers between devices with their start and end apart: 7 -> 7, of which waited for: 5 -> 5; matrix products, arithmetic and copies ran while one was open for 10% -> 10% of each run, Pallas kernels for 32% -> 31%
where the time goes in v15:
time: 83.6 us; the launch traced here: 82.9 us
  Pallas kernels  30.2 us (36%)
  waiting for transfers between devices  23.5 us (28%)
  starting transfers between devices  16.2 us (19%)
  local copies, waits for them, and re-layouts  5.74 us (7%)
  other arithmetic  3.92 us (5%)
  between operations  3.32 us (4%)
    ppermute x6, waiting for transfers between devices, from_behind(): return lax.ppermute(value, axis, pairs)  19 us
    pallas_call x4, Pallas kernels, held_backward(): pl.pallas_call(held_kernel, out_shape=(jax.ShapeDtypeStruct((rows, width)...  16.8 us
    ppermute x6, starting transfers between devices, from_behind(): return lax.ppermute(value, axis, pairs)  12.7 us
    pallas_call x1, Pallas kernels, kept_backward(): pl.pallas_call(kept_kernel, out_shape=out_shape, grid_spec=grid_spec, cos...  10.9 us
    all_to_all x1, waiting for transfers between devices, body(): lax.all_to_all(split, 'tensor', split_axis=0, concat_axis=0, tiled=True)  4.52 us
    all_to_all x1, starting transfers between devices, body(): lax.all_to_all(split, 'tensor', split_axis=0, concat_axis=0, tiled=True)  3.46 us
    pallas_call x1, Pallas kernels, assemble(): pl.pallas_call(functools.partial(assemble_kernel, tuple(bounds)), out_sha...  2.51 us
  transfers between devices with their start and end apart: 7, of which 5 were waited for; matrix products, arithmetic and copies ran while one was open for 10% of the time, Pallas kernels for 31%

profile of v15, /device:TPU:0, one launch (start us, length us, event | category | flops | bytes accessed | tf_op | source)
XLA Modules:
  0.0 82.9 jit_solution(7628190631681205201)
XLA Ops:
  0.6 0.0 copy-start
  0.6 5.1 %collective-permute-start.1 = (bf16[2,16,6144]{2,1,0:T(8,128)(2,1)}, bf16[2,16,6144]{2,1,0:T(8,128)(2,1)S(1)}, u32[]{:S(2)}, u32[]{:S(2)}) collective-permute-start(bf16[2,16,6144]{2,1,0:T(8,128)(2,1)} %bitcast.45), channel_id=1, source_target_pairs={{0,12},{4,0},{8,4},{12,8},{1,13},{5,1},{9,5},{13,9},{2,14},{6,2},{... | collective-permute-start | bytes 1179656 | tf_op jit(solution)/shard_map/ppermute | solution.py:20
  5.7 0.8 constant_dynamic-slice_fusion
  6.6 0.5 slice.62
  8.4 1.1 %slice.61 = bf16[1,1,1,192,1536]{4,3,2,1,0:T(8,128)(2,1)S(1)} slice(bf16[1,1,3,192,1536]{4,3,2,1,0:T(8,128)(2,1)} %param.6), slice={[0:1], [0:1], [0:1], [0:192], [0:1536]} | slice | bytes 1179648 | tf_op jit(solution)/shard_map/slice | solution.py:257
  10.1 0.1 dynamic-slice_bitcast_fusion
  10.2 0.0 copy-done
  10.2 0.1 slice_bitcast_fusion.1
  10.4 0.8 pad_maximum_fusion
  11.1 0.0 collective-permute-start
  11.2 3.0 %collective-permute-start.2 = (bf16[448,384]{1,0:T(8,128)(2,1)S(1)}, bf16[448,384]{1,0:T(8,128)(2,1)S(1)}, u32[]{:S(2)}, u32[]{:S(2)}) collective-permute-start(bf16[448,384]{1,0:T(8,128)(2,1)S(1)} %pad_maximum_fusion.1), channel_id=1, source_target_pairs={{0,8},{4,12},{8,0},{12,4},{1,9},{5,13},{9,1},{13,5},{2,10},{6,14},... | collective-permute-start | bytes 1032200 | tf_op jit(solution)/shard_map/ppermute | solution.py:20
  14.2 0.1 collective-permute-start.3
  14.3 3.0 %collective-permute-start.4 = (bf16[448,384]{1,0:T(8,128)(2,1)S(1)}, bf16[448,384]{1,0:T(8,128)(2,1)S(1)}, u32[]{:S(2)}, u32[]{:S(2)}) collective-permute-start(bf16[448,384]{1,0:T(8,128)(2,1)S(1)} %pad_maximum_fusion.3), channel_id=1, source_target_pairs={{0,8},{4,12},{8,0},{12,4},{1,9},{5,13},{9,1},{13,5},{2,10},{6,14},... | collective-permute-start | bytes 1032200 | tf_op jit(solution)/shard_map/ppermute | solution.py:20
  18.0 0.0 collective-permute-done.1
  18.0 0.3 reshape.26
  18.3 0.8 copy.14
  19.1 3.5 %all-to-all-start = ((bf16[4,2,16,1536]{3,2,1,0:T(8,128)(2,1)}), bf16[4,2,16,1536]{3,2,1,0:T(8,128)(2,1)S(1)}, u32[]{:S(2)}, u32[]{:S(2)}) async-start(bf16[4,2,16,1536]{3,2,1,0:T(8,128)(2,1)} %copy.14), calls=%async_computation | async-start | bytes 786432 | tf_op jit(solution)/shard_map/all_to_all | solution.py:268
  22.5 0.6 fusion.1
  23.1 1.1 %pad_add_fusion.1.meta_ref = s32[2]{0:T(128)} fusion(s32[1]{0:T(128)} %bitcast.33, s32[1]{0:T(128)} %bitcast.7), kind=kLoop, calls=%fused_computation.18 | loop fusion | flops 2 | bytes 16 | tf_op jit(solution)/shard_map/stack | solution.py:136
  24.2 1.2 %pad_add_fusion.meta_ref = s32[2]{0:T(128)} fusion(s32[1]{0:T(128)} %bitcast.1, s32[1]{0:T(128)} %bitcast), kind=kLoop, calls=%fused_computation.17 | loop fusion | flops 2 | bytes 16 | tf_op jit(solution)/shard_map/stack | solution.py:166
  25.4 4.5 %all-to-all-done = bf16[4,2,16,1536]{3,2,1,0:T(8,128)(2,1)S(1)} async-done(((bf16[4,2,16,1536]{3,2,1,0:T(8,128)(2,1)}), bf16[4,2,16,1536]{3,2,1,0:T(8,128)(2,1)S(1)}, u32[]{:S(2)}, u32[]{:S(2)}) %all-to-all-start) | async-done | bytes 393248 | tf_op jit(solution)/shard_map/all_to_all | solution.py:268
  29.9 0.8 copy.15
  30.7 10.9 %kept_backward.1 = (bf16[2,64,1536]{2,1,0:T(8,128)(2,1)}, bf16[2,2,192,1536]{3,2,1,0:T(8,128)(2,1)}, f32[3,1536]{1,0:T(4,128)}) custom-call(s32[2]{0:T(128)} %pad_add_fusion.1.meta_ref, bf16[3,192,1536]{2,1,0:T(8,128)(2,1)} %bitcast.41, bf16[2,64,1536]{2,1,0:T(8,128)(2,1)} %bitcast.34), custom_call_target="tpu_custom_call" | custom-call | flops 226492416 | bytes 2949120 | tf_op jit(solution)/shard_map/kept_backward/pallas_call | solution.py:137
  41.6 0.0 copy-start.1
  41.6 10.3 %collective-permute-done.x_ref = bf16[448,384]{1,0:T(8,128)(2,1)S(1)} collective-permute-done((bf16[448,384]{1,0:T(8,128)(2,1)}, bf16[448,384]{1,0:T(8,128)(2,1)S(1)}, u32[]{:S(2)}, u32[]{:S(2)}) %collective-permute-start) | collective-permute-done | bytes 344096 | tf_op jit(solution)/shard_map/ppermute | solution.py:20
  51.9 4.2 %held_backward.4 = (bf16[64,384]{1,0:T(8,128)(2,1)}, bf16[2,192,384]{2,1,0:T(8,128)(2,1)}, f32[3,384]{1,0:T(4,128)}) custom-call(s32[2]{0:T(128)} %pad_add_fusion.meta_ref, bf16[448,384]{1,0:T(8,128)(2,1)S(1)} %collective-permute-done.x_ref, bf16[2,64,1536]{2,1,0:T(8,128)(2,1)} %bitcast.35), custom_call_target="tpu_custom_call" | custom-call | flops 56623104 | bytes 737280 | tf_op jit(solution)/shard_map/held_backward/pallas_call | solution.py:167
  56.1 0.0 copy-start.2
  56.1 3.2 %collective-permute-done.2.x_ref = bf16[448,384]{1,0:T(8,128)(2,1)S(1)} collective-permute-done((bf16[448,384]{1,0:T(8,128)(2,1)S(1)}, bf16[448,384]{1,0:T(8,128)(2,1)S(1)}, u32[]{:S(2)}, u32[]{:S(2)}) %collective-permute-start.2) | collective-permute-done | bytes 344096 | tf_op jit(solution)/shard_map/ppermute | solution.py:20
  59.2 4.2 %held_backward.5 = (bf16[64,384]{1,0:T(8,128)(2,1)}, bf16[2,192,384]{2,1,0:T(8,128)(2,1)}, f32[3,384]{1,0:T(4,128)}) custom-call(s32[2]{0:T(128)} %pad_add_fusion.meta_ref, bf16[448,384]{1,0:T(8,128)(2,1)S(1)} %collective-permute-done.2.x_ref, bf16[2,64,1536]{2,1,0:T(8,128)(2,1)} %bitcast.36), custom_call_target="tpu_custom_call" | custom-call | flops 56623104 | bytes 737280 | tf_op jit(solution)/shard_map/held_backward/pallas_call | solution.py:167
  63.5 3.2 %collective-permute-done.3.x_ref = bf16[448,384]{1,0:T(8,128)(2,1)S(1)} collective-permute-done((bf16[448,384]{1,0:T(8,128)(2,1)S(1)}, bf16[448,384]{1,0:T(8,128)(2,1)S(1)}, u32[]{:S(2)}, u32[]{:S(2)}) %collective-permute-start.3) | collective-permute-done | bytes 344096 | tf_op jit(solution)/shard_map/ppermute | solution.py:20
  66.6 4.2 %held_backward.6 = (bf16[64,384]{1,0:T(8,128)(2,1)}, bf16[2,192,384]{2,1,0:T(8,128)(2,1)}, f32[3,384]{1,0:T(4,128)}) custom-call(s32[2]{0:T(128)} %pad_add_fusion.meta_ref, bf16[448,384]{1,0:T(8,128)(2,1)S(1)} %collective-permute-done.3.x_ref, bf16[2,64,1536]{2,1,0:T(8,128)(2,1)} %bitcast.37), custom_call_target="tpu_custom_call" | custom-call | flops 56623104 | bytes 737280 | tf_op jit(solution)/shard_map/held_backward/pallas_call | solution.py:167
  70.8 2.4 %collective-permute-done.4.x_ref = bf16[448,384]{1,0:T(8,128)(2,1)S(1)} collective-permute-done((bf16[448,384]{1,0:T(8,128)(2,1)S(1)}, bf16[448,384]{1,0:T(8,128)(2,1)S(1)}, u32[]{:S(2)}, u32[]{:S(2)}) %collective-permute-start.4) | collective-permute-done | bytes 344096 | tf_op jit(solution)/shard_map/ppermute | solution.py:20
  73.2 4.2 %held_backward.7 = (bf16[64,384]{1,0:T(8,128)(2,1)}, bf16[2,192,384]{2,1,0:T(8,128)(2,1)}, f32[3,384]{1,0:T(4,128)}) custom-call(s32[2]{0:T(128)} %pad_add_fusion.meta_ref, bf16[448,384]{1,0:T(8,128)(2,1)S(1)} %collective-permute-done.4.x_ref, bf16[2,64,1536]{2,1,0:T(8,128)(2,1)} %bitcast.38), custom_call_target="tpu_custom_call" | custom-call | flops 56623104 | bytes 737280 | tf_op jit(solution)/shard_map/held_backward/pallas_call | solution.py:167
  77.4 0.0 copy-done.1
  77.4 0.0 copy-done.2
  77.4 0.7 maximum_add_fusion
  78.2 1.6 %collective-permute-start.5 = (f32[3,1536]{1,0:T(4,128)S(1)}, f32[3,1536]{1,0:T(4,128)S(1)}, u32[]{:S(2)}, u32[]{:S(2)}) collective-permute-start(f32[3,1536]{1,0:T(4,128)S(1)} %maximum_add_fusion), channel_id=1, source_target_pairs={{0,16},{16,0},{1,17},{17,1},{2,18},{18,2},{3,19},{19,3},{4,20},{20... | collective-permute-start | bytes 55304 | tf_op jit(solution)/shard_map/ppermute | solution.py:20
  79.8 2.5 %assemble_held.1 = (bf16[2,64,1536]{2,1,0:T(8,128)(2,1)}, bf16[2,2,192,1536]{3,2,1,0:T(8,128)(2,1)}) custom-call(bf16[64,384]{1,0:T(8,128)(2,1)} %get-tuple-element.28.refs_0_, bf16[64,384]{1,0:T(8,128)(2,1)} %get-tuple-element.29.refs_1_, bf16[64,384]{1,0:T(8,128)(2,1)} %get-tuple-element.30.refs_2_, ...), custom_call_target="tpu_custom_call", output_to_operand_aliasing={{0}: (8, {}), {1}: (9, {})} | custom-call | bytes 2752512 | tf_op jit(solution)/shard_map/assemble_held/pallas_call | solution.py:200
  82.3 0.0 collective-permute-done.5
  82.3 0.6 copy.16
  (5 shorter events, 0.1 us)
Async XLA Ops:
  0.6 9.6 %copy-start = (bf16[1,1,3,192,1536]{4,3,2,1,0:T(8,128)(2,1)S(1)}, bf16[1,1,3,192,1536]{4,3,2,1,0:T(8,128)(2,1)}, u32[]{:S(2)}) copy-start(bf16[1,1,3,192,1536]{4,3,2,1,0:T(8,128)(2,1)} %param.6) | copy-start | bytes 5308420
  0.6 17.3 %collective-permute-start.1 = (bf16[2,16,6144]{2,1,0:T(8,128)(2,1)}, bf16[2,16,6144]{2,1,0:T(8,128)(2,1)S(1)}, u32[]{:S(2)}, u32[]{:S(2)}) collective-permute-start(bf16[2,16,6144]{2,1,0:T(8,128)(2,1)} %bitcast.45), channel_id=1, source_target_pairs={{0,12},{4,0},{8,4},{12,8},{1,13},{5,1},{9,5},{13,9},{2,14},{6,2},{... | collective-permute-start | bytes 1179656 | tf_op jit(solution)/shard_map/ppermute | solution.py:20
  11.1 40.7 %collective-permute-start = (bf16[448,384]{1,0:T(8,128)(2,1)}, bf16[448,384]{1,0:T(8,128)(2,1)S(1)}, u32[]{:S(2)}, u32[]{:S(2)}) collective-permute-start(bf16[448,384]{1,0:T(8,128)(2,1)} %pad_maximum_fusion), channel_id=1, source_target_pairs={{0,8},{4,12},{8,0},{12,4},{1,9},{5,13},{9,1},{13,5},{2,10},{6,14},... | collective-permute-start | bytes 1032200 | tf_op jit(solution)/shard_map/ppermute | solution.py:20
  11.2 48.0 %collective-permute-start.2 = (bf16[448,384]{1,0:T(8,128)(2,1)S(1)}, bf16[448,384]{1,0:T(8,128)(2,1)S(1)}, u32[]{:S(2)}, u32[]{:S(2)}) collective-permute-start(bf16[448,384]{1,0:T(8,128)(2,1)S(1)} %pad_maximum_fusion.1), channel_id=1, source_target_pairs={{0,8},{4,12},{8,0},{12,4},{1,9},{5,13},{9,1},{13,5},{2,10},{6,14},... | collective-permute-start | bytes 1032200 | tf_op jit(solution)/shard_map/ppermute | solution.py:20
  14.2 52.4 %collective-permute-start.3 = (bf16[448,384]{1,0:T(8,128)(2,1)S(1)}, bf16[448,384]{1,0:T(8,128)(2,1)S(1)}, u32[]{:S(2)}, u32[]{:S(2)}) collective-permute-start(bf16[448,384]{1,0:T(8,128)(2,1)S(1)} %pad_maximum_fusion.2), channel_id=1, source_target_pairs={{0,8},{4,12},{8,0},{12,4},{1,9},{5,13},{9,1},{13,5},{2,10},{6,14},... | collective-permute-start | bytes 1032200 | tf_op jit(solution)/shard_map/ppermute | solution.py:20
  14.3 58.9 %collective-permute-start.4 = (bf16[448,384]{1,0:T(8,128)(2,1)S(1)}, bf16[448,384]{1,0:T(8,128)(2,1)S(1)}, u32[]{:S(2)}, u32[]{:S(2)}) collective-permute-start(bf16[448,384]{1,0:T(8,128)(2,1)S(1)} %pad_maximum_fusion.3), channel_id=1, source_target_pairs={{0,8},{4,12},{8,0},{12,4},{1,9},{5,13},{9,1},{13,5},{2,10},{6,14},... | collective-permute-start | bytes 1032200 | tf_op jit(solution)/shard_map/ppermute | solution.py:20
  19.1 10.9 %all-to-all-start = ((bf16[4,2,16,1536]{3,2,1,0:T(8,128)(2,1)}), bf16[4,2,16,1536]{3,2,1,0:T(8,128)(2,1)S(1)}, u32[]{:S(2)}, u32[]{:S(2)}) async-start(bf16[4,2,16,1536]{3,2,1,0:T(8,128)(2,1)} %copy.14), calls=%async_computation | async-start | bytes 786432 | tf_op jit(solution)/shard_map/all_to_all | solution.py:268
  41.6 35.8 %copy-start.1 = (f32[3,1536]{1,0:T(4,128)S(1)}, f32[3,1536]{1,0:T(4,128)}, u32[]{:S(2)}) copy-start(f32[3,1536]{1,0:T(4,128)} %get-tuple-element.40) | copy-start | bytes 55300
  56.1 21.4 %copy-start.2 = (f32[3,384]{1,0:T(4,128)S(1)}, f32[3,384]{1,0:T(4,128)}, u32[]{:S(2)}) copy-start(f32[3,384]{1,0:T(4,128)} %get-tuple-element.41) | copy-start | bytes 13828
  78.2 4.1 %collective-permute-start.5 = (f32[3,1536]{1,0:T(4,128)S(1)}, f32[3,1536]{1,0:T(4,128)S(1)}, u32[]{:S(2)}, u32[]{:S(2)}) collective-permute-start(f32[3,1536]{1,0:T(4,128)S(1)} %maximum_add_fusion), channel_id=1, source_target_pairs={{0,16},{16,0},{1,17},{17,1},{2,18},{18,2},{3,19},{19,3},{4,20},{20... | collective-permute-start | bytes 55304 | tf_op jit(solution)/shard_map/ppermute | solution.py:20

commit v16 on v13

--- a/solution.py
+++ b/solution.py
@@ -154,7 +154,7 @@
         num_scalar_prefetch=1,
         grid=(1,),
         in_specs=[
-            pl.BlockSpec((part.shape[0], width), lambda i, m: (0, 0)),
+            pl.BlockSpec(memory_space=pltpu.VMEM),
             pl.BlockSpec((None, rows, width), lambda i, m: (m[1], 0, chunk)),
         ],
         out_specs=(
@@ -174,7 +174,7 @@
         grid_spec=grid_spec,
         cost_estimate=kernel_cost(rows, keys, width),
         name="held_backward",
-    )(meta, part, grads)
+    )(meta, pltpu.with_memory_space_constraint(part, pltpu.VMEM), grads)
 
 
 def assemble_kernel(bounds, *refs):
@@ -184,8 +184,8 @@
     copies = []
     for c, (lo, hi) in enumerate(bounds):
         cols = pl.ds(lo, hi - lo)
-        copies.append(pltpu.make_async_copy(q_parts[c], qg_ref.at[1, :, cols], sems.at[2 * c]))
-        copies.append(pltpu.make_async_copy(kv_parts[c], kv_ref.at[1, :, :, cols], sems.at[2 * c + 1]))
+        copies.append(pltpu.make_async_copy(q_parts[c], qg_ref.at[pl.ds(0, 1), pl.ds(0, qg_ref.shape[1]), cols], sems.at[2 * c]))
+        copies.append(pltpu.make_async_copy(kv_parts[c], kv_ref.at[pl.ds(0, 1), pl.ds(0, 2), pl.ds(0, kv_ref.shape[2]), cols], sems.at[2 * c + 1]))
     for copy in copies:
         copy.start()
     for copy in copies:
@@ -195,21 +195,26 @@
 def assemble(bounds, held_parts, qg, kv):
     rows, feats = qg.shape[1], qg.shape[2]
     keys = kv.shape[2]
+    anywhere = pl.BlockSpec(memory_space=pl.ANY)
     count = len(held_parts)
-    anywhere = pl.BlockSpec(memory_space=pl.ANY)
+    first_alias = 2 * count
     return pl.pallas_call(
         functools.partial(assemble_kernel, tuple(bounds)),
         out_shape=(
             jax.ShapeDtypeStruct(qg.shape, qg.dtype),
             jax.ShapeDtypeStruct(kv.shape, kv.dtype),
         ),
+        grid=(1,),
         in_specs=[anywhere] * (2 * count + 2),
-        out_specs=(anywhere, anywhere),
+        out_specs=(
+            pl.BlockSpec((1, rows, feats), lambda i: (1, 0, 0)),
+            pl.BlockSpec((1, 2, keys, feats), lambda i: (1, 0, 0, 0)),
+        ),
         scratch_shapes=[pltpu.SemaphoreType.DMA((2 * count,))],
-        input_output_aliases={2 * count: 0, 2 * count + 1: 1},
+        input_output_aliases={first_alias: 0, first_alias + 1: 1},
         cost_estimate=pl.CostEstimate(flops=0, transcendentals=0, bytes_accessed=4 * feats * (rows + 2 * keys)),
         name="assemble_held",
-    )(*[p[0] for p in held_parts], *[p[1] for p in held_parts], qg, kv)
+    )(*[p[0][None] for p in held_parts], *[p[1][None] for p in held_parts], qg, kv)
 
 
 def chunk_bounds(heads):

time: 125 us -> 83.5 us (0.67)
  Pallas kernels: 71.2 us -> 30.2 us
  local copies, waits for them, and re-layouts: 8.62 us -> 5.74 us
  waiting for transfers between devices: 20.7 us -> 23.5 us
    pallas_call x1, Pallas kernels: 42.9 us -> 2.46 us  [assemble(): pl.pallas_call(functools.partial(assemble_kernel, tuple(bounds)), out_sha...]
    unnamed x15 -> x7, local copies, waits for them, and re-layouts: 3.55 us -> 0.64 us
    ppermute x6, waiting for transfers between devices: 16.3 us -> 19 us  [from_behind(): return lax.ppermute(value, axis, pairs)]
  transfers between devices with their start and end apart: 7 -> 7, of which waited for: 5 -> 5; matrix products, arithmetic and copies ran while one was open for 7% -> 10% of each run, Pallas kernels for 54% -> 31%
where the time goes in v16:
time: 83.5 us; the launch traced here: 82.9 us
  Pallas kernels  30.2 us (36%)
  waiting for transfers between devices  23.5 us (28%)
  starting transfers between devices  16.2 us (19%)
  local copies, waits for them, and re-layouts  5.74 us (7%)
  other arithmetic  3.92 us (5%)
  between operations  3.34 us (4%)
    ppermute x6, waiting for transfers between devices, from_behind(): return lax.ppermute(value, axis, pairs)  19 us
    pallas_call x4, Pallas kernels, held_backward(): pl.pallas_call(held_kernel, out_shape=(jax.ShapeDtypeStruct((rows, width)...  16.8 us
    ppermute x6, starting transfers between devices, from_behind(): return lax.ppermute(value, axis, pairs)  12.7 us
    pallas_call x1, Pallas kernels, kept_backward(): pl.pallas_call(kept_kernel, out_shape=out_shape, grid_spec=grid_spec, cos...  10.9 us
    all_to_all x1, waiting for transfers between devices, body(): lax.all_to_all(split, 'tensor', split_axis=0, concat_axis=0, tiled=True)  4.52 us
    all_to_all x1, starting transfers between devices, body(): lax.all_to_all(split, 'tensor', split_axis=0, concat_axis=0, tiled=True)  3.46 us
    pallas_call x1, Pallas kernels, assemble(): pl.pallas_call(functools.partial(assemble_kernel, tuple(bounds)), out_sha...  2.46 us
  transfers between devices with their start and end apart: 7, of which 5 were waited for; matrix products, arithmetic and copies ran while one was open for 10% of the time, Pallas kernels for 31%

profile of v16, /device:TPU:0, one launch (start us, length us, event | category | flops | bytes accessed | tf_op | source)
XLA Modules:
  0.0 82.9 jit_solution(14630640677412517728)
XLA Ops:
  0.6 0.0 copy-start
  0.6 5.1 %collective-permute-start.1 = (bf16[2,16,6144]{2,1,0:T(8,128)(2,1)}, bf16[2,16,6144]{2,1,0:T(8,128)(2,1)S(1)}, u32[]{:S(2)}, u32[]{:S(2)}) collective-permute-start(bf16[2,16,6144]{2,1,0:T(8,128)(2,1)} %bitcast.61), channel_id=1, source_target_pairs={{0,12},{4,0},{8,4},{12,8},{1,13},{5,1},{9,5},{13,9},{2,14},{6,2},{... | collective-permute-start | bytes 1179656 | tf_op jit(solution)/shard_map/ppermute | solution.py:20
  5.7 0.8 constant_dynamic-slice_fusion
  6.6 0.5 slice.62
  8.4 1.1 %slice.61 = bf16[1,1,1,192,1536]{4,3,2,1,0:T(8,128)(2,1)S(1)} slice(bf16[1,1,3,192,1536]{4,3,2,1,0:T(8,128)(2,1)} %param.6), slice={[0:1], [0:1], [0:1], [0:192], [0:1536]} | slice | bytes 1179648 | tf_op jit(solution)/shard_map/slice | solution.py:259
  10.1 0.1 dynamic-slice_bitcast_fusion
  10.2 0.0 copy-done
  10.2 0.1 slice_bitcast_fusion.1
  10.4 0.8 pad_maximum_fusion
  11.1 0.0 collective-permute-start
  11.2 3.0 %collective-permute-start.2 = (bf16[448,384]{1,0:T(8,128)(2,1)S(1)}, bf16[448,384]{1,0:T(8,128)(2,1)S(1)}, u32[]{:S(2)}, u32[]{:S(2)}) collective-permute-start(bf16[448,384]{1,0:T(8,128)(2,1)S(1)} %pad_maximum_fusion.1), channel_id=1, source_target_pairs={{0,8},{4,12},{8,0},{12,4},{1,9},{5,13},{9,1},{13,5},{2,10},{6,14},... | collective-permute-start | bytes 1032200 | tf_op jit(solution)/shard_map/ppermute | solution.py:20
  14.2 0.1 collective-permute-start.3
  14.3 3.0 %collective-permute-start.4 = (bf16[448,384]{1,0:T(8,128)(2,1)S(1)}, bf16[448,384]{1,0:T(8,128)(2,1)S(1)}, u32[]{:S(2)}, u32[]{:S(2)}) collective-permute-start(bf16[448,384]{1,0:T(8,128)(2,1)S(1)} %pad_maximum_fusion.3), channel_id=1, source_target_pairs={{0,8},{4,12},{8,0},{12,4},{1,9},{5,13},{9,1},{13,5},{2,10},{6,14},... | collective-permute-start | bytes 1032200 | tf_op jit(solution)/shard_map/ppermute | solution.py:20
  18.0 0.0 collective-permute-done.1
  18.0 0.3 reshape.26
  18.3 0.8 copy.14
  19.1 3.5 %all-to-all-start = ((bf16[4,2,16,1536]{3,2,1,0:T(8,128)(2,1)}), bf16[4,2,16,1536]{3,2,1,0:T(8,128)(2,1)S(1)}, u32[]{:S(2)}, u32[]{:S(2)}) async-start(bf16[4,2,16,1536]{3,2,1,0:T(8,128)(2,1)} %copy.14), calls=%async_computation | async-start | bytes 786432 | tf_op jit(solution)/shard_map/all_to_all | solution.py:270
  22.5 0.6 fusion.1
  23.1 1.1 %pad_add_fusion.1.meta_ref = s32[2]{0:T(128)} fusion(s32[1]{0:T(128)} %bitcast.41, s32[1]{0:T(128)} %bitcast.7), kind=kLoop, calls=%fused_computation.18 | loop fusion | flops 2 | bytes 16 | tf_op jit(solution)/shard_map/stack | solution.py:136
  24.2 1.2 %pad_add_fusion.meta_ref = s32[2]{0:T(128)} fusion(s32[1]{0:T(128)} %bitcast.1, s32[1]{0:T(128)} %bitcast), kind=kLoop, calls=%fused_computation.17 | loop fusion | flops 2 | bytes 16 | tf_op jit(solution)/shard_map/stack | solution.py:166
  25.4 4.5 %all-to-all-done = bf16[4,2,16,1536]{3,2,1,0:T(8,128)(2,1)S(1)} async-done(((bf16[4,2,16,1536]{3,2,1,0:T(8,128)(2,1)}), bf16[4,2,16,1536]{3,2,1,0:T(8,128)(2,1)S(1)}, u32[]{:S(2)}, u32[]{:S(2)}) %all-to-all-start) | async-done | bytes 393248 | tf_op jit(solution)/shard_map/all_to_all | solution.py:270
  29.9 0.8 copy.15
  30.7 10.9 %kept_backward.1 = (bf16[2,64,1536]{2,1,0:T(8,128)(2,1)}, bf16[2,2,192,1536]{3,2,1,0:T(8,128)(2,1)}, f32[3,1536]{1,0:T(4,128)}) custom-call(s32[2]{0:T(128)} %pad_add_fusion.1.meta_ref, bf16[3,192,1536]{2,1,0:T(8,128)(2,1)} %bitcast.49, bf16[2,64,1536]{2,1,0:T(8,128)(2,1)} %bitcast.42), custom_call_target="tpu_custom_call" | custom-call | flops 226492416 | bytes 2949120 | tf_op jit(solution)/shard_map/kept_backward/pallas_call | solution.py:137
  41.6 0.0 copy-start.1
  41.6 10.3 %collective-permute-done.x_ref = bf16[448,384]{1,0:T(8,128)(2,1)S(1)} collective-permute-done((bf16[448,384]{1,0:T(8,128)(2,1)}, bf16[448,384]{1,0:T(8,128)(2,1)S(1)}, u32[]{:S(2)}, u32[]{:S(2)}) %collective-permute-start) | collective-permute-done | bytes 344096 | tf_op jit(solution)/shard_map/ppermute | solution.py:20
  51.9 4.2 %held_backward.4 = (bf16[64,384]{1,0:T(8,128)(2,1)}, bf16[2,192,384]{2,1,0:T(8,128)(2,1)}, f32[3,384]{1,0:T(4,128)}) custom-call(s32[2]{0:T(128)} %pad_add_fusion.meta_ref, bf16[448,384]{1,0:T(8,128)(2,1)S(1)} %collective-permute-done.x_ref, bf16[2,64,1536]{2,1,0:T(8,128)(2,1)} %bitcast.43), custom_call_target="tpu_custom_call" | custom-call | flops 56623104 | bytes 737280 | tf_op jit(solution)/shard_map/held_backward/pallas_call | solution.py:167
  56.1 0.0 copy-start.2
  56.1 3.2 %collective-permute-done.2.x_ref = bf16[448,384]{1,0:T(8,128)(2,1)S(1)} collective-permute-done((bf16[448,384]{1,0:T(8,128)(2,1)S(1)}, bf16[448,384]{1,0:T(8,128)(2,1)S(1)}, u32[]{:S(2)}, u32[]{:S(2)}) %collective-permute-start.2) | collective-permute-done | bytes 344096 | tf_op jit(solution)/shard_map/ppermute | solution.py:20
  59.2 4.2 %held_backward.5 = (bf16[64,384]{1,0:T(8,128)(2,1)}, bf16[2,192,384]{2,1,0:T(8,128)(2,1)}, f32[3,384]{1,0:T(4,128)}) custom-call(s32[2]{0:T(128)} %pad_add_fusion.meta_ref, bf16[448,384]{1,0:T(8,128)(2,1)S(1)} %collective-permute-done.2.x_ref, bf16[2,64,1536]{2,1,0:T(8,128)(2,1)} %bitcast.44), custom_call_target="tpu_custom_call" | custom-call | flops 56623104 | bytes 737280 | tf_op jit(solution)/shard_map/held_backward/pallas_call | solution.py:167
  63.5 3.2 %collective-permute-done.3.x_ref = bf16[448,384]{1,0:T(8,128)(2,1)S(1)} collective-permute-done((bf16[448,384]{1,0:T(8,128)(2,1)S(1)}, bf16[448,384]{1,0:T(8,128)(2,1)S(1)}, u32[]{:S(2)}, u32[]{:S(2)}) %collective-permute-start.3) | collective-permute-done | bytes 344096 | tf_op jit(solution)/shard_map/ppermute | solution.py:20
  66.6 4.2 %held_backward.6 = (bf16[64,384]{1,0:T(8,128)(2,1)}, bf16[2,192,384]{2,1,0:T(8,128)(2,1)}, f32[3,384]{1,0:T(4,128)}) custom-call(s32[2]{0:T(128)} %pad_add_fusion.meta_ref, bf16[448,384]{1,0:T(8,128)(2,1)S(1)} %collective-permute-done.3.x_ref, bf16[2,64,1536]{2,1,0:T(8,128)(2,1)} %bitcast.45), custom_call_target="tpu_custom_call" | custom-call | flops 56623104 | bytes 737280 | tf_op jit(solution)/shard_map/held_backward/pallas_call | solution.py:167
  70.8 2.4 %collective-permute-done.4.x_ref = bf16[448,384]{1,0:T(8,128)(2,1)S(1)} collective-permute-done((bf16[448,384]{1,0:T(8,128)(2,1)S(1)}, bf16[448,384]{1,0:T(8,128)(2,1)S(1)}, u32[]{:S(2)}, u32[]{:S(2)}) %collective-permute-start.4) | collective-permute-done | bytes 344096 | tf_op jit(solution)/shard_map/ppermute | solution.py:20
  73.2 4.2 %held_backward.7 = (bf16[64,384]{1,0:T(8,128)(2,1)}, bf16[2,192,384]{2,1,0:T(8,128)(2,1)}, f32[3,384]{1,0:T(4,128)}) custom-call(s32[2]{0:T(128)} %pad_add_fusion.meta_ref, bf16[448,384]{1,0:T(8,128)(2,1)S(1)} %collective-permute-done.4.x_ref, bf16[2,64,1536]{2,1,0:T(8,128)(2,1)} %bitcast.46), custom_call_target="tpu_custom_call" | custom-call | flops 56623104 | bytes 737280 | tf_op jit(solution)/shard_map/held_backward/pallas_call | solution.py:167
  77.4 0.0 copy-done.1
  77.4 0.0 copy-done.2
  77.4 0.7 maximum_add_fusion
  78.2 1.6 %collective-permute-start.5 = (f32[3,1536]{1,0:T(4,128)S(1)}, f32[3,1536]{1,0:T(4,128)S(1)}, u32[]{:S(2)}, u32[]{:S(2)}) collective-permute-start(f32[3,1536]{1,0:T(4,128)S(1)} %maximum_add_fusion), channel_id=1, source_target_pairs={{0,16},{16,0},{1,17},{17,1},{2,18},{18,2},{3,19},{19,3},{4,20},{20... | collective-permute-start | bytes 55304 | tf_op jit(solution)/shard_map/ppermute | solution.py:20
  79.8 2.5 %assemble_held.1 = (bf16[2,64,1536]{2,1,0:T(8,128)(2,1)}, bf16[2,2,192,1536]{3,2,1,0:T(8,128)(2,1)}) custom-call(bf16[1,64,384]{2,1,0:T(8,128)(2,1)} %bitcast.57, bf16[1,64,384]{2,1,0:T(8,128)(2,1)} %bitcast.58, bf16[1,64,384]{2,1,0:T(8,128)(2,1)} %bitcast.59, bf16[1,64,384]{2,1,0:T(8,128)(2,1)} %bitcast.60, ...), custom_call_target="tpu_custom_call", output_to_operand_aliasing={{0}: (8, {}), {1}: (9, {})} | custom-call | bytes 2752512 | tf_op jit(solution)/shard_map/assemble_held/pallas_call | solution.py:201
  82.2 0.0 collective-permute-done.5
  82.2 0.6 copy.16
  (5 shorter events, 0.1 us)
Async XLA Ops:
  0.6 9.6 %copy-start = (bf16[1,1,3,192,1536]{4,3,2,1,0:T(8,128)(2,1)S(1)}, bf16[1,1,3,192,1536]{4,3,2,1,0:T(8,128)(2,1)}, u32[]{:S(2)}) copy-start(bf16[1,1,3,192,1536]{4,3,2,1,0:T(8,128)(2,1)} %param.6) | copy-start | bytes 5308420
  0.6 17.3 %collective-permute-start.1 = (bf16[2,16,6144]{2,1,0:T(8,128)(2,1)}, bf16[2,16,6144]{2,1,0:T(8,128)(2,1)S(1)}, u32[]{:S(2)}, u32[]{:S(2)}) collective-permute-start(bf16[2,16,6144]{2,1,0:T(8,128)(2,1)} %bitcast.61), channel_id=1, source_target_pairs={{0,12},{4,0},{8,4},{12,8},{1,13},{5,1},{9,5},{13,9},{2,14},{6,2},{... | collective-permute-start | bytes 1179656 | tf_op jit(solution)/shard_map/ppermute | solution.py:20
  11.1 40.7 %collective-permute-start = (bf16[448,384]{1,0:T(8,128)(2,1)}, bf16[448,384]{1,0:T(8,128)(2,1)S(1)}, u32[]{:S(2)}, u32[]{:S(2)}) collective-permute-start(bf16[448,384]{1,0:T(8,128)(2,1)} %pad_maximum_fusion), channel_id=1, source_target_pairs={{0,8},{4,12},{8,0},{12,4},{1,9},{5,13},{9,1},{13,5},{2,10},{6,14},... | collective-permute-start | bytes 1032200 | tf_op jit(solution)/shard_map/ppermute | solution.py:20
  11.2 48.0 %collective-permute-start.2 = (bf16[448,384]{1,0:T(8,128)(2,1)S(1)}, bf16[448,384]{1,0:T(8,128)(2,1)S(1)}, u32[]{:S(2)}, u32[]{:S(2)}) collective-permute-start(bf16[448,384]{1,0:T(8,128)(2,1)S(1)} %pad_maximum_fusion.1), channel_id=1, source_target_pairs={{0,8},{4,12},{8,0},{12,4},{1,9},{5,13},{9,1},{13,5},{2,10},{6,14},... | collective-permute-start | bytes 1032200 | tf_op jit(solution)/shard_map/ppermute | solution.py:20
  14.2 52.4 %collective-permute-start.3 = (bf16[448,384]{1,0:T(8,128)(2,1)S(1)}, bf16[448,384]{1,0:T(8,128)(2,1)S(1)}, u32[]{:S(2)}, u32[]{:S(2)}) collective-permute-start(bf16[448,384]{1,0:T(8,128)(2,1)S(1)} %pad_maximum_fusion.2), channel_id=1, source_target_pairs={{0,8},{4,12},{8,0},{12,4},{1,9},{5,13},{9,1},{13,5},{2,10},{6,14},... | collective-permute-start | bytes 1032200 | tf_op jit(solution)/shard_map/ppermute | solution.py:20
  14.3 58.9 %collective-permute-start.4 = (bf16[448,384]{1,0:T(8,128)(2,1)S(1)}, bf16[448,384]{1,0:T(8,128)(2,1)S(1)}, u32[]{:S(2)}, u32[]{:S(2)}) collective-permute-start(bf16[448,384]{1,0:T(8,128)(2,1)S(1)} %pad_maximum_fusion.3), channel_id=1, source_target_pairs={{0,8},{4,12},{8,0},{12,4},{1,9},{5,13},{9,1},{13,5},{2,10},{6,14},... | collective-permute-start | bytes 1032200 | tf_op jit(solution)/shard_map/ppermute | solution.py:20
  19.1 10.9 %all-to-all-start = ((bf16[4,2,16,1536]{3,2,1,0:T(8,128)(2,1)}), bf16[4,2,16,1536]{3,2,1,0:T(8,128)(2,1)S(1)}, u32[]{:S(2)}, u32[]{:S(2)}) async-start(bf16[4,2,16,1536]{3,2,1,0:T(8,128)(2,1)} %copy.14), calls=%async_computation | async-start | bytes 786432 | tf_op jit(solution)/shard_map/all_to_all | solution.py:270
  41.6 35.8 %copy-start.1 = (f32[3,1536]{1,0:T(4,128)S(1)}, f32[3,1536]{1,0:T(4,128)}, u32[]{:S(2)}) copy-start(f32[3,1536]{1,0:T(4,128)} %get-tuple-element.40) | copy-start | bytes 55300
  56.1 21.4 %copy-start.2 = (f32[3,384]{1,0:T(4,128)S(1)}, f32[3,384]{1,0:T(4,128)}, u32[]{:S(2)}) copy-start(f32[3,384]{1,0:T(4,128)} %get-tuple-element.41) | copy-start | bytes 13828
  78.2 4.1 %collective-permute-start.5 = (f32[3,1536]{1,0:T(4,128)S(1)}, f32[3,1536]{1,0:T(4,128)S(1)}, u32[]{:S(2)}, u32[]{:S(2)}) collective-permute-start(f32[3,1536]{1,0:T(4,128)S(1)} %maximum_add_fusion), channel_id=1, source_target_pairs={{0,16},{16,0},{1,17},{17,1},{2,18},{18,2},{3,19},{19,3},{4,20},{20... | collective-permute-start | bytes 55304 | tf_op jit(solution)/shard_map/ppermute | solution.py:20
